TPU v7x, 256 devices: a whole 4x4x8 slice. The times are simulated.
256 devices in a mesh: tm: 64 (over y, z, core), state: 4 (over x).
Axes of the slice: x: 4, y: 4, z: 8, core: 2. Of those that a mesh axis runs over, the one named last changes fastest.
Arguments:
- dynamics: float32 [512, 512], P('state'), may hold values from -1 to 1
- pattern: int32 [4, 4], replicated, may hold values from 0 to 1
- initial_mean: float32 [4, 512], replicated, may hold values from -6 to 6
- observed: float32 [1024, 4], P('tm'), may hold values from -6 to 6
- obs_index: int32 [1024], P('tm'), may hold values from 0 to 511
- obs_noise: float32 [1024], P('tm'), may hold values from 0.5 to 4
Outputs:
- filtered: float32 [1024, 4, 512], P('tm', 'state')
- smoothed: float32 [1024, 4, 512], P('tm', 'state')
All inputs are finite; a program needn't handle non-finite values.
Results may differ from a plain program's by a relative error of at most 0.0003.
Values sent between devices are 32-bit elements; how exact they have to be, the bound alone decides.
No kernel may reach another device: no remote copies, remote signals or barrier semaphores. Data moves between devices by JAX's collectives and lax.ppermute only.
A program may use at most 256 MiB of HBM per device.

v0:
```python
import jax
import jax.numpy as jnp
from jax import lax
from jax.sharding import PartitionSpec as P


def passed_along(block, axis, distance):
    devices = range(lax.axis_size(axis))
    route = [(i - distance, i) for i in devices if i - distance in devices]
    return lax.ppermute(block, axis, route)


def product(left, right):
    return jnp.dot(left, right, precision=lax.Precision.HIGHEST, preferred_element_type=jnp.float32)


def transposed(left, right):
    return lax.dot_general(
        left,
        right,
        (((1,), (1,)), ((), ())),
        precision=lax.Precision.HIGHEST,
        preferred_element_type=jnp.float32,
    )


def select_tree(usable, first_tree, second_tree):

    def select_leaf(first_leaf, second_leaf):
        return jnp.where(usable, first_leaf, second_leaf)

    return jax.tree.map(select_leaf, first_tree, second_tree)


def per_device(dynamics, pattern, initial_mean, observed, obs_index, obs_noise):
    row_count = dynamics.shape[0]
    state_width = dynamics.shape[1]
    blocks = pattern.shape[0]
    block_span = state_width // blocks
    seq_total = initial_mean.shape[0]
    steps_here = observed.shape[0]
    members = lax.axis_size("state")
    member = lax.axis_index("state")
    segments = lax.axis_size("tm")
    segment = lax.axis_index("tm")
    batch_here = seq_total // members
    present = jnp.maximum(pattern, jnp.eye(blocks, dtype=jnp.int32))
    block_mask = jnp.repeat(jnp.repeat(present, block_span, 0), block_span, 1).astype(jnp.float32)
    transition = lax.all_gather(dynamics, "state", axis=0, tiled=True) * block_mask
    kalman_gains = 1.0 / (1.0 + obs_noise)
    state_index = jnp.arange(state_width, dtype=jnp.int32)
    observed_masks = (state_index[None, :] == obs_index[:, None]).astype(jnp.float32)
    scale_factors = 1.0 - kalman_gains[:, None] * observed_masks
    final_local = jnp.arange(steps_here, dtype=jnp.int32) == steps_here - 1
    retain_flags = 1.0 - jnp.where((segment == segments - 1) & final_local, 1.0, 0.0).astype(
        jnp.float32
    )
    first_row = member * row_count
    owned_rows = (
        jnp.arange(row_count, dtype=jnp.int32)[:, None] + first_row == state_index[None, :]
    ).astype(jnp.float32)
    batch_start = member * batch_here
    local_observations = lax.dynamic_slice_in_dim(observed, batch_start, batch_here, 1)

    def combine_rows(earlier_full, later):
        return (
            product(later[0], earlier_full[0]),
            transposed(earlier_full[1], later[0]) + later[1],
        )

    def doubling(element, direction):
        identity = (owned_rows, jnp.zeros((seq_total, row_count), jnp.float32))
        distances = [1]
        for level_turn in range(9):
            if 2**level_turn < segments:
                distances.append(2**level_turn)
        current = element
        for level_turn, distance in enumerate(distances):
            arrived = passed_along(current, "tm", direction * distance)
            if direction > 0:
                usable = segment >= distance
            else:
                usable = segment + distance < segments
            if level_turn == 0:
                current = select_tree(usable, arrived, identity)
            else:
                gathered = (
                    lax.all_gather(arrived[0], "state", axis=0, tiled=True),
                    lax.all_gather(arrived[1], "state", axis=1, tiled=True),
                )
                current = select_tree(usable, combine_rows(gathered, current), current)
        return current

    def entering(element, start_mean, direction):
        map_rows, map_offsets = doubling(element, direction)
        if start_mean is None:
            entry_rows = map_offsets
        else:
            entry_rows = map_offsets + transposed(start_mean, map_rows)
        return lax.all_to_all(entry_rows, "state", split_axis=0, concat_axis=1, tiled=True)

    def filter_portion(carried, inputs):
        row_block, offsets = carried
        hit_mask, scaling, gain_now, obs_now = inputs
        column_now = product(row_block, hit_mask)
        offsets = offsets + gain_now * obs_now[:, None] * column_now[None, :]
        row_block = product(row_block * scaling[None, :], transition)
        return ((row_block, offsets), None)

    initial_shifts = jnp.zeros((seq_total, row_count), jnp.float32)
    (filter_rows, filter_offsets), unused_value = lax.scan(
        filter_portion,
        (owned_rows, initial_shifts),
        (observed_masks, scale_factors, kalman_gains, observed),
        reverse=True,
    )
    filter_input = entering((filter_rows, filter_offsets), initial_mean, 1)

    def forward_sweep(current_state, inputs):
        scaling, hit_mask, gain_now, obs_now = inputs
        current_state = (
            transposed(current_state, transition) * scaling[None, :]
            + gain_now * obs_now[:, None] * hit_mask[None, :]
        )
        return (current_state, current_state)

    unused_value, filtered = lax.scan(
        forward_sweep,
        filter_input,
        (scale_factors, observed_masks, kalman_gains, local_observations),
    )
    flat_means = filtered.reshape(steps_here * batch_here, state_width)
    backward_mapped = product(transposed(flat_means, transition), transition).reshape(
        steps_here, batch_here, state_width
    )
    residual_terms = (
        filtered - retain_flags[:, None, None] * backward_mapped * scale_factors[:, None, :]
    )

    def smoother_update(current_state, inputs):
        scaling, keep_flag, gap_term = inputs
        current_state = keep_flag * product(current_state, transition) * scaling[None, :] + gap_term
        return (current_state, current_state)

    zero_portion = jnp.zeros((batch_here, state_width), jnp.float32)
    local_shifts, unused_value = lax.scan(
        smoother_update, zero_portion, (scale_factors, retain_flags, residual_terms), reverse=True
    )
    smooth_offsets = lax.all_to_all(local_shifts, "state", split_axis=1, concat_axis=0, tiled=True)

    def smoother_portion(row_block, inputs):
        scaling, keep_flag = inputs
        return (keep_flag * transposed(row_block * scaling[None, :], transition), None)

    smoother_rows, unused_value = lax.scan(
        smoother_portion, owned_rows, (scale_factors, retain_flags)
    )
    smoother_input = entering((smoother_rows, smooth_offsets), None, -1)
    unused_value, smoothed = lax.scan(
        smoother_update, smoother_input, (scale_factors, retain_flags, residual_terms), reverse=True
    )
    return (filtered, smoothed)


def solution(mesh):
    return jax.shard_map(
        per_device,
        mesh=mesh,
        in_specs=(P("state", None), P(), P(), P("tm", None), P("tm"), P("tm")),
        out_specs=(P("tm", "state", None), P("tm", "state", None)),
        check_vma=False,
    )
```

profile of v0, /device:TPU:232, one launch (start us, length us, event | category | flops | bytes accessed | tf_op | source)
XLA Modules:
  0.0 766.1 jit_solution(12369168793150731097)
XLA Ops:
  10.4 26.4 %all-gather.13.cloned.1.call-done = f32[512,512]{1,0:T(8,128)} async-done(((f32[128,512]{1,0:T(8,128)}), f32[512,512]{1,0:T(8,128)}) %all-gather.13.cloned.1.call-update) | async-done | bytes 1048592 | tf_op jit(solution)/shard_map/all_gather | solution.py:49
  38.2 40.3 %while.71 = (s32[]{:T(128)}, f32[128,512]{1,0:T(8,128)S(1)}, f32[16]{0:T(128)S(1)}, f32[16,512]{1,0:T(8,128)S(1)}, f32[512,512]{1,0:T(8,128)S(1)}, /*index=5*/s32[]{:T(128)}) while((s32[]{:T(128)}, f32[128,512]{1,0:T(8,128)S(1)}, f32[16]{0:T(128)S(1)}, f32[16,512]{1,0:T(8,128)S(1)}, f32[512,512]{1,0:T(8,128)S(1)}, /*index=5*/s32[]{:T(128)}) %tuple.143), condition=%wide.region_7.8_spmd, body=%wide.region_6.7_spmd.sunk | while | flops 402784256 | bytes 2103393 | solution.py:155
  80.5 38.8 %while.73 = (s32[]{:T(128)}, f32[128,512]{1,0:T(8,128)S(1)}, f32[4,128]{1,0:T(4,128)S(1)}, f32[16,512]{1,0:T(8,128)S(1)}, f32[512,512]{1,0:T(8,128)S(1)}, /*inde...) while((s32[]{:T(128)}, f32[128,512]{1,0:T(8,128)S(1)}, ...), condition=%wide.region_1.2_spmd.clone, body=%wide.region_0.1_spmd.clone.sunk | while | flops 403506688 | bytes 2372823 | solution.py:111
  121.7 5.3 collective-permute-done.2
  129.0 5.8 collective-permute-done.4
  135.5 29.5 %all-gather.15.cloned.1.call-done = f32[512,512]{1,0:T(8,128)} async-done(((f32[128,512]{1,0:T(8,128)}), f32[512,512]{1,0:T(8,128)}) %all-gather.15.cloned.1.call-update) | async-done | bytes 1048592 | tf_op jit(solution)/shard_map/all_gather | solution.py:88
  167.0 2.8 collective-permute-start.6
  169.8 5.5 collective-permute-done.6
  178.0 3.9 collective-permute-done.18
  182.6 21.9 %all-gather.17.cloned.1.call-done = f32[512,512]{1,0:T(8,128)} async-done(((f32[128,512]{1,0:T(8,128)}), f32[512,512]{1,0:T(8,128)}) %all-gather.17.cloned.1.call-update) | async-done | bytes 1048592 | tf_op jit(solution)/shard_map/all_gather | solution.py:88
  206.5 3.7 collective-permute-start.8
  210.2 10.6 %collective-permute-done.8 = f32[128,512]{1,0:T(8,128)S(1)} collective-permute-done((f32[128,512]{1,0:T(8,128)S(1)}, f32[128,512]{1,0:T(8,128)S(1)}, u32[]{:S(2)}, u32[]{:S(2)}) %collective-permute-start.8) | collective-permute-done | bytes 262176 | tf_op jit(solution)/shard_map/ppermute | solution.py:10
  221.6 11.6 %all-gather.27.cloned.1.call-done = f32[512,512]{1,0:T(8,128)} async-done(((f32[128,512]{1,0:T(8,128)}), f32[512,512]{1,0:T(8,128)}) %all-gather.27.cloned.1.call-update) | async-done | bytes 1048592 | tf_op jit(solution)/shard_map/all_gather | solution.py:88
  235.2 3.3 collective-permute-start.20
  238.5 7.1 collective-permute-done.20
  246.4 15.6 %all-gather.19.cloned.1.call-done = f32[512,512]{1,0:T(8,128)} async-done(((f32[128,512]{1,0:T(8,128)}), f32[512,512]{1,0:T(8,128)}) %all-gather.19.cloned.1.call-update) | async-done | bytes 1048592 | tf_op jit(solution)/shard_map/all_gather | solution.py:88
  263.9 5.7 collective-permute-start.10
  269.6 10.7 %collective-permute-done.10 = f32[128,512]{1,0:T(8,128)S(1)} collective-permute-done((f32[128,512]{1,0:T(8,128)S(1)}, f32[128,512]{1,0:T(8,128)S(1)}, u32[]{:S(2)}, u32[]{:S(2)}) %collective-permute-start.10) | collective-permute-done | bytes 262176 | tf_op jit(solution)/shard_map/ppermute | solution.py:10
  281.1 9.5 %all-gather.29.cloned.1.call-done = f32[512,512]{1,0:T(8,128)} async-done(((f32[128,512]{1,0:T(8,128)}), f32[512,512]{1,0:T(8,128)}) %all-gather.29.cloned.1.call-update) | async-done | bytes 1048592 | tf_op jit(solution)/shard_map/all_gather | solution.py:88
  292.6 4.1 collective-permute-start.22
  296.7 11.4 %collective-permute-done.22 = f32[128,512]{1,0:T(8,128)S(1)} collective-permute-done((f32[128,512]{1,0:T(8,128)S(1)}, f32[128,512]{1,0:T(8,128)S(1)}, u32[]{:S(2)}, u32[]{:S(2)}) %collective-permute-start.22) | collective-permute-done | bytes 262176 | tf_op jit(solution)/shard_map/ppermute | solution.py:10
  308.9 10.6 %all-gather.21.cloned.1.call-done = f32[512,512]{1,0:T(8,128)} async-done(((f32[128,512]{1,0:T(8,128)}), f32[512,512]{1,0:T(8,128)}) %all-gather.21.cloned.1.call-update) | async-done | bytes 1048592 | tf_op jit(solution)/shard_map/all_gather | solution.py:88
  321.5 3.4 collective-permute-start.12
  324.9 4.9 collective-permute-done.12
  330.5 17.9 %all-gather.31.cloned.1.call-done = f32[512,512]{1,0:T(8,128)} async-done(((f32[128,512]{1,0:T(8,128)}), f32[512,512]{1,0:T(8,128)}) %all-gather.31.cloned.1.call-update) | async-done | bytes 1048592 | tf_op jit(solution)/shard_map/all_gather | solution.py:88
  350.3 4.8 collective-permute-start.24
  355.1 12.6 %collective-permute-done.24 = f32[128,512]{1,0:T(8,128)} collective-permute-done((f32[128,512]{1,0:T(8,128)S(1)}, f32[128,512]{1,0:T(8,128)}, u32[]{:S(2)}, u32[]{:S(2)}) %collective-permute-start.24) | collective-permute-done | bytes 262176 | tf_op jit(solution)/shard_map/ppermute | solution.py:10
  367.8 9.4 %all-gather.23.cloned.1.call-done = f32[512,512]{1,0:T(8,128)} async-done(((f32[128,512]{1,0:T(8,128)}), f32[512,512]{1,0:T(8,128)}) %all-gather.23.cloned.1.call-update) | async-done | bytes 1048592 | tf_op jit(solution)/shard_map/all_gather | solution.py:88
  379.9 4.7 collective-permute-start.13
  391.4 3.0 collective-permute-done.1
  394.4 10.5 %all_gather.73 = f32[4,512]{1,0:T(4,128)S(1)} all-gather(f32[4,128]{1,0:T(4,128)S(1)} %collective-permute-done.1), channel_id=1, replica_groups=mesh['tm'=64,'state'=4] {'state'}, dimensions={1}, use_global_device_ids=true | all-gather | bytes 10240 | tf_op jit(solution)/shard_map/all_gather | solution.py:89
  405.2 5.2 collective-permute-start.3
  411.6 10.5 %all_gather.74 = f32[4,512]{1,0:T(4,128)S(1)} all-gather(f32[4,128]{1,0:T(4,128)S(1)} %collective-permute-done.3), channel_id=1, replica_groups=mesh['tm'=64,'state'=4] {'state'}, dimensions={1}, use_global_device_ids=true | all-gather | bytes 10240 | tf_op jit(solution)/shard_map/all_gather | solution.py:89
  422.4 3.7 collective-permute-start.5
  426.1 2.8 collective-permute-done.5
  428.9 10.4 %all_gather.76 = f32[4,512]{1,0:T(4,128)S(1)} all-gather(f32[4,128]{1,0:T(4,128)S(1)} %collective-permute-done.5), channel_id=1, replica_groups=mesh['tm'=64,'state'=4] {'state'}, dimensions={1}, use_global_device_ids=true | all-gather | bytes 10240 | tf_op jit(solution)/shard_map/all_gather | solution.py:89
  439.6 6.8 collective-permute-start.7
  446.4 2.7 collective-permute-done.7
  449.0 10.6 %all_gather.78 = f32[4,512]{1,0:T(4,128)S(1)} all-gather(f32[4,128]{1,0:T(4,128)S(1)} %collective-permute-done.7), channel_id=1, replica_groups=mesh['tm'=64,'state'=4] {'state'}, dimensions={1}, use_global_device_ids=true | all-gather | bytes 10240 | tf_op jit(solution)/shard_map/all_gather | solution.py:89
  459.8 3.1 collective-permute-start.9
  465.4 10.6 %all_gather.80 = f32[4,512]{1,0:T(4,128)S(1)} all-gather(f32[4,128]{1,0:T(4,128)S(1)} %collective-permute-done.9), channel_id=1, replica_groups=mesh['tm'=64,'state'=4] {'state'}, dimensions={1}, use_global_device_ids=true | all-gather | bytes 10240 | tf_op jit(solution)/shard_map/all_gather | solution.py:89
  476.3 3.5 collective-permute-start.11
  481.8 3.7 collective-permute-start.26
  485.5 10.6 %all_gather.82 = f32[4,512]{1,0:T(4,128)S(1)} all-gather(f32[4,128]{1,0:T(4,128)S(1)} %collective-permute-done.11), channel_id=1, replica_groups=mesh['tm'=64,'state'=4] {'state'}, dimensions={1}, use_global_device_ids=true | all-gather | bytes 10240 | tf_op jit(solution)/shard_map/all_gather | solution.py:89
  499.3 3.6 all-to-all-start
  503.6 4.5 all-to-all-done
  508.1 55.4 %while.70 = (s32[]{:T(128)}, f32[1,512]{1,0:T(1,128)S(1)}, f32[16,1,512]{2,1,0:T(1,128)S(1)}, f32[512,512]{1,0:T(8,128)S(1)}, f32[16,512]{1,0:T(8,128)S(1)}, /*i...) while((s32[]{:T(128)}, f32[1,512]{1,0:T(1,128)S(1)}, ...), condition=%wide.region_3.4_spmd, body=%wide.region_2.3_spmd.sunk | while | flops 3147267 | bytes 1063049 | solution.py:127
  565.1 30.2 %while.74 = (s32[]{:T(128)}, f32[1,512]{1,0:T(1,128)S(1)}, f32[16]{0:T(128)S(1)}, f32[512,512]{1,0:T(8,128)S(1)}, f32[16,512]{1,0:T(8,128)S(1)}, /*index=5*/f32[...) while((s32[]{:T(128)}, f32[1,512]{1,0:T(1,128)S(1)}, f32[16]{0:T(128)S(1)}, ...), condition=%wide.region_5.6_spmd.clone, body=%wide.region_4.5_spmd.clone.sunk | while | flops 3147780 | bytes 1065103 | solution.py:146
  595.4 7.6 all_to_all.48
  606.2 4.3 collective-permute-start.15
  610.5 5.2 collective-permute-done.15
  615.8 10.4 %all_gather.85 = f32[4,512]{1,0:T(4,128)S(1)} all-gather(f32[4,128]{1,0:T(4,128)S(1)} %collective-permute-done.15), channel_id=1, replica_groups=mesh['tm'=64,'state'=4] {'state'}, dimensions={1}, use_global_device_ids=true | all-gather | bytes 10240 | tf_op jit(solution)/shard_map/all_gather | solution.py:89
  628.4 5.9 collective-permute-done.17
  634.4 10.6 %all_gather.86 = f32[4,512]{1,0:T(4,128)S(1)} all-gather(f32[4,128]{1,0:T(4,128)S(1)} %collective-permute-done.17), channel_id=1, replica_groups=mesh['tm'=64,'state'=4] {'state'}, dimensions={1}, use_global_device_ids=true | all-gather | bytes 10240 | tf_op jit(solution)/shard_map/all_gather | solution.py:89
  647.2 6.6 collective-permute-done.19
  653.7 10.4 %all_gather.88 = f32[4,512]{1,0:T(4,128)S(1)} all-gather(f32[4,128]{1,0:T(4,128)S(1)} %collective-permute-done.19), channel_id=1, replica_groups=mesh['tm'=64,'state'=4] {'state'}, dimensions={1}, use_global_device_ids=true | all-gather | bytes 10240 | tf_op jit(solution)/shard_map/all_gather | solution.py:89
  666.5 8.2 %collective-permute-done.21 = f32[4,128]{1,0:T(4,128)S(1)} collective-permute-done((f32[4,128]{1,0:T(4,128)S(1)}, f32[4,128]{1,0:T(4,128)S(1)}, u32[]{:S(2)}, u32[]{:S(2)}) %collective-permute-start.21) | collective-permute-done | bytes 2080 | tf_op jit(solution)/shard_map/ppermute | solution.py:10
  674.8 10.5 %all_gather.90 = f32[4,512]{1,0:T(4,128)S(1)} all-gather(f32[4,128]{1,0:T(4,128)S(1)} %collective-permute-done.21), channel_id=1, replica_groups=mesh['tm'=64,'state'=4] {'state'}, dimensions={1}, use_global_device_ids=true | all-gather | bytes 10240 | tf_op jit(solution)/shard_map/all_gather | solution.py:89
  685.5 3.7 collective-permute-start.23
  691.1 10.4 %all_gather.92 = f32[4,512]{1,0:T(4,128)S(1)} all-gather(f32[4,128]{1,0:T(4,128)S(1)} %collective-permute-done.23), channel_id=1, replica_groups=mesh['tm'=64,'state'=4] {'state'}, dimensions={1}, use_global_device_ids=true | all-gather | bytes 10240 | tf_op jit(solution)/shard_map/all_gather | solution.py:89
  705.1 3.7 collective-permute-done.25
  708.8 10.5 %all_gather.94 = f32[4,512]{1,0:T(4,128)S(1)} all-gather(f32[4,128]{1,0:T(4,128)S(1)} %collective-permute-done.25), channel_id=1, replica_groups=mesh['tm'=64,'state'=4] {'state'}, dimensions={1}, use_global_device_ids=true | all-gather | bytes 10240 | tf_op jit(solution)/shard_map/all_gather | solution.py:89
  719.6 8.7 %all_to_all.49 = f32[4,1,128]{2,1,0:T(1,128)S(1)} all-to-all(f32[4,1,128]{2,1,0:T(1,128)S(1)} %bitcast.189), channel_id=1, replica_groups=mesh['tm'=64,'state'=4] {'state'}, dimensions={0} | all-to-all | bytes 4096 | tf_op jit(solution)/shard_map/all_to_all | solution.py:100
  728.4 30.3 %while.72 = (s32[]{:T(128)}, f32[1,512]{1,0:T(1,128)S(1)}, f32[16,1,512]{2,1,0:T(1,128)S(1)}, f32[16]{0:T(128)S(1)}, f32[512,512]{1,0:T(8,128)S(1)}, /*index=5*/...) while((s32[]{:T(128)}, f32[1,512]{1,0:T(1,128)S(1)}, f32[16,1,512]{2,1,0:T(1,128)S(1)}, ...), condition=%wide.region_9.10_spmd, body=%wide.region_8.9_spmd.sunk | while | flops 3147267 | bytes 1067141 | solution.py:159
  (500 shorter events, 263.5 us)
Async XLA Ops:
  7.2 490.9 %copy-start = (f32[4,512]{1,0:T(4,128)S(1)}, f32[4,512]{1,0:T(4,128)}, u32[]{:S(2)}) copy-start(f32[4,512]{1,0:T(4,128)} %param.18) | copy-start | bytes 24580
  7.2 29.6 %all-gather.13.cloned.1.call-start = ((), (), s32[]{:S(2)}) async-start(), calls=%async_computation.3 | async-start | bytes 1310720 | tf_op jit(solution)/shard_map/all_gather | solution.py:49
  7.9 157.1 %all-gather.15.cloned.1.call-start = ((), (), s32[]{:S(2)}) async-start(), calls=%async_computation.4 | async-start | bytes 1310720 | tf_op jit(solution)/shard_map/all_gather | solution.py:88
  8.1 0.7 copy-start.16
  8.8 0.7 copy-start.18
  8.9 0.7 copy-start.17
  9.6 0.7 copy-start.15
  36.8 1.2 copy-start.3
  78.6 43.1 %collective-permute-start.16 = (f32[128,512]{1,0:T(8,128)S(1)}, f32[128,512]{1,0:T(8,128)S(1)}, u32[]{:S(2)}, u32[]{:S(2)}) collective-permute-start(f32[128,512]{1,0:T(8,128)S(1)} %get-tuple-element.499), channel_id=1, source_target_pairs={{4,0},{8,4},{12,8},{16,12},{20,16},{24,20},{28,24},{32,28},{36,32}... | collective-permute-start | bytes 786440 | tf_op jit(solution)/shard_map/ppermute | solution.py:10
  119.2 7.7 %collective-permute-start.2 = (f32[128,512]{1,0:T(8,128)S(1)}, f32[128,512]{1,0:T(8,128)S(1)}, u32[]{:S(2)}, u32[]{:S(2)}) collective-permute-start(f32[128,512]{1,0:T(8,128)S(1)} %get-tuple-element.496), channel_id=1, source_target_pairs={{0,4},{4,8},{8,12},{12,16},{16,20},{20,24},{24,28},{28,32},{32,36}... | collective-permute-start | bytes 786440 | tf_op jit(solution)/shard_map/ppermute | solution.py:10
  127.0 7.7 %collective-permute-start.4 = (f32[128,512]{1,0:T(8,128)S(1)}, f32[128,512]{1,0:T(8,128)S(1)}, u32[]{:S(2)}, u32[]{:S(2)}) collective-permute-start(f32[128,512]{1,0:T(8,128)S(1)} %get-tuple-element.664), channel_id=1, source_target_pairs={{0,4},{4,8},{8,12},{12,16},{16,20},{20,24},{24,28},{28,32},{32,36}... | collective-permute-start | bytes 786440 | tf_op jit(solution)/shard_map/ppermute | solution.py:10
  134.7 0.7 copy-start.13
  135.4 69.1 %all-gather.17.cloned.1.call-start = ((), (), s32[]{:S(2)}) async-start(), calls=%async_computation.5 | async-start | bytes 1310720 | tf_op jit(solution)/shard_map/all_gather | solution.py:88
  167.0 8.3 %collective-permute-start.6 = (f32[128,512]{1,0:T(8,128)S(1)}, f32[128,512]{1,0:T(8,128)S(1)}, u32[]{:S(2)}, u32[]{:S(2)}) collective-permute-start(f32[128,512]{1,0:T(8,128)S(1)} %convolution_select_fusion.10), channel_id=1, source_target_pairs={{0,8},{4,12},{8,16},{12,20},{16,24},{20,28},{24,32},{28,36},{32,40... | collective-permute-start | bytes 786440 | tf_op jit(solution)/shard_map/ppermute | solution.py:10
  175.3 0.7 copy-start.12
  176.0 57.2 %all-gather.27.cloned.1.call-start = ((), (), s32[]{:S(2)}) async-start(), calls=%async_computation.10 | async-start | bytes 1310720 | tf_op jit(solution)/shard_map/all_gather | solution.py:88
  176.1 5.8 collective-permute-start.18
  181.8 0.7 copy-start.10
  182.6 79.4 %all-gather.19.cloned.1.call-start = ((), (), s32[]{:S(2)}) async-start(), calls=%async_computation.6 | async-start | bytes 1310720 | tf_op jit(solution)/shard_map/all_gather | solution.py:88
  206.5 14.4 %collective-permute-start.8 = (f32[128,512]{1,0:T(8,128)S(1)}, f32[128,512]{1,0:T(8,128)S(1)}, u32[]{:S(2)}, u32[]{:S(2)}) collective-permute-start(f32[128,512]{1,0:T(8,128)S(1)} %convolution_select_fusion.9), channel_id=1, source_target_pairs={{0,16},{4,20},{8,24},{12,28},{16,32},{20,36},{24,40},{28,44},{32,4... | collective-permute-start | bytes 786440 | tf_op jit(solution)/shard_map/ppermute | solution.py:10
  220.9 0.7 copy-start.11
  221.6 69.1 %all-gather.29.cloned.1.call-start = ((), (), s32[]{:S(2)}) async-start(), calls=%async_computation.11 | async-start | bytes 1310720 | tf_op jit(solution)/shard_map/all_gather | solution.py:88
  235.2 10.4 %collective-permute-start.20 = (f32[128,512]{1,0:T(8,128)S(1)}, f32[128,512]{1,0:T(8,128)S(1)}, u32[]{:S(2)}, u32[]{:S(2)}) collective-permute-start(f32[128,512]{1,0:T(8,128)S(1)} %convolution_select_fusion.4), channel_id=1, source_target_pairs={{8,0},{12,4},{16,8},{20,12},{24,16},{28,20},{32,24},{36,28},{40,32... | collective-permute-start | bytes 786440 | tf_op jit(solution)/shard_map/ppermute | solution.py:10
  245.6 0.7 copy-start.6
  246.3 73.2 %all-gather.21.cloned.1.call-start = ((), (), s32[]{:S(2)}) async-start(), calls=%async_computation.7 | async-start | bytes 1310720 | tf_op jit(solution)/shard_map/all_gather | solution.py:88
  263.9 16.4 %collective-permute-start.10 = (f32[128,512]{1,0:T(8,128)S(1)}, f32[128,512]{1,0:T(8,128)S(1)}, u32[]{:S(2)}, u32[]{:S(2)}) collective-permute-start(f32[128,512]{1,0:T(8,128)S(1)} %convolution_select_fusion.8), channel_id=1, source_target_pairs={{0,32},{4,36},{8,40},{12,44},{16,48},{20,52},{24,56},{28,60},{32,6... | collective-permute-start | bytes 786440 | tf_op jit(solution)/shard_map/ppermute | solution.py:10
  280.3 0.7 copy-start.7
  281.1 67.3 %all-gather.31.cloned.1.call-start = ((), (), s32[]{:S(2)}) async-start(), calls=%async_computation.12 | async-start | bytes 1310720 | tf_op jit(solution)/shard_map/all_gather | solution.py:88
  292.6 15.5 %collective-permute-start.22 = (f32[128,512]{1,0:T(8,128)S(1)}, f32[128,512]{1,0:T(8,128)S(1)}, u32[]{:S(2)}, u32[]{:S(2)}) collective-permute-start(f32[128,512]{1,0:T(8,128)S(1)} %convolution_select_fusion.3), channel_id=1, source_target_pairs={{16,0},{20,4},{24,8},{28,12},{32,16},{36,20},{40,24},{44,28},{48,3... | collective-permute-start | bytes 786440 | tf_op jit(solution)/shard_map/ppermute | solution.py:10
  308.2 0.7 copy-start.8
  308.9 68.3 %all-gather.23.cloned.1.call-start = ((), (), s32[]{:S(2)}) async-start(), calls=%async_computation.8 | async-start | bytes 1310720 | tf_op jit(solution)/shard_map/all_gather | solution.py:88
  321.5 8.3 %collective-permute-start.12 = (f32[128,512]{1,0:T(8,128)S(1)}, f32[128,512]{1,0:T(8,128)S(1)}, u32[]{:S(2)}, u32[]{:S(2)}) collective-permute-start(f32[128,512]{1,0:T(8,128)S(1)} %convolution_select_fusion.7), channel_id=1, source_target_pairs={{0,64},{4,68},{8,72},{12,76},{16,80},{20,84},{24,88},{28,92},{32,9... | collective-permute-start | bytes 786440 | tf_op jit(solution)/shard_map/ppermute | solution.py:10
  329.7 0.7 copy-start.9
  330.5 149.3 %all-gather.33.cloned.1.call-start = ((), (), s32[]{:S(2)}) async-start(), calls=%async_computation.13 | async-start | bytes 1310720 | tf_op jit(solution)/shard_map/all_gather | solution.py:88
  350.3 17.4 %collective-permute-start.24 = (f32[128,512]{1,0:T(8,128)S(1)}, f32[128,512]{1,0:T(8,128)}, u32[]{:S(2)}, u32[]{:S(2)}) collective-permute-start(f32[128,512]{1,0:T(8,128)S(1)} %convolution_select_fusion.2), channel_id=1, source_target_pairs={{32,0},{36,4},{40,8},{44,12},{48,16},{52,20},{56,24},{60,28},{64,3... | collective-permute-start | bytes 786440 | tf_op jit(solution)/shard_map/ppermute | solution.py:10
  367.8 128.3 %all-gather.25.cloned.1.call-start = ((), (), s32[]{:S(2)}) async-start(), calls=%async_computation.9 | async-start | bytes 1310720 | tf_op jit(solution)/shard_map/all_gather | solution.py:88
  379.2 0.7 copy-start.1
  379.9 7.9 %collective-permute-start.13 = (f32[128,512]{1,0:T(8,128)S(1)}, f32[128,512]{1,0:T(8,128)}, u32[]{:S(2)}, u32[]{:S(2)}) collective-permute-start(f32[128,512]{1,0:T(8,128)S(1)} %convolution_select_fusion.6), channel_id=1, source_target_pairs={{0,128},{4,132},{8,136},{12,140},{16,144},{20,148},{24,152},{28,15... | collective-permute-start | bytes 786440 | tf_op jit(solution)/shard_map/ppermute | solution.py:10
  384.6 4.9 collective-permute-start
  389.5 4.9 collective-permute-start.1
  405.2 6.5 collective-permute-start.3
  422.4 6.5 collective-permute-start.5
  439.6 9.5 %collective-permute-start.7 = (f32[4,128]{1,0:T(4,128)S(1)}, f32[4,128]{1,0:T(4,128)S(1)}, u32[]{:S(2)}, u32[]{:S(2)}) collective-permute-start(f32[4,128]{1,0:T(4,128)S(1)} %fusion.32), channel_id=1, source_target_pairs={{0,32},{4,36},{8,40},{12,44},{16,48},{20,52},{24,56},{28,60},{32,6... | collective-permute-start | bytes 6152 | tf_op jit(solution)/shard_map/ppermute | solution.py:10
  459.8 5.5 collective-permute-start.9
  476.3 19.8 %copy-start.2 = (f32[128,512]{1,0:T(8,128)S(1)}, f32[128,512]{1,0:T(8,128)}, u32[]{:S(2)}) copy-start(f32[128,512]{1,0:T(8,128)} %copy-done.1) | copy-start | bytes 786436
  476.3 9.2 %collective-permute-start.11 = (f32[4,128]{1,0:T(4,128)S(1)}, f32[4,128]{1,0:T(4,128)S(1)}, u32[]{:S(2)}, u32[]{:S(2)}) collective-permute-start(f32[4,128]{1,0:T(4,128)S(1)} %fusion.30), channel_id=1, source_target_pairs={{0,128},{4,132},{8,136},{12,140},{16,144},{20,148},{24,152},{28,15... | collective-permute-start | bytes 6152 | tf_op jit(solution)/shard_map/ppermute | solution.py:10
  481.8 21.1 %collective-permute-start.26 = (f32[128,512]{1,0:T(8,128)S(1)}, f32[128,512]{1,0:T(8,128)S(1)}, u32[]{:S(2)}, u32[]{:S(2)}) collective-permute-start(f32[128,512]{1,0:T(8,128)S(1)} %convolution_select_fusion.1), channel_id=1, source_target_pairs={{64,0},{68,4},{72,8},{76,12},{80,16},{84,20},{88,24},{92,28},{96,3... | collective-permute-start | bytes 786440 | tf_op jit(solution)/shard_map/ppermute | solution.py:10
  499.3 8.8 %all-to-all-start = ((f32[4,1,128]{2,1,0:T(1,128)}), f32[4,1,128]{2,1,0:T(1,128)S(1)}, u32[]{:S(2)}, u32[]{:S(2)}) async-start(f32[4,1,128]{2,1,0:T(1,128)} %bitcast.18), calls=%async_computation | async-start | bytes 4096 | tf_op jit(solution)/shard_map/all_to_all | solution.py:100
  502.9 200.3 %all-gather.35.cloned.1.call-start = ((), (), s32[]{:S(2)}) async-start(), calls=%async_computation.14 | async-start | bytes 1310720 | tf_op jit(solution)/shard_map/all_gather | solution.py:88
  502.9 0.7 copy-start.5
  563.5 1.0 copy-start.4
  603.0 3.2 collective-permute-start.14
  606.2 9.6 %collective-permute-start.15 = (f32[4,128]{1,0:T(4,128)S(1)}, f32[4,128]{1,0:T(4,128)S(1)}, u32[]{:S(2)}, u32[]{:S(2)}) collective-permute-start(f32[4,128]{1,0:T(4,128)S(1)} %broadcast_select_fusion.2), channel_id=1, source_target_pairs={{4,0},{8,4},{12,8},{16,12},{20,16},{24,20},{28,24},{32,28},{36,32}... | collective-permute-start | bytes 6152 | tf_op jit(solution)/shard_map/ppermute | solution.py:10
  626.4 7.9 %collective-permute-start.17 = (f32[4,128]{1,0:T(4,128)S(1)}, f32[4,128]{1,0:T(4,128)S(1)}, u32[]{:S(2)}, u32[]{:S(2)}) collective-permute-start(f32[4,128]{1,0:T(4,128)S(1)} %fusion.27), channel_id=1, source_target_pairs={{8,0},{12,4},{16,8},{20,12},{24,16},{28,20},{32,24},{36,28},{40,32... | collective-permute-start | bytes 6152 | tf_op jit(solution)/shard_map/ppermute | solution.py:10
  645.2 8.6 %collective-permute-start.19 = (f32[4,128]{1,0:T(4,128)S(1)}, f32[4,128]{1,0:T(4,128)S(1)}, u32[]{:S(2)}, u32[]{:S(2)}) collective-permute-start(f32[4,128]{1,0:T(4,128)S(1)} %fusion.26), channel_id=1, source_target_pairs={{16,0},{20,4},{24,8},{28,12},{32,16},{36,20},{40,24},{44,28},{48,3... | collective-permute-start | bytes 6152 | tf_op jit(solution)/shard_map/ppermute | solution.py:10
  664.4 10.4 %collective-permute-start.21 = (f32[4,128]{1,0:T(4,128)S(1)}, f32[4,128]{1,0:T(4,128)S(1)}, u32[]{:S(2)}, u32[]{:S(2)}) collective-permute-start(f32[4,128]{1,0:T(4,128)S(1)} %fusion.25), channel_id=1, source_target_pairs={{32,0},{36,4},{40,8},{44,12},{48,16},{52,20},{56,24},{60,28},{64,3... | collective-permute-start | bytes 6152 | tf_op jit(solution)/shard_map/ppermute | solution.py:10
  685.5 5.5 collective-permute-start.23
  701.8 7.1 collective-permute-start.25
  758.7 0.6 copy-start.14
Sparse Core Ops, SparseCore 0:
  9.8 26.9 all-gather.12
  135.6 29.4 all-gather.14
  176.1 28.3 all-gather.16
  206.2 27.0 all-gather.26
  234.9 27.0 all-gather.18
  263.6 27.0 all-gather.28
  292.5 27.0 all-gather.20
  321.3 27.0 all-gather.30
  350.2 27.0 all-gather.22
  378.9 26.9 all-gather.32
  407.7 27.1 all-gather.24
  505.1 30.8 all-gather.34
where the time goes:
time: 770 us; the launch traced here: 766 us
  waiting for transfers between devices  283 us (37%)
  blocking collectives  143 us (19%)
  matrix products  117 us (15%)
  starting transfers between devices  91.8 us (12%)
  local copies, waits for them, and re-layouts  61 us (8%)
  other arithmetic  53.3 us (7%)
  between operations  14.8 us (2%)
    all_gather x12, blocking collectives, doubling(): lax.all_gather(arrived[1], 'state', axis=1, tiled=True)  126 us
    all_gather x11, waiting for transfers between devices, doubling(): lax.all_gather(arrived[0], 'state', axis=0, tiled=True)  126 us
    ppermute x27, waiting for transfers between devices, passed_along(): return lax.ppermute(block, axis, route)  126 us
    ppermute x27, starting transfers between devices, passed_along(): return lax.ppermute(block, axis, route)  87.8 us
    dot_general x46, matrix products, transposed(): lax.dot_general(left, right, (((1,), (1,)), ((), ())), precision=lax.Prec...  59.6 us
    dot_general x76, matrix products, product(): jnp.dot(left, right, precision=lax.Precision.HIGHEST, preferred_element_t...  57.1 us
    dynamic_slice x112, local copies, waits for them, and re-layouts, per_device(): lax.scan(filter_portion, (owned_rows, initial_shifts), (observed_masks, s...  49.2 us
    all_gather x1, waiting for transfers between devices, per_device(): lax.all_gather(dynamics, 'state', axis=0, tiled=True) * block_mask  26.4 us
  transfers between devices with their start and end apart: 40, of which 34 were waited for; matrix products, arithmetic and copies ran while one was open for 19% of the time, Pallas kernels for 0%

commit v1 on v0

v1 whole, which is shorter than its diff:
```python
import jax
import jax.numpy as jnp
from jax import lax
from jax.sharding import PartitionSpec as P

AXES = ("tm", "state")


def product(left, right):
    return jnp.dot(left, right, precision=lax.Precision.HIGHEST, preferred_element_type=jnp.float32)


def transposed(left, right):
    return lax.dot_general(
        left,
        right,
        (((1,), (1,)), ((), ())),
        precision=lax.Precision.HIGHEST,
        preferred_element_type=jnp.float32,
    )


def leading(left, right):
    return lax.dot_general(
        left,
        right,
        (((0,), (0,)), ((), ())),
        precision=lax.Precision.HIGHEST,
        preferred_element_type=jnp.float32,
    )


def shifted(block, distance, total):
    route = [(i, i + distance) for i in range(total) if 0 <= i + distance < total]
    return lax.ppermute(block, AXES, route)


def per_device(dynamics, pattern, initial_mean, observed, obs_index, obs_noise):
    state_width = dynamics.shape[1]
    blocks = pattern.shape[0]
    block_span = state_width // blocks
    seq_total = initial_mean.shape[0]
    members = lax.axis_size("state")
    segments = lax.axis_size("tm") * members
    member = lax.axis_index("state")
    segment = lax.axis_index(AXES)
    span = observed.shape[0] // members
    steps_total = span * segments

    present = jnp.maximum(pattern, jnp.eye(blocks, dtype=jnp.int32))
    block_mask = jnp.repeat(jnp.repeat(present, block_span, 0), block_span, 1).astype(jnp.float32)
    transition = lax.all_gather(dynamics, "state", axis=0, tiled=True) * block_mask

    first = member * span
    obs_here = lax.dynamic_slice_in_dim(observed, first, span, 0)
    index_here = lax.dynamic_slice_in_dim(obs_index, first, span, 0)
    noise_here = lax.dynamic_slice_in_dim(obs_noise, first, span, 0)
    gains = 1.0 / (1.0 + noise_here)
    state_index = jnp.arange(state_width, dtype=jnp.int32)
    hits = (state_index[None, :] == index_here[:, None]).astype(jnp.float32)
    scales = 1.0 - gains[:, None] * hits
    global_step = segment * span + jnp.arange(span, dtype=jnp.int32)
    keeps = jnp.where(global_step == steps_total - 1, 0.0, 1.0).astype(jnp.float32)
    pushes = [(gains[j] * obs_here[j])[:, None] * hits[j][None, :] for j in range(span)]

    filt_a = transition * scales[0][:, None]
    filt_b = pushes[0]
    for j in range(1, span):
        filt_a = product(transition, filt_a) * scales[j][:, None]
        filt_b = transposed(filt_b, transition) * scales[j][None, :] + pushes[j]
    last = span - 1
    smooth_q = keeps[last] * (transition.T * scales[last][:, None])
    for j in range(last - 1, -1, -1):
        smooth_q = keeps[j] * (leading(transition, smooth_q) * scales[j][:, None])

    levels = 0
    while 2 ** (levels + 1) < segments:
        levels += 1
    stored_q = []
    for level in range(levels):
        distance = 2**level
        arrived_a, arrived_b = shifted((filt_a, filt_b), distance, segments)
        arrived_q = shifted(smooth_q, -distance, segments)
        usable = segment >= distance
        new_a = product(filt_a, arrived_a)
        new_b = transposed(arrived_b, filt_a) + filt_b
        filt_a = jnp.where(usable, new_a, filt_a)
        filt_b = jnp.where(usable, new_b, filt_b)
        stored_q.append(smooth_q)
        smooth_q = jnp.where(segment + distance < segments, product(smooth_q, arrived_q), smooth_q)
    stored_q.append(smooth_q)

    top = 2**levels
    prefix = transposed(initial_mean, filt_a) + filt_b
    if top < segments:
        arrived = shifted(prefix, top, segments)
        prefix = jnp.where(segment >= top, transposed(arrived, filt_a) + filt_b, prefix)
    entry = jnp.where(segment == 0, initial_mean, shifted(prefix, 1, segments))

    filtered = []
    current = entry
    for j in range(span):
        current = transposed(current, transition) * scales[j][None, :] + pushes[j]
        filtered.append(current)
    filtered = jnp.stack(filtered)
    mapped = product(
        transposed(filtered.reshape(span * seq_total, state_width), transition), transition
    ).reshape(span, seq_total, state_width)
    gaps = filtered - keeps[:, None, None] * mapped * scales[:, None, :]

    offsets = jnp.zeros((seq_total, state_width), jnp.float32)
    for j in range(last, -1, -1):
        offsets = keeps[j] * product(offsets, transition) * scales[j][None, :] + gaps[j]
    for level in range(levels):
        distance = 2**level
        arrived = shifted(offsets, -distance, segments)
        offsets = jnp.where(
            segment + distance < segments, transposed(arrived, stored_q[level]) + offsets, offsets
        )
    if top < segments:
        arrived = shifted(offsets, -top, segments)
        offsets = jnp.where(
            segment + top < segments, transposed(arrived, stored_q[levels]) + offsets, offsets
        )
    current = shifted(offsets, -1, segments)

    smoothed = [None] * span
    for j in range(last, -1, -1):
        current = keeps[j] * product(current, transition) * scales[j][None, :] + gaps[j]
        smoothed[j] = current
    smoothed = jnp.stack(smoothed)

    both = jnp.stack([filtered, smoothed])
    both = lax.all_to_all(both, "state", split_axis=2, concat_axis=1, tiled=True)
    return (both[0], both[1])


def solution(mesh):
    return jax.shard_map(
        per_device,
        mesh=mesh,
        in_specs=(P("state", None), P(), P(), P("tm", None), P("tm"), P("tm")),
        out_specs=(P("tm", "state", None), P("tm", "state", None)),
        check_vma=False,
    )
```

time: 770 us -> 532 us (0.69)
  blocking collectives: 143 us -> 9.88 us
  local copies, waits for them, and re-layouts: 61 us -> 6.3 us
  starting transfers between devices: 91.8 us -> 143 us
  other arithmetic: 53.3 us -> 3.34 us
  waiting for transfers between devices: 283 us -> 234 us
    all_gather x12 -> x0, blocking collectives: 126 us -> none  [doubling(): lax.all_gather(arrived[1], 'state', axis=1, tiled=True)]
    all_gather x11 -> x0, waiting for transfers between devices: 126 us -> none  [doubling(): lax.all_gather(arrived[0], 'state', axis=0, tiled=True)]
    ppermute x27 -> x32, waiting for transfers between devices: 126 us -> 206 us  [shifted(): return lax.ppermute(block, AXES, route)]
    ppermute x27 -> x32, starting transfers between devices: 87.8 us -> 143 us  [shifted(): return lax.ppermute(block, AXES, route)]
    dynamic_slice x113 -> x2, local copies, waits for them, and re-layouts: 49.2 us -> 0.15 us  [the longest x1 0.08 us: per_device(): obs_here = lax.dynamic_slice_in_dim(observed, first, span, 0)]
    mul x64 -> x1, other arithmetic: 50.8 us -> 2.76 us  [per_device(): gains[j] * obs_here[j]]
    dot_general x46 -> x25, matrix products: 59.6 us -> 35.1 us  [transposed(): lax.dot_general(left, right, (((1,), (1,)), ((), ())), precision=lax.Prec...]
    dot_general x0 -> x3, matrix products: none -> 9.98 us  [leading(): lax.dot_general(left, right, (((0,), (0,)), ((), ())), precision=lax.Prec...]
  transfers between devices with their start and end apart: 40 -> 33, of which waited for: 34 -> 20; matrix products, arithmetic and copies ran while one was open for 19% -> 19% of each run, Pallas kernels for 0% -> 0%
where the time goes in v1:
time: 532 us; the launch traced here: 523 us
  waiting for transfers between devices  234 us (44%)
  starting transfers between devices  143 us (27%)
  matrix products  111 us (21%)
  between operations  15.2 us (3%)
  blocking collectives  9.88 us (2%)
  local copies, waits for them, and re-layouts  6.3 us (1%)
    ppermute x32, waiting for transfers between devices, shifted(): return lax.ppermute(block, AXES, route)  206 us
    ppermute x32, starting transfers between devices, shifted(): return lax.ppermute(block, AXES, route)  143 us
    dot_general x26, matrix products, product(): jnp.dot(left, right, precision=lax.Precision.HIGHEST, preferred_element_t...  66.1 us
    dot_general x25, matrix products, transposed(): lax.dot_general(left, right, (((1,), (1,)), ((), ())), precision=lax.Prec...  35.1 us
    all_gather x1, waiting for transfers between devices, per_device(): lax.all_gather(dynamics, 'state', axis=0, tiled=True) * block_mask  27.4 us
  transfers between devices with their start and end apart: 33, of which 20 were waited for; matrix products, arithmetic and copies ran while one was open for 19% of the time, Pallas kernels for 0%

profile of v1, /device:TPU:232, one launch (start us, length us, event | category | flops | bytes accessed | tf_op | source)
XLA Modules:
  0.0 522.6 jit_solution(9289157682158466495)
XLA Ops:
  9.4 27.4 %all-gather.2.cloned.1.call-done = f32[512,512]{1,0:T(8,128)} async-done(((f32[128,512]{1,0:T(8,128)}), f32[512,512]{1,0:T(8,128)}) %all-gather.2.cloned.1.call-update) | async-done | bytes 1048592 | tf_op jit(solution)/shard_map/all_gather | solution.py:52
  43.9 2.2 collective-permute-start
  46.2 20.8 %collective-permute-done = f32[512,512]{1,0:T(8,128)} collective-permute-done((f32[512,512]{1,0:T(8,128)S(1)}, f32[512,512]{1,0:T(8,128)}, u32[]{:S(2)}, u32[]{:S(2)}) %collective-permute-start) | collective-permute-done | bytes 1048608 | tf_op jit(solution)/shard_map/ppermute | solution.py:35
  67.0 3.1 convolution_select_fusion.13
  70.1 6.3 %collective-permute-start.1 = (f32[512,512]{1,0:T(8,128)S(1)}, f32[512,512]{1,0:T(8,128)}, u32[]{:S(2)}, u32[]{:S(2)}) collective-permute-start(f32[512,512]{1,0:T(8,128)S(1)} %convolution_select_fusion.13), channel_id=1, source_target_pairs={{0,2},{1,3},{2,4},{3,5},{4,6},{5,7},{6,8},{7,9},{8,10},{9,11},{10,... | collective-permute-start | bytes 3145736 | tf_op jit(solution)/shard_map/ppermute | solution.py:35
  77.1 22.1 %collective-permute-done.1 = f32[512,512]{1,0:T(8,128)} collective-permute-done((f32[512,512]{1,0:T(8,128)S(1)}, f32[512,512]{1,0:T(8,128)}, u32[]{:S(2)}, u32[]{:S(2)}) %collective-permute-start.1) | collective-permute-done | bytes 1048608 | tf_op jit(solution)/shard_map/ppermute | solution.py:35
  99.2 3.1 convolution_select_fusion.12
  102.3 2.7 collective-permute-start.2
  105.0 4.9 fusion.7
  109.9 2.5 fusion.6
  112.4 2.6 fusion.5
  115.0 3.1 collective-permute-start.18
  118.9 2.9 convolution_select_fusion.11
  121.8 4.9 collective-permute-start.3
  126.6 2.8 multiply_reduce_fusion
  129.5 13.0 %collective-permute-done.18 = f32[512,512]{1,0:T(8,128)} collective-permute-done((f32[512,512]{1,0:T(8,128)S(1)}, f32[512,512]{1,0:T(8,128)}, u32[]{:S(2)}, u32[]{:S(2)}) %collective-permute-start.18) | collective-permute-done | bytes 1048608 | tf_op jit(solution)/shard_map/ppermute | solution.py:35
  142.4 3.1 convolution_select_fusion.6
  145.5 6.5 %collective-permute-start.20 = (f32[512,512]{1,0:T(8,128)S(1)}, f32[512,512]{1,0:T(8,128)S(1)}, u32[]{:S(2)}, u32[]{:S(2)}) collective-permute-start(f32[512,512]{1,0:T(8,128)S(1)} %convolution_select_fusion.6), channel_id=1, source_target_pairs={{2,0},{3,1},{4,2},{5,3},{6,4},{7,5},{8,6},{9,7},{10,8},{11,9},{12,... | collective-permute-start | bytes 3145736 | tf_op jit(solution)/shard_map/ppermute | solution.py:35
  153.0 3.7 convolution_select_fusion.10
  156.8 3.3 collective-permute-start.4
  164.1 11.0 %collective-permute-done.20 = f32[512,512]{1,0:T(8,128)S(1)} collective-permute-done((f32[512,512]{1,0:T(8,128)S(1)}, f32[512,512]{1,0:T(8,128)S(1)}, u32[]{:S(2)}, u32[]{:S(2)}) %collective-permute-start.20) | collective-permute-done | bytes 1048608 | tf_op jit(solution)/shard_map/ppermute | solution.py:35
  175.1 2.9 convolution_select_fusion.5
  177.9 2.4 collective-permute-start.22
  180.3 21.0 %collective-permute-done.7 = f32[4,512]{1,0:T(4,128)S(1)} collective-permute-done((f32[4,512]{1,0:T(4,128)S(1)}, f32[4,512]{1,0:T(4,128)S(1)}, u32[]{:S(2)}, u32[]{:S(2)}) %collective-permute-start.7) | collective-permute-done | bytes 8224 | tf_op jit(solution)/shard_map/ppermute | solution.py:35
  204.3 2.8 collective-permute-done.4
  207.2 2.9 convolution_select_fusion.9
  210.0 9.3 %collective-permute-start.5 = (f32[512,512]{1,0:T(8,128)}, f32[512,512]{1,0:T(8,128)}, u32[]{:S(2)}, u32[]{:S(2)}) collective-permute-start(f32[512,512]{1,0:T(8,128)} %convolution_select_fusion.9), channel_id=1, source_target_pairs={{0,32},{1,33},{2,34},{3,35},{4,36},{5,37},{6,38},{7,39},{8,40},{9,... | collective-permute-start | bytes 3145736 | tf_op jit(solution)/shard_map/ppermute | solution.py:35
  222.3 11.1 %collective-permute-done.9 = f32[4,512]{1,0:T(4,128)S(1)} collective-permute-done((f32[4,512]{1,0:T(4,128)S(1)}, f32[4,512]{1,0:T(4,128)S(1)}, u32[]{:S(2)}, u32[]{:S(2)}) %collective-permute-start.9) | collective-permute-done | bytes 8224 | tf_op jit(solution)/shard_map/ppermute | solution.py:35
  233.4 2.2 fusion.43
  235.6 2.1 collective-permute-start.10
  237.7 4.7 convolution_select_fusion.4
  242.4 3.9 collective-permute-start.24
  246.3 14.5 %collective-permute-done.10 = f32[4,512]{1,0:T(4,128)S(1)} collective-permute-done((f32[4,512]{1,0:T(4,128)S(1)}, f32[4,512]{1,0:T(4,128)S(1)}, u32[]{:S(2)}, u32[]{:S(2)}) %collective-permute-start.10) | collective-permute-done | bytes 8224 | tf_op jit(solution)/shard_map/ppermute | solution.py:35
  260.8 2.2 fusion.42
  263.0 18.0 %collective-permute-start.11 = (f32[4,512]{1,0:T(4,128)S(1)}, f32[4,512]{1,0:T(4,128)S(1)}, u32[]{:S(2)}, u32[]{:S(2)}) collective-permute-start(f32[4,512]{1,0:T(4,128)S(1)} %fusion.42), channel_id=1, source_target_pairs={{0,16},{1,17},{2,18},{3,19},{4,20},{5,21},{6,22},{7,23},{8,24},{9,... | collective-permute-start | bytes 24584 | tf_op jit(solution)/shard_map/ppermute | solution.py:35
  281.0 4.7 convolution_select_fusion.8
  288.6 2.5 collective-permute-start.12
  291.1 6.9 %collective-permute-done.12 = f32[4,512]{1,0:T(4,128)S(1)} collective-permute-done((f32[4,512]{1,0:T(4,128)S(1)}, f32[4,512]{1,0:T(4,128)S(1)}, u32[]{:S(2)}, u32[]{:S(2)}) %collective-permute-start.12) | collective-permute-done | bytes 8224 | tf_op jit(solution)/shard_map/ppermute | solution.py:35
  298.0 2.2 fusion.40
  302.1 4.7 convolution_select_fusion.3
  306.8 4.8 collective-permute-start.26
  311.7 2.2 fusion.39
  313.9 3.7 convolution_select_fusion.7
  322.2 2.2 fusion.38
  324.4 4.4 collective-permute-start.15
  328.8 30.4 %collective-permute-done.26 = f32[512,512]{1,0:T(8,128)} collective-permute-done((f32[512,512]{1,0:T(8,128)}, f32[512,512]{1,0:T(8,128)}, u32[]{:S(2)}, u32[]{:S(2)}) %collective-permute-start.26) | collective-permute-done | bytes 1048608 | tf_op jit(solution)/shard_map/ppermute | solution.py:35
  359.3 4.7 convolution_select_fusion.2
  378.5 20.1 %collective-permute-done.16 = f32[4,512]{1,0:T(4,128)S(1)} collective-permute-done((f32[4,512]{1,0:T(4,128)S(1)}, f32[4,512]{1,0:T(4,128)S(1)}, u32[]{:S(2)}, u32[]{:S(2)}) %collective-permute-start.16) | collective-permute-done | bytes 8224 | tf_op jit(solution)/shard_map/ppermute | solution.py:35
  399.6 32.2 %collective-permute-start.17 = (f32[4,512]{1,0:T(4,128)S(1)}, f32[4,512]{1,0:T(4,128)S(1)}, u32[]{:S(2)}, u32[]{:S(2)}) collective-permute-start(f32[4,512]{1,0:T(4,128)S(1)} %fusion.24), channel_id=1, source_target_pairs={{2,0},{3,1},{4,2},{5,3},{6,4},{7,5},{8,6},{9,7},{10,8},{11,9},{12,... | collective-permute-start | bytes 24584 | tf_op jit(solution)/shard_map/ppermute | solution.py:35
  434.1 3.3 collective-permute-start.19
  437.5 3.7 convolution_select_fusion.1
  441.2 2.2 collective-permute-start.30
  443.4 2.2 fusion.22
  445.6 4.6 collective-permute-start.21
  450.2 3.1 collective-permute-done.21
  453.3 2.2 fusion.21
  457.4 6.7 %collective-permute-done.23 = f32[4,512]{1,0:T(4,128)S(1)} collective-permute-done((f32[4,512]{1,0:T(4,128)S(1)}, f32[4,512]{1,0:T(4,128)S(1)}, u32[]{:S(2)}, u32[]{:S(2)}) %collective-permute-start.23) | collective-permute-done | bytes 8224 | tf_op jit(solution)/shard_map/ppermute | solution.py:35
  464.2 2.2 fusion.20
  468.3 8.4 %collective-permute-done.25 = f32[4,512]{1,0:T(4,128)S(1)} collective-permute-done((f32[4,512]{1,0:T(4,128)S(1)}, f32[4,512]{1,0:T(4,128)S(1)}, u32[]{:S(2)}, u32[]{:S(2)}) %collective-permute-start.25) | collective-permute-done | bytes 8224 | tf_op jit(solution)/shard_map/ppermute | solution.py:35
  476.7 2.2 fusion.19
  480.8 3.6 collective-permute-done.27
  488.6 3.9 collective-permute-done.29
  495.3 3.6 collective-permute-done.31
  504.1 9.9 %all_to_all.15 = f32[2,4,4,512]{3,1,0,2:T(4,128)S(1)} all-to-all(f32[2,4,4,512]{3,1,0,2:T(4,128)S(1)} %copy.10), channel_id=1, replica_groups=mesh['tm'=64,'state'=4] {'state'}, dimensions={2} | all-to-all | bytes 131072 | tf_op jit(solution)/shard_map/all_to_all | solution.py:134
  (111 shorter events, 68.0 us)
Async XLA Ops:
  7.2 111.0 %copy-start = (f32[16,4]{0,1:T(4,128)S(1)}, f32[16,4]{0,1:T(4,128)}, u32[]{:S(2)}) copy-start(f32[16,4]{0,1:T(4,128)} %param.9) | copy-start | bytes 772
  7.2 29.6 %all-gather.2.cloned.1.call-start = ((), (), s32[]{:S(2)}) async-start(), calls=%async_computation.1 | async-start | bytes 1310720 | tf_op jit(solution)/shard_map/all_gather | solution.py:52
  7.9 0.8 copy-start.13
  7.9 0.7 copy-start.12
  8.6 0.7 copy-start.11
  36.8 1.2 copy-start.9
  43.9 26.1 %copy-start.7 = (f32[512,512]{1,0:T(8,128)}, f32[512,512]{1,0:T(8,128)S(1)}, u32[]{:S(2)}) copy-start(f32[512,512]{1,0:T(8,128)S(1)} %convolution_multiply_fusion.3) | copy-start | bytes 3145732
  43.9 23.0 %collective-permute-start = (f32[512,512]{1,0:T(8,128)S(1)}, f32[512,512]{1,0:T(8,128)}, u32[]{:S(2)}, u32[]{:S(2)}) collective-permute-start(f32[512,512]{1,0:T(8,128)S(1)} %convolution_multiply_fusion.3), channel_id=1, source_target_pairs={{0,1},{1,2},{2,3},{3,4},{4,5},{5,6},{6,7},{7,8},{8,9},{9,10},{10,1... | collective-permute-start | bytes 3145736 | tf_op jit(solution)/shard_map/ppermute | solution.py:35
  70.1 32.2 %copy-start.1 = (f32[512,512]{1,0:T(8,128)}, f32[512,512]{1,0:T(8,128)S(1)}, u32[]{:S(2)}) copy-start(f32[512,512]{1,0:T(8,128)S(1)} %convolution_select_fusion.13) | copy-start | bytes 3145732
  70.1 29.1 %collective-permute-start.1 = (f32[512,512]{1,0:T(8,128)S(1)}, f32[512,512]{1,0:T(8,128)}, u32[]{:S(2)}, u32[]{:S(2)}) collective-permute-start(f32[512,512]{1,0:T(8,128)S(1)} %convolution_select_fusion.13), channel_id=1, source_target_pairs={{0,2},{1,3},{2,4},{3,5},{4,6},{5,7},{6,8},{7,9},{8,10},{9,11},{10,... | collective-permute-start | bytes 3145736 | tf_op jit(solution)/shard_map/ppermute | solution.py:35
  102.3 16.6 %copy-start.3 = (f32[512,512]{1,0:T(8,128)}, f32[512,512]{1,0:T(8,128)S(1)}, u32[]{:S(2)}) copy-start(f32[512,512]{1,0:T(8,128)S(1)} %convolution_select_fusion.12) | copy-start | bytes 3145732
  102.3 16.6 %collective-permute-start.2 = (f32[512,512]{1,0:T(8,128)S(1)}, f32[512,512]{1,0:T(8,128)S(1)}, u32[]{:S(2)}, u32[]{:S(2)}) collective-permute-start(f32[512,512]{1,0:T(8,128)S(1)} %convolution_select_fusion.12), channel_id=1, source_target_pairs={{0,4},{1,5},{2,6},{3,7},{4,8},{5,9},{6,10},{7,11},{8,12},{9,13},{1... | collective-permute-start | bytes 3145736 | tf_op jit(solution)/shard_map/ppermute | solution.py:35
  115.0 27.5 %collective-permute-start.18 = (f32[512,512]{1,0:T(8,128)S(1)}, f32[512,512]{1,0:T(8,128)}, u32[]{:S(2)}, u32[]{:S(2)}) collective-permute-start(f32[512,512]{1,0:T(8,128)S(1)} %fusion.5), channel_id=1, source_target_pairs={{1,0},{2,1},{3,2},{4,3},{5,4},{6,5},{7,6},{8,7},{9,8},{10,9},{11,1... | collective-permute-start | bytes 3145736 | tf_op jit(solution)/shard_map/ppermute | solution.py:35
  121.8 31.3 %collective-permute-start.3 = (f32[512,512]{1,0:T(8,128)}, f32[512,512]{1,0:T(8,128)}, u32[]{:S(2)}, u32[]{:S(2)}) collective-permute-start(f32[512,512]{1,0:T(8,128)} %convolution_select_fusion.11), channel_id=1, source_target_pairs={{0,8},{1,9},{2,10},{3,11},{4,12},{5,13},{6,14},{7,15},{8,16},{9,17... | collective-permute-start | bytes 3145736 | tf_op jit(solution)/shard_map/ppermute | solution.py:35
  145.5 29.5 %collective-permute-start.20 = (f32[512,512]{1,0:T(8,128)S(1)}, f32[512,512]{1,0:T(8,128)S(1)}, u32[]{:S(2)}, u32[]{:S(2)}) collective-permute-start(f32[512,512]{1,0:T(8,128)S(1)} %convolution_select_fusion.6), channel_id=1, source_target_pairs={{2,0},{3,1},{4,2},{5,3},{6,4},{7,5},{8,6},{9,7},{10,8},{11,9},{12,... | collective-permute-start | bytes 3145736 | tf_op jit(solution)/shard_map/ppermute | solution.py:35
  156.8 50.4 %copy-start.4 = (f32[512,512]{1,0:T(8,128)}, f32[512,512]{1,0:T(8,128)S(1)}, u32[]{:S(2)}) copy-start(f32[512,512]{1,0:T(8,128)S(1)} %convolution_select_fusion.10) | copy-start | bytes 3145732
  156.8 50.4 %collective-permute-start.4 = (f32[512,512]{1,0:T(8,128)S(1)}, f32[512,512]{1,0:T(8,128)S(1)}, u32[]{:S(2)}, u32[]{:S(2)}) collective-permute-start(f32[512,512]{1,0:T(8,128)S(1)} %convolution_select_fusion.10), channel_id=1, source_target_pairs={{0,16},{1,17},{2,18},{3,19},{4,20},{5,21},{6,22},{7,23},{8,24},{9,... | collective-permute-start | bytes 3145736 | tf_op jit(solution)/shard_map/ppermute | solution.py:35
  162.0 39.3 %copy-start.8 = (f32[512,512]{1,0:T(8,128)S(1)}, f32[512,512]{1,0:T(8,128)}, u32[]{:S(2)}) copy-start(f32[512,512]{1,0:T(8,128)} %copy-done.7) | copy-start | bytes 3145732
  162.0 39.3 %collective-permute-start.7 = (f32[4,512]{1,0:T(4,128)S(1)}, f32[4,512]{1,0:T(4,128)S(1)}, u32[]{:S(2)}, u32[]{:S(2)}) collective-permute-start(f32[4,512]{1,0:T(4,128)S(1)} %fusion.46), channel_id=1, source_target_pairs={{0,1},{1,2},{2,3},{3,4},{4,5},{5,6},{6,7},{7,8},{8,9},{9,10},{10,1... | collective-permute-start | bytes 24584 | tf_op jit(solution)/shard_map/ppermute | solution.py:35
  177.9 59.8 %collective-permute-start.22 = (f32[512,512]{1,0:T(8,128)}, f32[512,512]{1,0:T(8,128)}, u32[]{:S(2)}, u32[]{:S(2)}) collective-permute-start(f32[512,512]{1,0:T(8,128)} %convolution_select_fusion.5), channel_id=1, source_target_pairs={{4,0},{5,1},{6,2},{7,3},{8,4},{9,5},{10,6},{11,7},{12,8},{13,9},{1... | collective-permute-start | bytes 3145736 | tf_op jit(solution)/shard_map/ppermute | solution.py:35
  202.3 17.1 %copy-start.2 = (f32[512,512]{1,0:T(8,128)S(1)}, f32[512,512]{1,0:T(8,128)}, u32[]{:S(2)}) copy-start(f32[512,512]{1,0:T(8,128)} %copy-done.1) | copy-start | bytes 3145732
  202.3 17.1 %collective-permute-start.8 = (f32[4,512]{1,0:T(4,128)S(1)}, f32[4,512]{1,0:T(4,128)S(1)}, u32[]{:S(2)}, u32[]{:S(2)}) collective-permute-start(f32[4,512]{1,0:T(4,128)S(1)} %fusion.45), channel_id=1, source_target_pairs={{0,2},{1,3},{2,4},{3,5},{4,6},{5,7},{6,8},{7,9},{8,10},{9,11},{10,... | collective-permute-start | bytes 24584 | tf_op jit(solution)/shard_map/ppermute | solution.py:35
  210.0 70.9 %collective-permute-start.5 = (f32[512,512]{1,0:T(8,128)}, f32[512,512]{1,0:T(8,128)}, u32[]{:S(2)}, u32[]{:S(2)}) collective-permute-start(f32[512,512]{1,0:T(8,128)} %convolution_select_fusion.9), channel_id=1, source_target_pairs={{0,32},{1,33},{2,34},{3,35},{4,36},{5,37},{6,38},{7,39},{8,40},{9,... | collective-permute-start | bytes 3145736 | tf_op jit(solution)/shard_map/ppermute | solution.py:35
  220.4 13.0 %collective-permute-start.9 = (f32[4,512]{1,0:T(4,128)S(1)}, f32[4,512]{1,0:T(4,128)S(1)}, u32[]{:S(2)}, u32[]{:S(2)}) collective-permute-start(f32[4,512]{1,0:T(4,128)S(1)} %fusion.44), channel_id=1, source_target_pairs={{0,4},{1,5},{2,6},{3,7},{4,8},{5,9},{6,10},{7,11},{8,12},{9,13},{1... | collective-permute-start | bytes 24584 | tf_op jit(solution)/shard_map/ppermute | solution.py:35
  235.6 25.2 %collective-permute-start.10 = (f32[4,512]{1,0:T(4,128)S(1)}, f32[4,512]{1,0:T(4,128)S(1)}, u32[]{:S(2)}, u32[]{:S(2)}) collective-permute-start(f32[4,512]{1,0:T(4,128)S(1)} %fusion.43), channel_id=1, source_target_pairs={{0,8},{1,9},{2,10},{3,11},{4,12},{5,13},{6,14},{7,15},{8,16},{9,17... | collective-permute-start | bytes 24584 | tf_op jit(solution)/shard_map/ppermute | solution.py:35
  242.4 59.8 %collective-permute-start.24 = (f32[512,512]{1,0:T(8,128)}, f32[512,512]{1,0:T(8,128)}, u32[]{:S(2)}, u32[]{:S(2)}) collective-permute-start(f32[512,512]{1,0:T(8,128)} %convolution_select_fusion.4), channel_id=1, source_target_pairs={{8,0},{9,1},{10,2},{11,3},{12,4},{13,5},{14,6},{15,7},{16,8},{17,9... | collective-permute-start | bytes 3145736 | tf_op jit(solution)/shard_map/ppermute | solution.py:35
  262.9 24.6 %copy-start.5 = (f32[512,512]{1,0:T(8,128)S(1)}, f32[512,512]{1,0:T(8,128)}, u32[]{:S(2)}) copy-start(f32[512,512]{1,0:T(8,128)} %copy-done.4) | copy-start | bytes 3145732
  263.0 24.6 %collective-permute-start.11 = (f32[4,512]{1,0:T(4,128)S(1)}, f32[4,512]{1,0:T(4,128)S(1)}, u32[]{:S(2)}, u32[]{:S(2)}) collective-permute-start(f32[4,512]{1,0:T(4,128)S(1)} %fusion.42), channel_id=1, source_target_pairs={{0,16},{1,17},{2,18},{3,19},{4,20},{5,21},{6,22},{7,23},{8,24},{9,... | collective-permute-start | bytes 24584 | tf_op jit(solution)/shard_map/ppermute | solution.py:35
  285.7 28.2 %collective-permute-start.6 = (f32[512,512]{1,0:T(8,128)}, f32[512,512]{1,0:T(8,128)}, u32[]{:S(2)}, u32[]{:S(2)}) collective-permute-start(f32[512,512]{1,0:T(8,128)} %convolution_select_fusion.8), channel_id=1, source_target_pairs={{0,64},{1,65},{2,66},{3,67},{4,68},{5,69},{6,70},{7,71},{8,72},{9,... | collective-permute-start | bytes 3145736 | tf_op jit(solution)/shard_map/ppermute | solution.py:35
  288.6 9.5 %collective-permute-start.12 = (f32[4,512]{1,0:T(4,128)S(1)}, f32[4,512]{1,0:T(4,128)S(1)}, u32[]{:S(2)}, u32[]{:S(2)}) collective-permute-start(f32[4,512]{1,0:T(4,128)S(1)} %fusion.41), channel_id=1, source_target_pairs={{0,32},{1,33},{2,34},{3,35},{4,36},{5,37},{6,38},{7,39},{8,40},{9,... | collective-permute-start | bytes 24584 | tf_op jit(solution)/shard_map/ppermute | solution.py:35
  300.2 11.5 %collective-permute-start.13 = (f32[4,512]{1,0:T(4,128)S(1)}, f32[4,512]{1,0:T(4,128)S(1)}, u32[]{:S(2)}, u32[]{:S(2)}) collective-permute-start(f32[4,512]{1,0:T(4,128)S(1)} %fusion.40), channel_id=1, source_target_pairs={{0,64},{1,65},{2,66},{3,67},{4,68},{5,69},{6,70},{7,71},{8,72},{9,... | collective-permute-start | bytes 24584 | tf_op jit(solution)/shard_map/ppermute | solution.py:35
  306.8 52.4 %collective-permute-start.26 = (f32[512,512]{1,0:T(8,128)}, f32[512,512]{1,0:T(8,128)}, u32[]{:S(2)}, u32[]{:S(2)}) collective-permute-start(f32[512,512]{1,0:T(8,128)} %convolution_select_fusion.3), channel_id=1, source_target_pairs={{16,0},{17,1},{18,2},{19,3},{20,4},{21,5},{22,6},{23,7},{24,8},{25... | collective-permute-start | bytes 3145736 | tf_op jit(solution)/shard_map/ppermute | solution.py:35
  313.9 4.7 copy-start.10
  317.6 1.0 copy-start.6
  319.6 2.7 collective-permute-start.14
  324.4 41.5 %collective-permute-start.15 = (f32[4,512]{1,0:T(4,128)S(1)}, f32[4,512]{1,0:T(4,128)S(1)}, u32[]{:S(2)}, u32[]{:S(2)}) collective-permute-start(f32[4,512]{1,0:T(4,128)S(1)} %fusion.38), channel_id=1, source_target_pairs={{0,1},{1,2},{2,3},{3,4},{4,5},{5,6},{6,7},{7,8},{8,9},{9,10},{10,1... | collective-permute-start | bytes 24584 | tf_op jit(solution)/shard_map/ppermute | solution.py:35
  364.0 73.5 %collective-permute-start.28 = (f32[512,512]{1,0:T(8,128)}, f32[512,512]{1,0:T(8,128)}, u32[]{:S(2)}, u32[]{:S(2)}) collective-permute-start(f32[512,512]{1,0:T(8,128)} %convolution_select_fusion.2), channel_id=1, source_target_pairs={{32,0},{33,1},{34,2},{35,3},{36,4},{37,5},{38,6},{39,7},{40,8},{41... | collective-permute-start | bytes 3145736 | tf_op jit(solution)/shard_map/ppermute | solution.py:35
  376.6 22.0 %collective-permute-start.16 = (f32[4,512]{1,0:T(4,128)S(1)}, f32[4,512]{1,0:T(4,128)S(1)}, u32[]{:S(2)}, u32[]{:S(2)}) collective-permute-start(f32[4,512]{1,0:T(4,128)S(1)} %fusion.26), channel_id=1, source_target_pairs={{1,0},{2,1},{3,2},{4,3},{5,4},{6,5},{7,6},{8,7},{9,8},{10,9},{11,1... | collective-permute-start | bytes 24584 | tf_op jit(solution)/shard_map/ppermute | solution.py:35
  399.6 33.6 %collective-permute-start.17 = (f32[4,512]{1,0:T(4,128)S(1)}, f32[4,512]{1,0:T(4,128)S(1)}, u32[]{:S(2)}, u32[]{:S(2)}) collective-permute-start(f32[4,512]{1,0:T(4,128)S(1)} %fusion.24), channel_id=1, source_target_pairs={{2,0},{3,1},{4,2},{5,3},{6,4},{7,5},{8,6},{9,7},{10,8},{11,9},{12,... | collective-permute-start | bytes 24584 | tf_op jit(solution)/shard_map/ppermute | solution.py:35
  434.1 9.2 %collective-permute-start.19 = (f32[4,512]{1,0:T(4,128)S(1)}, f32[4,512]{1,0:T(4,128)S(1)}, u32[]{:S(2)}, u32[]{:S(2)}) collective-permute-start(f32[4,512]{1,0:T(4,128)S(1)} %fusion.23), channel_id=1, source_target_pairs={{4,0},{5,1},{6,2},{7,3},{8,4},{9,5},{10,6},{11,7},{12,8},{13,9},{1... | collective-permute-start | bytes 24584 | tf_op jit(solution)/shard_map/ppermute | solution.py:35
  441.2 45.5 %collective-permute-start.30 = (f32[512,512]{1,0:T(8,128)S(1)}, f32[512,512]{1,0:T(8,128)S(1)}, u32[]{:S(2)}, u32[]{:S(2)}) collective-permute-start(f32[512,512]{1,0:T(8,128)S(1)} %convolution_select_fusion.1), channel_id=1, source_target_pairs={{64,0},{65,1},{66,2},{67,3},{68,4},{69,5},{70,6},{71,7},{72,8},{73... | collective-permute-start | bytes 3145736 | tf_op jit(solution)/shard_map/ppermute | solution.py:35
  445.6 7.8 %collective-permute-start.21 = (f32[4,512]{1,0:T(4,128)S(1)}, f32[4,512]{1,0:T(4,128)S(1)}, u32[]{:S(2)}, u32[]{:S(2)}) collective-permute-start(f32[4,512]{1,0:T(4,128)S(1)} %fusion.22), channel_id=1, source_target_pairs={{8,0},{9,1},{10,2},{11,3},{12,4},{13,5},{14,6},{15,7},{16,8},{17,9... | collective-permute-start | bytes 24584 | tf_op jit(solution)/shard_map/ppermute | solution.py:35
  455.5 8.7 %collective-permute-start.23 = (f32[4,512]{1,0:T(4,128)S(1)}, f32[4,512]{1,0:T(4,128)S(1)}, u32[]{:S(2)}, u32[]{:S(2)}) collective-permute-start(f32[4,512]{1,0:T(4,128)S(1)} %fusion.21), channel_id=1, source_target_pairs={{16,0},{17,1},{18,2},{19,3},{20,4},{21,5},{22,6},{23,7},{24,8},{25... | collective-permute-start | bytes 24584 | tf_op jit(solution)/shard_map/ppermute | solution.py:35
  466.4 10.4 %collective-permute-start.25 = (f32[4,512]{1,0:T(4,128)S(1)}, f32[4,512]{1,0:T(4,128)S(1)}, u32[]{:S(2)}, u32[]{:S(2)}) collective-permute-start(f32[4,512]{1,0:T(4,128)S(1)} %fusion.20), channel_id=1, source_target_pairs={{32,0},{33,1},{34,2},{35,3},{36,4},{37,5},{38,6},{39,7},{40,8},{41... | collective-permute-start | bytes 24584 | tf_op jit(solution)/shard_map/ppermute | solution.py:35
  478.9 5.5 %collective-permute-start.27 = (f32[4,512]{1,0:T(4,128)S(1)}, f32[4,512]{1,0:T(4,128)S(1)}, u32[]{:S(2)}, u32[]{:S(2)}) collective-permute-start(f32[4,512]{1,0:T(4,128)S(1)} %fusion.19), channel_id=1, source_target_pairs={{64,0},{65,1},{66,2},{67,3},{68,4},{69,5},{70,6},{71,7},{72,8},{73... | collective-permute-start | bytes 24584 | tf_op jit(solution)/shard_map/ppermute | solution.py:35
  485.4 7.1 %collective-permute-start.29 = (f32[4,512]{1,0:T(4,128)S(1)}, f32[4,512]{1,0:T(4,128)S(1)}, u32[]{:S(2)}, u32[]{:S(2)}) collective-permute-start(f32[4,512]{1,0:T(4,128)S(1)} %fusion.18), channel_id=1, source_target_pairs={{128,0},{129,1},{130,2},{131,3},{132,4},{133,5},{134,6},{135,7},{1... | collective-permute-start | bytes 24584 | tf_op jit(solution)/shard_map/ppermute | solution.py:35
  493.4 5.5 %collective-permute-start.31 = (f32[4,512]{1,0:T(4,128)S(1)}, f32[4,512]{1,0:T(4,128)S(1)}, u32[]{:S(2)}, u32[]{:S(2)}) collective-permute-start(f32[4,512]{1,0:T(4,128)S(1)} %fusion.17), channel_id=1, source_target_pairs={{1,0},{2,1},{3,2},{4,3},{5,4},{6,5},{7,6},{8,7},{9,8},{10,9},{11,1... | collective-permute-start | bytes 24584 | tf_op jit(solution)/shard_map/ppermute | solution.py:35
Sparse Core Ops, SparseCore 0:
  9.8 26.9 all-gather.1

commit v2 on v1

--- a/solution.py
+++ b/solution.py
@@ -35,6 +35,14 @@
     return lax.ppermute(block, AXES, route)
 
 
+def filter_apply(rows, power, left, right, offsets):
+    return transposed(rows, power) + transposed(product(rows, right), left) + offsets
+
+
+def smoother_apply(rows, power, left, right, offsets):
+    return product(rows, power) + transposed(product(rows, right), left) + offsets
+
+
 def per_device(dynamics, pattern, initial_mean, observed, obs_index, obs_noise):
     state_width = dynamics.shape[1]
     blocks = pattern.shape[0]
@@ -46,6 +54,7 @@
     segment = lax.axis_index(AXES)
     span = observed.shape[0] // members
     steps_total = span * segments
+    last = span - 1
 
     present = jnp.maximum(pattern, jnp.eye(blocks, dtype=jnp.int32))
     block_mask = jnp.repeat(jnp.repeat(present, block_span, 0), block_span, 1).astype(jnp.float32)
@@ -62,40 +71,79 @@
     global_step = segment * span + jnp.arange(span, dtype=jnp.int32)
     keeps = jnp.where(global_step == steps_total - 1, 0.0, 1.0).astype(jnp.float32)
     pushes = [(gains[j] * obs_here[j])[:, None] * hits[j][None, :] for j in range(span)]
+    column = jnp.arange(span, dtype=jnp.int32)[:, None]
 
-    filt_a = transition * scales[0][:, None]
+    chain = max(1, segments // 4)
+    powers = []
+    power = transition
+    length = 1
+    while length < span:
+        power = product(power, power)
+        length *= 2
+    powers.append(power)
+    while len(powers) < chain.bit_length():
+        power = product(power, power)
+        powers.append(power)
+
+    hit_columns = hits.T
+    moved = [hit_columns]
+    for _ in range(last):
+        moved.append(product(transition, moved[-1]))
+    filt_u = jnp.stack([-gains[j] * moved[last - j][:, j] for j in range(span)], axis=1)
+    reach = product(hits, transition)
+    for m in range(last - 1, -1, -1):
+        reach = jnp.where(column > m, product(reach * scales[m][None, :], transition), reach)
+    filt_v = reach.T
     filt_b = pushes[0]
     for j in range(1, span):
-        filt_a = product(transition, filt_a) * scales[j][:, None]
         filt_b = transposed(filt_b, transition) * scales[j][None, :] + pushes[j]
-    last = span - 1
-    smooth_q = keeps[last] * (transition.T * scales[last][:, None])
-    for j in range(last - 1, -1, -1):
-        smooth_q = keeps[j] * (leading(transition, smooth_q) * scales[j][:, None])
+    value = initial_mean
+    for j in range(span):
+        value = transposed(value, transition) * scales[j][None, :] + pushes[j]
 
-    levels = 0
-    while 2 ** (levels + 1) < segments:
-        levels += 1
-    stored_q = []
-    for level in range(levels):
+    moved = [hit_columns]
+    for _ in range(last):
+        moved.append(leading(transition, moved[-1]))
+    smooth_u = jnp.stack([-gains[j] * moved[j][:, j] for j in range(span)], axis=1)
+    reach = transposed(hits, transition)
+    for m in range(1, span):
+        reach = jnp.where(column < m, transposed(reach * scales[m][None, :], transition), reach)
+    smooth_v = reach.T
+
+    stored = []
+    level = 0
+    while 2**level < chain:
         distance = 2**level
-        arrived_a, arrived_b = shifted((filt_a, filt_b), distance, segments)
-        arrived_q = shifted(smooth_q, -distance, segments)
-        usable = segment >= distance
-        new_a = product(filt_a, arrived_a)
-        new_b = transposed(arrived_b, filt_a) + filt_b
-        filt_a = jnp.where(usable, new_a, filt_a)
-        filt_b = jnp.where(usable, new_b, filt_b)
-        stored_q.append(smooth_q)
-        smooth_q = jnp.where(segment + distance < segments, product(smooth_q, arrived_q), smooth_q)
-    stored_q.append(smooth_q)
+        power = powers[level]
+        arrived_u, arrived_v, arrived_b, arrived_value = shifted(
+            (filt_u, filt_v, filt_b, value), distance, segments
+        )
+        new_value = filter_apply(arrived_value, power, filt_u, filt_v, filt_b)
+        value = jnp.where((segment >= distance) & (segment < 2 * distance), new_value, value)
+        new_u = jnp.concatenate(
+            [product(power, arrived_u) + product(filt_u, leading(filt_v, arrived_u)), filt_u], axis=1
+        )
+        new_v = jnp.concatenate([arrived_v, leading(power, filt_v)], axis=1)
+        filt_b = transposed(arrived_b, power) + transposed(product(arrived_b, filt_v), filt_u) + filt_b
+        filt_u, filt_v = new_u, new_v
 
-    top = 2**levels
-    prefix = transposed(initial_mean, filt_a) + filt_b
-    if top < segments:
-        arrived = shifted(prefix, top, segments)
-        prefix = jnp.where(segment >= top, transposed(arrived, filt_a) + filt_b, prefix)
-    entry = jnp.where(segment == 0, initial_mean, shifted(prefix, 1, segments))
+        stored.append((smooth_u, smooth_v))
+        arrived_u, arrived_v = shifted((smooth_u, smooth_v), -distance, segments)
+        new_u = jnp.concatenate(
+            [leading(power, arrived_u) + product(smooth_u, leading(smooth_v, arrived_u)), smooth_u], axis=1
+        )
+        new_v = jnp.concatenate([arrived_v, product(power, smooth_v)], axis=1)
+        smooth_u, smooth_v = new_u, new_v
+        level += 1
+    stored.append((smooth_u, smooth_v))
+    power = powers[level]
+
+    hops = (segments + chain - 1) // chain - 1
+    for hop in range(1, hops + 1):
+        arrived_value = shifted(value, chain, segments)
+        new_value = filter_apply(arrived_value, power, filt_u, filt_v, filt_b)
+        value = jnp.where((segment >= hop * chain) & (segment < (hop + 1) * chain), new_value, value)
+    entry = jnp.where(segment == 0, initial_mean, shifted(value, 1, segments))
 
     filtered = []
     current = entry
@@ -111,17 +159,21 @@
     offsets = jnp.zeros((seq_total, state_width), jnp.float32)
     for j in range(last, -1, -1):
         offsets = keeps[j] * product(offsets, transition) * scales[j][None, :] + gaps[j]
-    for level in range(levels):
+    for level in range(len(stored) - 1):
         distance = 2**level
+        left, right = stored[level]
         arrived = shifted(offsets, -distance, segments)
         offsets = jnp.where(
-            segment + distance < segments, transposed(arrived, stored_q[level]) + offsets, offsets
+            segment + distance < segments,
+            smoother_apply(arrived, powers[level], left, right, offsets),
+            offsets,
         )
-    if top < segments:
-        arrived = shifted(offsets, -top, segments)
-        offsets = jnp.where(
-            segment + top < segments, transposed(arrived, stored_q[levels]) + offsets, offsets
-        )
+    left, right = stored[-1]
+    for hop in range(1, hops + 1):
+        arrived = shifted(offsets, -chain, segments)
+        new_offsets = smoother_apply(arrived, power, left, right, offsets)
+        band = segments - hop * chain
+        offsets = jnp.where((segment >= band - chain) & (segment < band), new_offsets, offsets)
     current = shifted(offsets, -1, segments)
 
     smoothed = [None] * span

time: 532 us -> 486 us (0.914)
  waiting for transfers between devices: 234 us -> 76.3 us
  matrix products: 111 us -> 171 us
  local copies, waits for them, and re-layouts: 6.3 us -> 36.6 us
  starting transfers between devices: 143 us -> 154 us
  other arithmetic: 3.34 us -> 12.1 us
    ppermute x32 -> x50, waiting for transfers between devices: 206 us -> 56.5 us  [shifted(): return lax.ppermute(block, AXES, route)]
    dot_general x25 -> x55, matrix products: 35.1 us -> 64.8 us  [transposed(): lax.dot_general(left, right, (((1,), (1,)), ((), ())), precision=lax.Prec...]
    concatenate x0 -> x12, local copies, waits for them, and re-layouts: none -> 24.6 us  [the longest x6 13.4 us: per_device(): jnp.concatenate([product(power, arrived_u) + product(filt_u, leading(filt...]
    dot_general x26 -> x81, matrix products: 66.1 us -> 82.3 us  [product(): jnp.dot(left, right, precision=lax.Precision.HIGHEST, preferred_element_t...]
    dot_general x3 -> x27, matrix products: 9.98 us -> 23.6 us  [leading(): lax.dot_general(left, right, (((0,), (0,)), ((), ())), precision=lax.Prec...]
    ppermute x32 -> x50, starting transfers between devices: 143 us -> 154 us  [shifted(): return lax.ppermute(block, AXES, route)]
    all_gather x1, waiting for transfers between devices: 27.4 us -> 19.1 us  [per_device(): lax.all_gather(dynamics, 'state', axis=0, tiled=True) * block_mask]
    concatenate x0 -> x10, other arithmetic: none -> 8.04 us  [the longest x5 4.45 us: per_device(): new_v = jnp.concatenate([arrived_v, product(power, smooth_v)], axis=1)]
  transfers between devices with their start and end apart: 33 -> 51, of which waited for: 20 -> 13; matrix products, arithmetic and copies ran while one was open for 19% -> 36% of each run, Pallas kernels for 0% -> 0%
where the time goes in v2:
time: 486 us; the launch traced here: 477 us
  matrix products  171 us (35%)
  starting transfers between devices  154 us (32%)
  waiting for transfers between devices  76.3 us (16%)
  local copies, waits for them, and re-layouts  36.6 us (8%)
  between operations  19.1 us (4%)
  other arithmetic  12.1 us (2%)
  blocking collectives  8.78 us (2%)
    ppermute x50, starting transfers between devices, shifted(): return lax.ppermute(block, AXES, route)  154 us
    dot_general x81, matrix products, product(): jnp.dot(left, right, precision=lax.Precision.HIGHEST, preferred_element_t...  82.3 us
    dot_general x55, matrix products, transposed(): lax.dot_general(left, right, (((1,), (1,)), ((), ())), precision=lax.Prec...  64.8 us
    ppermute x50, waiting for transfers between devices, shifted(): return lax.ppermute(block, AXES, route)  56.5 us
    dot_general x27, matrix products, leading(): lax.dot_general(left, right, (((0,), (0,)), ((), ())), precision=lax.Prec...  23.6 us
    all_gather x1, waiting for transfers between devices, per_device(): lax.all_gather(dynamics, 'state', axis=0, tiled=True) * block_mask  19.1 us
    concatenate x6, local copies, waits for them, and re-layouts, per_device(): jnp.concatenate([product(power, arrived_u) + product(filt_u, leading(filt...  13.4 us
    concatenate x6, local copies, waits for them, and re-layouts, per_device(): jnp.concatenate([leading(power, arrived_u) + product(smooth_u, leading(sm...  11.2 us
  transfers between devices with their start and end apart: 51, of which 13 were waited for; matrix products, arithmetic and copies ran while one was open for 36% of the time, Pallas kernels for 0%

profile of v2, /device:TPU:232, one launch (start us, length us, event | category | flops | bytes accessed | tf_op | source)
XLA Modules:
  0.0 477.3 jit_solution(12026779211801622284)
XLA Ops:
  10.7 2.7 multiply_reduce_fusion
  17.7 19.1 %all-gather.2.cloned.1.call-done = f32[512,512]{1,0:T(8,128)} async-done(((f32[128,512]{1,0:T(8,128)}), f32[512,512]{1,0:T(8,128)}) %all-gather.2.cloned.1.call-update) | async-done | bytes 1048592 | tf_op jit(solution)/shard_map/all_gather | solution.py:61
  52.2 12.7 %fusion.62 = f32[4,512]{1,0:T(4,128)S(1)} fusion(f32[4,512]{1,0:T(4,128)S(1)} %fusion.63, f32[512,512]{1,0:T(8,128)S(1)} %bitcast_multiply_fusion, f32[512]{0:T(512)S(1)} %bitcast.381, f32[4]{0:T(128)S(1)} %get-tuple-element.2, f32[512]{0:T(512)S(1)} %bitcast.367), kind=kOutput, calls=%fused_computation.113 | convolution fusion | flops 12589056 | bytes 1069072 | tf_op jit(solution)/shard_map/dot_general | solution.py:14
  64.9 2.2 collective-permute-start
  69.0 3.6 collective-permute-start.4
  77.0 2.8 collective-permute-start.2
  91.2 2.8 fusion.184
  97.9 5.8 %collective-permute-start.30 = (f32[512,4]{0,1:T(4,128)S(1)}, f32[512,4]{0,1:T(4,128)S(1)}, u32[]{:S(2)}, u32[]{:S(2)}) collective-permute-start(f32[512,4]{0,1:T(4,128)S(1)} %bitcast.359), channel_id=1, source_target_pairs={{1,0},{2,1},{3,2},{4,3},{5,4},{6,5},{7,6},{8,7},{9,8},{10,9},{11,1... | collective-permute-start | bytes 24584 | tf_op jit(solution)/shard_map/ppermute | solution.py:35
  103.7 2.5 collective-permute-start.31
  107.7 2.3 collective-permute-start.1
  112.5 2.6 collective-permute-start.8
  115.1 4.6 collective-permute-start.6
  119.7 7.6 %collective-permute-start.7 = (f32[512,8]{0,1:T(8,128)S(1)}, f32[512,8]{0,1:T(8,128)S(1)}, u32[]{:S(2)}, u32[]{:S(2)}) collective-permute-start(f32[512,8]{0,1:T(8,128)S(1)} %concatenate.85), channel_id=1, source_target_pairs={{0,2},{1,3},{2,4},{3,5},{4,6},{5,7},{6,8},{7,9},{8,10},{9,11},{10,... | collective-permute-start | bytes 49160 | tf_op jit(solution)/shard_map/ppermute | solution.py:35
  136.0 2.2 fusion.61
  138.2 5.5 %collective-permute-start.5 = (f32[4,512]{1,0:T(4,128)S(1)}, f32[4,512]{1,0:T(4,128)S(1)}, u32[]{:S(2)}, u32[]{:S(2)}) collective-permute-start(f32[4,512]{1,0:T(4,128)S(1)} %fusion.61), channel_id=1, source_target_pairs={{0,4},{1,5},{2,6},{3,7},{4,8},{5,9},{6,10},{7,11},{8,12},{9,13},{1... | collective-permute-start | bytes 24584 | tf_op jit(solution)/shard_map/ppermute | solution.py:35
  150.7 2.2 fusion.58
  152.9 3.2 collective-permute-start.9
  159.8 3.5 collective-permute-start.16
  164.2 3.2 collective-permute-start.36
  173.3 2.2 convolution_add_fusion.7
  176.2 8.3 %collective-permute-start.15 = (f32[512,32]{0,1:T(8,128)S(1)}, f32[512,32]{0,1:T(8,128)}, u32[]{:S(2)}, u32[]{:S(2)}) collective-permute-start(f32[512,32]{0,1:T(8,128)S(1)} %concatenate.89), channel_id=1, source_target_pairs={{0,8},{1,9},{2,10},{3,11},{4,12},{5,13},{6,14},{7,15},{8,16},{9,17... | collective-permute-start | bytes 196616 | tf_op jit(solution)/shard_map/ppermute | solution.py:35
  186.6 2.8 fusion.55
  194.2 2.3 fusion.50
  196.4 3.3 collective-permute-start.20
  202.3 3.9 collective-permute-start.39
  215.3 2.3 convolution_add_fusion.5
  219.1 5.4 %collective-permute-start.19 = (f32[512,64]{0,1:T(8,128)S(1)}, f32[512,64]{0,1:T(8,128)S(1)}, u32[]{:S(2)}, u32[]{:S(2)}) collective-permute-start(f32[512,64]{0,1:T(8,128)S(1)} %concatenate.91), channel_id=1, source_target_pairs={{0,16},{1,17},{2,18},{3,19},{4,20},{5,21},{6,22},{7,23},{8,24},{9,... | collective-permute-start | bytes 393224 | tf_op jit(solution)/shard_map/ppermute | solution.py:35
  226.7 2.3 fusion.52
  229.1 6.9 %collective-permute-start.17 = (f32[4,512]{1,0:T(4,128)}, f32[4,512]{1,0:T(4,128)}, u32[]{:S(2)}, u32[]{:S(2)}) collective-permute-start(f32[4,512]{1,0:T(4,128)} %fusion.52), channel_id=1, source_target_pairs={{0,32},{1,33},{2,34},{3,35},{4,36},{5,37},{6,38},{7,39},{8,40},{9,... | collective-permute-start | bytes 24584 | tf_op jit(solution)/shard_map/ppermute | solution.py:35
  238.7 2.3 fusion.47
  241.0 2.4 collective-permute-start.24
  244.7 2.2 convolution_add_fusion.4
  250.1 4.0 concatenate.93
  259.0 2.3 fusion.49
  264.9 2.1 collective-permute-start.22
  267.0 2.3 fusion.44
  269.3 2.3 fusion.149
  271.7 6.7 %collective-permute-done.23 = f32[512,128]{0,1:T(8,128)S(1)} collective-permute-done((f32[512,128]{0,1:T(8,128)S(1)}, f32[512,128]{0,1:T(8,128)S(1)}, u32[]{:S(2)}, u32[]{:S(2)}) %collective-permute-start.23) | collective-permute-done | bytes 262176 | tf_op jit(solution)/shard_map/ppermute | solution.py:35
  282.0 7.9 %concatenate.95 = f32[512,256]{0,1:T(8,128)} concatenate(f32[512,128]{0,1:T(8,128)} %convolution_add_fusion.1, f32[512,64]{0,1:T(8,128)S(1)} %copy-done.26, f32[512,32]{0,1:T(8,128)} %copy-done.31, f32[512,16]{0,1:T(8,128)} %copy-done.38, f32[512,8]{0,1:T(8,128)} %copy-done.44, f32[512,4]{0,1:T(4,128)} %copy-done.54, f32[512,1]{0,1:T(1,128)} %copy-done.69, f32[512,1]{0,1:T(1,128)} %copy-done.84, ...), dimensions={1} | concatenate | bytes 1048576 | tf_op jit(solution)/shard_map/concatenate | solution.py:123
  292.9 2.3 fusion.46
  298.9 3.1 concatenate.103
  304.1 2.7 collective-permute-start.43
  315.4 5.5 %collective-permute-done.26 = f32[4,512]{1,0:T(4,128)S(1)} collective-permute-done((f32[4,512]{1,0:T(4,128)S(1)}, f32[4,512]{1,0:T(4,128)S(1)}, u32[]{:S(2)}, u32[]{:S(2)}) %collective-permute-start.26) | collective-permute-done | bytes 8224 | tf_op jit(solution)/shard_map/ppermute | solution.py:35
  324.1 3.8 collective-permute-start.27
  329.1 2.1 collective-permute-done.27
  343.2 2.4 collective-permute-start.28
  352.7 4.3 collective-permute-done.29
  362.2 3.8 concatenate.105
  366.1 5.7 %collective-permute-start.45 = (f32[512,128]{0,1:T(8,128)}, f32[512,128]{0,1:T(8,128)}, u32[]{:S(2)}, u32[]{:S(2)}) collective-permute-start(f32[512,128]{0,1:T(8,128)} %pad_maximum_fusion.9), channel_id=1, source_target_pairs={{32,0},{33,1},{34,2},{35,3},{36,4},{37,5},{38,6},{39,7},{40,8},{41... | collective-permute-start | bytes 786440 | tf_op jit(solution)/shard_map/ppermute | solution.py:35
  371.7 3.9 collective-permute-start.46
  379.4 4.1 collective-permute-start.35
  383.4 2.1 fusion.145
  385.6 13.2 %collective-permute-done.35 = f32[4,512]{1,0:T(4,128)S(1)} collective-permute-done((f32[4,512]{1,0:T(4,128)S(1)}, f32[4,512]{1,0:T(4,128)S(1)}, u32[]{:S(2)}, u32[]{:S(2)}) %collective-permute-start.35) | collective-permute-done | bytes 8224 | tf_op jit(solution)/shard_map/ppermute | solution.py:35
  399.7 2.2 collective-permute-start.38
  403.2 5.2 %collective-permute-done.38 = f32[4,512]{1,0:T(4,128)S(1)} collective-permute-done((f32[4,512]{1,0:T(4,128)S(1)}, f32[4,512]{1,0:T(4,128)S(1)}, u32[]{:S(2)}, u32[]{:S(2)}) %collective-permute-start.38) | collective-permute-done | bytes 8224 | tf_op jit(solution)/shard_map/ppermute | solution.py:35
  411.2 2.4 collective-permute-start.41
  414.9 6.6 %collective-permute-done.41 = f32[4,512]{1,0:T(4,128)S(1)} collective-permute-done((f32[4,512]{1,0:T(4,128)S(1)}, f32[4,512]{1,0:T(4,128)S(1)}, u32[]{:S(2)}, u32[]{:S(2)}) %collective-permute-start.41) | collective-permute-done | bytes 8224 | tf_op jit(solution)/shard_map/ppermute | solution.py:35
  424.6 2.4 collective-permute-start.44
  432.7 2.3 collective-permute-start.47
  435.0 3.3 collective-permute-done.47
  440.7 2.3 collective-permute-start.48
  443.0 3.3 collective-permute-done.48
  450.8 3.6 collective-permute-done.49
  460.1 8.8 %all_to_all.15 = f32[2,4,4,512]{3,1,0,2:T(4,128)S(1)} all-to-all(f32[2,4,4,512]{3,1,0,2:T(4,128)S(1)} %copy.10), channel_id=1, replica_groups=mesh['tm'=64,'state'=4] {'state'}, dimensions={2} | all-to-all | bytes 131072 | tf_op jit(solution)/shard_map/all_to_all | solution.py:186
  (512 shorter events, 191.7 us)
Async XLA Ops:
  7.2 29.6 %all-gather.2.cloned.1.call-start = ((), (), s32[]{:S(2)}) async-start(), calls=%async_computation.1 | async-start | bytes 1310720 | tf_op jit(solution)/shard_map/all_gather | solution.py:61
  17.0 152.7 %copy-start.72 = (f32[512,1]{0,1:T(1,128)}, f32[512,1]{0,1:T(1,128)S(1)}, u32[]{:S(2)}) copy-start(f32[512,1]{0,1:T(1,128)S(1)} %get-tuple-element.10) | copy-start | bytes 6148
  17.1 158.5 %copy-start.82 = (f32[512,1]{0,1:T(1,128)}, f32[512,1]{0,1:T(1,128)S(1)}, u32[]{:S(2)}) copy-start(f32[512,1]{0,1:T(1,128)S(1)} %get-tuple-element.11) | copy-start | bytes 6148
  17.7 77.3 %copy-start.62 = (f32[1,512]{1,0:T(1,128)}, f32[1,512]{1,0:T(1,128)S(1)}, u32[]{:S(2)}) copy-start(f32[1,512]{1,0:T(1,128)S(1)} %get-tuple-element.13) | copy-start | bytes 6148
  17.7 78.2 %copy-start.88 = (f32[1,512]{1,0:T(1,128)}, f32[1,512]{1,0:T(1,128)S(1)}, u32[]{:S(2)}) copy-start(f32[1,512]{1,0:T(1,128)S(1)} %get-tuple-element.12) | copy-start | bytes 6148
  44.2 131.3 %copy-start.69 = (f32[512,1]{0,1:T(1,128)}, f32[512,1]{0,1:T(1,128)S(1)}, u32[]{:S(2)}) copy-start(f32[512,1]{0,1:T(1,128)S(1)} %convolution_multiply_fusion.20) | copy-start | bytes 6148
  45.6 124.2 %copy-start.65 = (f32[512,1]{0,1:T(1,128)}, f32[512,1]{0,1:T(1,128)S(1)}, u32[]{:S(2)}) copy-start(f32[512,1]{0,1:T(1,128)S(1)} %convolution_multiply_fusion.19) | copy-start | bytes 6148
  45.6 130.0 %copy-start.83 = (f32[512,1]{0,1:T(1,128)}, f32[512,1]{0,1:T(1,128)S(1)}, u32[]{:S(2)}) copy-start(f32[512,1]{0,1:T(1,128)S(1)} %get-tuple-element.28) | copy-start | bytes 6148
  45.6 130.0 %copy-start.84 = (f32[512,1]{0,1:T(1,128)}, f32[512,1]{0,1:T(1,128)S(1)}, u32[]{:S(2)}) copy-start(f32[512,1]{0,1:T(1,128)S(1)} %get-tuple-element.29) | copy-start | bytes 6148
  45.6 124.1 %copy-start.76 = (f32[512,1]{0,1:T(1,128)}, f32[512,1]{0,1:T(1,128)S(1)}, u32[]{:S(2)}) copy-start(f32[512,1]{0,1:T(1,128)S(1)} %get-tuple-element.30) | copy-start | bytes 6148
  45.6 124.1 %copy-start.79 = (f32[512,1]{0,1:T(1,128)}, f32[512,1]{0,1:T(1,128)S(1)}, u32[]{:S(2)}) copy-start(f32[512,1]{0,1:T(1,128)S(1)} %get-tuple-element.31) | copy-start | bytes 6148
  64.9 38.8 %collective-permute-start = (f32[4,512]{1,0:T(4,128)S(1)}, f32[4,512]{1,0:T(4,128)S(1)}, u32[]{:S(2)}, u32[]{:S(2)}) collective-permute-start(f32[4,512]{1,0:T(4,128)S(1)} %fusion.67), channel_id=1, source_target_pairs={{0,1},{1,2},{2,3},{3,4},{4,5},{5,6},{6,7},{7,8},{8,9},{9,10},{10,1... | collective-permute-start | bytes 24584 | tf_op jit(solution)/shard_map/ppermute | solution.py:35
  69.0 37.5 %collective-permute-start.4 = (f32[4,512]{1,0:T(4,128)S(1)}, f32[4,512]{1,0:T(4,128)S(1)}, u32[]{:S(2)}, u32[]{:S(2)}) collective-permute-start(f32[4,512]{1,0:T(4,128)S(1)} %fusion.62), channel_id=1, source_target_pairs={{0,1},{1,2},{2,3},{3,4},{4,5},{5,6},{6,7},{7,8},{8,9},{9,10},{10,1... | collective-permute-start | bytes 24584 | tf_op jit(solution)/shard_map/ppermute | solution.py:35
  77.0 38.0 %collective-permute-start.2 = (f32[512,4]{0,1:T(4,128)S(1)}, f32[512,4]{0,1:T(4,128)S(1)}, u32[]{:S(2)}, u32[]{:S(2)}) collective-permute-start(f32[512,4]{0,1:T(4,128)S(1)} %bitcast.344), channel_id=1, source_target_pairs={{0,1},{1,2},{2,3},{3,4},{4,5},{5,6},{6,7},{7,8},{8,9},{9,10},{10,1... | collective-permute-start | bytes 24584 | tf_op jit(solution)/shard_map/ppermute | solution.py:35
  79.8 30.2 %collective-permute-start.3 = (f32[512,4]{0,1:T(4,128)S(1)}, f32[512,4]{0,1:T(4,128)S(1)}, u32[]{:S(2)}, u32[]{:S(2)}) collective-permute-start(f32[512,4]{0,1:T(4,128)S(1)} %pad_maximum_fusion.20), channel_id=1, source_target_pairs={{0,1},{1,2},{2,3},{3,4},{4,5},{5,6},{6,7},{7,8},{8,9},{9,10},{10,1... | collective-permute-start | bytes 24584 | tf_op jit(solution)/shard_map/ppermute | solution.py:35
  97.9 65.3 %copy-start.58 = (f32[512,4]{0,1:T(4,128)}, f32[512,4]{0,1:T(4,128)S(1)}, u32[]{:S(2)}) copy-start(f32[512,4]{0,1:T(4,128)S(1)} %fusion.195) | copy-start | bytes 24580
  97.9 29.7 %collective-permute-start.30 = (f32[512,4]{0,1:T(4,128)S(1)}, f32[512,4]{0,1:T(4,128)S(1)}, u32[]{:S(2)}, u32[]{:S(2)}) collective-permute-start(f32[512,4]{0,1:T(4,128)S(1)} %bitcast.359), channel_id=1, source_target_pairs={{1,0},{2,1},{3,2},{4,3},{5,4},{6,5},{7,6},{8,7},{9,8},{10,9},{11,1... | collective-permute-start | bytes 24584 | tf_op jit(solution)/shard_map/ppermute | solution.py:35
  103.7 16.0 %collective-permute-start.31 = (f32[512,4]{0,1:T(4,128)S(1)}, f32[512,4]{0,1:T(4,128)S(1)}, u32[]{:S(2)}, u32[]{:S(2)}) collective-permute-start(f32[512,4]{0,1:T(4,128)S(1)} %pad_maximum_fusion.21), channel_id=1, source_target_pairs={{1,0},{2,1},{3,2},{4,3},{5,4},{6,5},{7,6},{8,7},{9,8},{10,9},{11,1... | collective-permute-start | bytes 24584 | tf_op jit(solution)/shard_map/ppermute | solution.py:35
  107.7 25.6 %collective-permute-start.1 = (f32[4,512]{1,0:T(4,128)S(1)}, f32[4,512]{1,0:T(4,128)S(1)}, u32[]{:S(2)}, u32[]{:S(2)}) collective-permute-start(f32[4,512]{1,0:T(4,128)S(1)} %fusion.66), channel_id=1, source_target_pairs={{0,2},{1,3},{2,4},{3,5},{4,6},{5,7},{6,8},{7,9},{8,10},{9,11},{10,... | collective-permute-start | bytes 24584 | tf_op jit(solution)/shard_map/ppermute | solution.py:35
  112.5 23.2 %collective-permute-start.8 = (f32[4,512]{1,0:T(4,128)S(1)}, f32[4,512]{1,0:T(4,128)S(1)}, u32[]{:S(2)}, u32[]{:S(2)}) collective-permute-start(f32[4,512]{1,0:T(4,128)S(1)} %fusion.59), channel_id=1, source_target_pairs={{0,2},{1,3},{2,4},{3,5},{4,6},{5,7},{6,8},{7,9},{8,10},{9,11},{10,... | collective-permute-start | bytes 24584 | tf_op jit(solution)/shard_map/ppermute | solution.py:35
  115.1 35.1 %collective-permute-start.6 = (f32[512,8]{0,1:T(8,128)S(1)}, f32[512,8]{0,1:T(8,128)S(1)}, u32[]{:S(2)}, u32[]{:S(2)}) collective-permute-start(f32[512,8]{0,1:T(8,128)S(1)} %pad_maximum_fusion.18), channel_id=1, source_target_pairs={{0,2},{1,3},{2,4},{3,5},{4,6},{5,7},{6,8},{7,9},{8,10},{9,11},{10,... | collective-permute-start | bytes 49160 | tf_op jit(solution)/shard_map/ppermute | solution.py:35
  119.7 25.0 %collective-permute-start.7 = (f32[512,8]{0,1:T(8,128)S(1)}, f32[512,8]{0,1:T(8,128)S(1)}, u32[]{:S(2)}, u32[]{:S(2)}) collective-permute-start(f32[512,8]{0,1:T(8,128)S(1)} %concatenate.85), channel_id=1, source_target_pairs={{0,2},{1,3},{2,4},{3,5},{4,6},{5,7},{6,8},{7,9},{8,10},{9,11},{10,... | collective-permute-start | bytes 49160 | tf_op jit(solution)/shard_map/ppermute | solution.py:35
  127.7 35.9 %collective-permute-start.33 = (f32[512,8]{0,1:T(8,128)S(1)}, f32[512,8]{0,1:T(8,128)S(1)}, u32[]{:S(2)}, u32[]{:S(2)}) collective-permute-start(f32[512,8]{0,1:T(8,128)S(1)} %pad_maximum_fusion.19), channel_id=1, source_target_pairs={{2,0},{3,1},{4,2},{5,3},{6,4},{7,5},{8,6},{9,7},{10,8},{11,9},{12,... | collective-permute-start | bytes 49160 | tf_op jit(solution)/shard_map/ppermute | solution.py:35
  133.2 66.5 %copy-start.52 = (f32[512,8]{0,1:T(8,128)}, f32[512,8]{0,1:T(8,128)S(1)}, u32[]{:S(2)}) copy-start(f32[512,8]{0,1:T(8,128)S(1)} %fusion.116) | copy-start | bytes 49156
  133.3 26.4 %collective-permute-start.34 = (f32[512,8]{0,1:T(8,128)S(1)}, f32[512,8]{0,1:T(8,128)S(1)}, u32[]{:S(2)}, u32[]{:S(2)}) collective-permute-start(f32[512,8]{0,1:T(8,128)S(1)} %concatenate.97), channel_id=1, source_target_pairs={{2,0},{3,1},{4,2},{5,3},{6,4},{7,5},{8,6},{9,7},{10,8},{11,9},{12,... | collective-permute-start | bytes 49160 | tf_op jit(solution)/shard_map/ppermute | solution.py:35
  138.2 9.9 %collective-permute-start.5 = (f32[4,512]{1,0:T(4,128)S(1)}, f32[4,512]{1,0:T(4,128)S(1)}, u32[]{:S(2)}, u32[]{:S(2)}) collective-permute-start(f32[4,512]{1,0:T(4,128)S(1)} %fusion.61), channel_id=1, source_target_pairs={{0,4},{1,5},{2,6},{3,7},{4,8},{5,9},{6,10},{7,11},{8,12},{9,13},{1... | collective-permute-start | bytes 24584 | tf_op jit(solution)/shard_map/ppermute | solution.py:35
  144.7 5.7 %collective-permute-start.12 = (f32[4,512]{1,0:T(4,128)S(1)}, f32[4,512]{1,0:T(4,128)S(1)}, u32[]{:S(2)}, u32[]{:S(2)}) collective-permute-start(f32[4,512]{1,0:T(4,128)S(1)} %fusion.56), channel_id=1, source_target_pairs={{0,4},{1,5},{2,6},{3,7},{4,8},{5,9},{6,10},{7,11},{8,12},{9,13},{1... | collective-permute-start | bytes 24584 | tf_op jit(solution)/shard_map/ppermute | solution.py:35
  148.0 23.0 %collective-permute-start.11 = (f32[512,16]{0,1:T(8,128)S(1)}, f32[512,16]{0,1:T(8,128)S(1)}, u32[]{:S(2)}, u32[]{:S(2)}) collective-permute-start(f32[512,16]{0,1:T(8,128)S(1)} %concatenate.87), channel_id=1, source_target_pairs={{0,4},{1,5},{2,6},{3,7},{4,8},{5,9},{6,10},{7,11},{8,12},{9,13},{1... | collective-permute-start | bytes 98312 | tf_op jit(solution)/shard_map/ppermute | solution.py:35
  152.9 23.4 %collective-permute-start.9 = (f32[4,512]{1,0:T(4,128)S(1)}, f32[4,512]{1,0:T(4,128)}, u32[]{:S(2)}, u32[]{:S(2)}) collective-permute-start(f32[4,512]{1,0:T(4,128)S(1)} %fusion.58), channel_id=1, source_target_pairs={{0,8},{1,9},{2,10},{3,11},{4,12},{5,13},{6,14},{7,15},{8,16},{9,17... | collective-permute-start | bytes 24584 | tf_op jit(solution)/shard_map/ppermute | solution.py:35
  156.7 27.8 %collective-permute-start.10 = (f32[512,16]{0,1:T(8,128)}, f32[512,16]{0,1:T(8,128)S(1)}, u32[]{:S(2)}, u32[]{:S(2)}) collective-permute-start(f32[512,16]{0,1:T(8,128)} %pad_maximum_fusion.15), channel_id=1, source_target_pairs={{0,4},{1,5},{2,6},{3,7},{4,8},{5,9},{6,10},{7,11},{8,12},{9,13},{1... | collective-permute-start | bytes 98312 | tf_op jit(solution)/shard_map/ppermute | solution.py:35
  159.8 25.8 %collective-permute-start.16 = (f32[4,512]{1,0:T(4,128)S(1)}, f32[4,512]{1,0:T(4,128)}, u32[]{:S(2)}, u32[]{:S(2)}) collective-permute-start(f32[4,512]{1,0:T(4,128)S(1)} %fusion.53), channel_id=1, source_target_pairs={{0,8},{1,9},{2,10},{3,11},{4,12},{5,13},{6,14},{7,15},{8,16},{9,17... | collective-permute-start | bytes 24584 | tf_op jit(solution)/shard_map/ppermute | solution.py:35
  164.2 37.4 %collective-permute-start.36 = (f32[512,16]{0,1:T(8,128)}, f32[512,16]{0,1:T(8,128)S(1)}, u32[]{:S(2)}, u32[]{:S(2)}) collective-permute-start(f32[512,16]{0,1:T(8,128)} %pad_maximum_fusion.17), channel_id=1, source_target_pairs={{4,0},{5,1},{6,2},{7,3},{8,4},{9,5},{10,6},{11,7},{12,8},{13,9},{1... | collective-permute-start | bytes 98312 | tf_op jit(solution)/shard_map/ppermute | solution.py:35
  169.8 73.6 %copy-start.32 = (f32[512,16]{0,1:T(8,128)}, f32[512,16]{0,1:T(8,128)S(1)}, u32[]{:S(2)}) copy-start(f32[512,16]{0,1:T(8,128)S(1)} %fusion.123) | copy-start | bytes 98308
  171.0 25.4 %collective-permute-start.37 = (f32[512,16]{0,1:T(8,128)}, f32[512,16]{0,1:T(8,128)}, u32[]{:S(2)}, u32[]{:S(2)}) collective-permute-start(f32[512,16]{0,1:T(8,128)} %concatenate.99), channel_id=1, source_target_pairs={{4,0},{5,1},{6,2},{7,3},{8,4},{9,5},{10,6},{11,7},{12,8},{13,9},{1... | collective-permute-start | bytes 98312 | tf_op jit(solution)/shard_map/ppermute | solution.py:35
  176.2 35.7 %collective-permute-start.15 = (f32[512,32]{0,1:T(8,128)S(1)}, f32[512,32]{0,1:T(8,128)}, u32[]{:S(2)}, u32[]{:S(2)}) collective-permute-start(f32[512,32]{0,1:T(8,128)S(1)} %concatenate.89), channel_id=1, source_target_pairs={{0,8},{1,9},{2,10},{3,11},{4,12},{5,13},{6,14},{7,15},{8,16},{9,17... | collective-permute-start | bytes 196616 | tf_op jit(solution)/shard_map/ppermute | solution.py:35
  189.4 29.7 %collective-permute-start.13 = (f32[4,512]{1,0:T(4,128)}, f32[4,512]{1,0:T(4,128)}, u32[]{:S(2)}, u32[]{:S(2)}) collective-permute-start(f32[4,512]{1,0:T(4,128)} %fusion.55), channel_id=1, source_target_pairs={{0,16},{1,17},{2,18},{3,19},{4,20},{5,21},{6,22},{7,23},{8,24},{9,... | collective-permute-start | bytes 24584 | tf_op jit(solution)/shard_map/ppermute | solution.py:35
  192.1 32.4 %collective-permute-start.14 = (f32[512,32]{0,1:T(8,128)}, f32[512,32]{0,1:T(8,128)S(1)}, u32[]{:S(2)}, u32[]{:S(2)}) collective-permute-start(f32[512,32]{0,1:T(8,128)} %pad_maximum_fusion.12), channel_id=1, source_target_pairs={{0,8},{1,9},{2,10},{3,11},{4,12},{5,13},{6,14},{7,15},{8,16},{9,17... | collective-permute-start | bytes 196616 | tf_op jit(solution)/shard_map/ppermute | solution.py:35
  196.4 29.2 %collective-permute-start.20 = (f32[4,512]{1,0:T(4,128)}, f32[4,512]{1,0:T(4,128)}, u32[]{:S(2)}, u32[]{:S(2)}) collective-permute-start(f32[4,512]{1,0:T(4,128)} %fusion.50), channel_id=1, source_target_pairs={{0,16},{1,17},{2,18},{3,19},{4,20},{5,21},{6,22},{7,23},{8,24},{9,... | collective-permute-start | bytes 24584 | tf_op jit(solution)/shard_map/ppermute | solution.py:35
  202.3 95.1 %collective-permute-start.39 = (f32[512,32]{0,1:T(8,128)}, f32[512,32]{0,1:T(8,128)}, u32[]{:S(2)}, u32[]{:S(2)}) collective-permute-start(f32[512,32]{0,1:T(8,128)} %pad_maximum_fusion.13), channel_id=1, source_target_pairs={{8,0},{9,1},{10,2},{11,3},{12,4},{13,5},{14,6},{15,7},{16,8},{17,9... | collective-permute-start | bytes 196616 | tf_op jit(solution)/shard_map/ppermute | solution.py:35
  212.0 29.0 %collective-permute-start.40 = (f32[512,32]{0,1:T(8,128)}, f32[512,32]{0,1:T(8,128)}, u32[]{:S(2)}, u32[]{:S(2)}) collective-permute-start(f32[512,32]{0,1:T(8,128)} %concatenate.101), channel_id=1, source_target_pairs={{8,0},{9,1},{10,2},{11,3},{12,4},{13,5},{14,6},{15,7},{16,8},{17,9... | collective-permute-start | bytes 196616 | tf_op jit(solution)/shard_map/ppermute | solution.py:35
  219.1 28.5 %collective-permute-start.19 = (f32[512,64]{0,1:T(8,128)S(1)}, f32[512,64]{0,1:T(8,128)S(1)}, u32[]{:S(2)}, u32[]{:S(2)}) collective-permute-start(f32[512,64]{0,1:T(8,128)S(1)} %concatenate.91), channel_id=1, source_target_pairs={{0,16},{1,17},{2,18},{3,19},{4,20},{5,21},{6,22},{7,23},{8,24},{9,... | collective-permute-start | bytes 393224 | tf_op jit(solution)/shard_map/ppermute | solution.py:35
  229.1 27.0 %collective-permute-start.17 = (f32[4,512]{1,0:T(4,128)}, f32[4,512]{1,0:T(4,128)}, u32[]{:S(2)}, u32[]{:S(2)}) collective-permute-start(f32[4,512]{1,0:T(4,128)} %fusion.52), channel_id=1, source_target_pairs={{0,32},{1,33},{2,34},{3,35},{4,36},{5,37},{6,38},{7,39},{8,40},{9,... | collective-permute-start | bytes 24584 | tf_op jit(solution)/shard_map/ppermute | solution.py:35
  236.6 19.4 %collective-permute-start.18 = (f32[512,64]{0,1:T(8,128)}, f32[512,64]{0,1:T(8,128)}, u32[]{:S(2)}, u32[]{:S(2)}) collective-permute-start(f32[512,64]{0,1:T(8,128)} %pad_maximum_fusion.10), channel_id=1, source_target_pairs={{0,16},{1,17},{2,18},{3,19},{4,20},{5,21},{6,22},{7,23},{8,24},{9,... | collective-permute-start | bytes 393224 | tf_op jit(solution)/shard_map/ppermute | solution.py:35
  241.0 16.6 %collective-permute-start.24 = (f32[4,512]{1,0:T(4,128)}, f32[4,512]{1,0:T(4,128)}, u32[]{:S(2)}, u32[]{:S(2)}) collective-permute-start(f32[4,512]{1,0:T(4,128)} %fusion.47), channel_id=1, source_target_pairs={{0,32},{1,33},{2,34},{3,35},{4,36},{5,37},{6,38},{7,39},{8,40},{9,... | collective-permute-start | bytes 24584 | tf_op jit(solution)/shard_map/ppermute | solution.py:35
  254.1 24.3 %collective-permute-start.23 = (f32[512,128]{0,1:T(8,128)S(1)}, f32[512,128]{0,1:T(8,128)S(1)}, u32[]{:S(2)}, u32[]{:S(2)}) collective-permute-start(f32[512,128]{0,1:T(8,128)S(1)} %concatenate.93), channel_id=1, source_target_pairs={{0,32},{1,33},{2,34},{3,35},{4,36},{5,37},{6,38},{7,39},{8,40},{9,... | collective-permute-start | bytes 786440 | tf_op jit(solution)/shard_map/ppermute | solution.py:35
  261.3 28.6 %collective-permute-start.21 = (f32[4,512]{1,0:T(4,128)}, f32[4,512]{1,0:T(4,128)}, u32[]{:S(2)}, u32[]{:S(2)}) collective-permute-start(f32[4,512]{1,0:T(4,128)} %fusion.49), channel_id=1, source_target_pairs={{0,64},{1,65},{2,66},{3,67},{4,68},{5,69},{6,70},{7,71},{8,72},{9,... | collective-permute-start | bytes 24584 | tf_op jit(solution)/shard_map/ppermute | solution.py:35
  264.9 25.0 %collective-permute-start.22 = (f32[512,128]{0,1:T(8,128)}, f32[512,128]{0,1:T(8,128)}, u32[]{:S(2)}, u32[]{:S(2)}) collective-permute-start(f32[512,128]{0,1:T(8,128)} %pad_maximum_fusion.8), channel_id=1, source_target_pairs={{0,32},{1,33},{2,34},{3,35},{4,36},{5,37},{6,38},{7,39},{8,40},{9,... | collective-permute-start | bytes 786440 | tf_op jit(solution)/shard_map/ppermute | solution.py:35
  295.3 11.5 %collective-permute-start.25 = (f32[4,512]{1,0:T(4,128)}, f32[4,512]{1,0:T(4,128)}, u32[]{:S(2)}, u32[]{:S(2)}) collective-permute-start(f32[4,512]{1,0:T(4,128)} %fusion.46), channel_id=1, source_target_pairs={{0,64},{1,65},{2,66},{3,67},{4,68},{5,69},{6,70},{7,71},{8,72},{9,... | collective-permute-start | bytes 24584 | tf_op jit(solution)/shard_map/ppermute | solution.py:35
  302.1 58.5 %collective-permute-start.42 = (f32[512,64]{0,1:T(8,128)}, f32[512,64]{0,1:T(8,128)}, u32[]{:S(2)}, u32[]{:S(2)}) collective-permute-start(f32[512,64]{0,1:T(8,128)} %pad_maximum_fusion.11), channel_id=1, source_target_pairs={{16,0},{17,1},{18,2},{19,3},{20,4},{21,5},{22,6},{23,7},{24,8},{25... | collective-permute-start | bytes 393224 | tf_op jit(solution)/shard_map/ppermute | solution.py:35
  304.1 23.8 %collective-permute-start.43 = (f32[512,64]{0,1:T(8,128)}, f32[512,64]{0,1:T(8,128)S(1)}, u32[]{:S(2)}, u32[]{:S(2)}) collective-permute-start(f32[512,64]{0,1:T(8,128)} %concatenate.103), channel_id=1, source_target_pairs={{16,0},{17,1},{18,2},{19,3},{20,4},{21,5},{22,6},{23,7},{24,8},{25... | collective-permute-start | bytes 393224 | tf_op jit(solution)/shard_map/ppermute | solution.py:35
  311.4 9.5 %collective-permute-start.26 = (f32[4,512]{1,0:T(4,128)S(1)}, f32[4,512]{1,0:T(4,128)S(1)}, u32[]{:S(2)}, u32[]{:S(2)}) collective-permute-start(f32[4,512]{1,0:T(4,128)S(1)} %fusion.43), channel_id=1, source_target_pairs={{0,64},{1,65},{2,66},{3,67},{4,68},{5,69},{6,70},{7,71},{8,72},{9,... | collective-permute-start | bytes 24584 | tf_op jit(solution)/shard_map/ppermute | solution.py:35
  324.1 7.1 %collective-permute-start.27 = (f32[4,512]{1,0:T(4,128)S(1)}, f32[4,512]{1,0:T(4,128)S(1)}, u32[]{:S(2)}, u32[]{:S(2)}) collective-permute-start(f32[4,512]{1,0:T(4,128)S(1)} %fusion.41), channel_id=1, source_target_pairs={{0,1},{1,2},{2,3},{3,4},{4,5},{5,6},{6,7},{7,8},{8,9},{9,10},{10,1... | collective-permute-start | bytes 24584 | tf_op jit(solution)/shard_map/ppermute | solution.py:35
  343.2 5.7 %collective-permute-start.28 = (f32[4,512]{1,0:T(4,128)S(1)}, f32[4,512]{1,0:T(4,128)S(1)}, u32[]{:S(2)}, u32[]{:S(2)}) collective-permute-start(f32[4,512]{1,0:T(4,128)S(1)} %fusion.28), channel_id=1, source_target_pairs={{1,0},{2,1},{3,2},{4,3},{5,4},{6,5},{7,6},{8,7},{9,8},{10,9},{11,1... | collective-permute-start | bytes 24584 | tf_op jit(solution)/shard_map/ppermute | solution.py:35
  349.8 7.2 %collective-permute-start.29 = (f32[4,512]{1,0:T(4,128)S(1)}, f32[4,512]{1,0:T(4,128)S(1)}, u32[]{:S(2)}, u32[]{:S(2)}) collective-permute-start(f32[4,512]{1,0:T(4,128)S(1)} %fusion.26), channel_id=1, source_target_pairs={{2,0},{3,1},{4,2},{5,3},{6,4},{7,5},{8,6},{9,7},{10,8},{11,9},{12,... | collective-permute-start | bytes 24584 | tf_op jit(solution)/shard_map/ppermute | solution.py:35
  358.5 17.2 %collective-permute-start.32 = (f32[4,512]{1,0:T(4,128)}, f32[4,512]{1,0:T(4,128)}, u32[]{:S(2)}, u32[]{:S(2)}) collective-permute-start(f32[4,512]{1,0:T(4,128)} %fusion.24), channel_id=1, source_target_pairs={{4,0},{5,1},{6,2},{7,3},{8,4},{9,5},{10,6},{11,7},{12,8},{13,9},{1... | collective-permute-start | bytes 24584 | tf_op jit(solution)/shard_map/ppermute | solution.py:35
  366.1 63.6 %collective-permute-start.45 = (f32[512,128]{0,1:T(8,128)}, f32[512,128]{0,1:T(8,128)}, u32[]{:S(2)}, u32[]{:S(2)}) collective-permute-start(f32[512,128]{0,1:T(8,128)} %pad_maximum_fusion.9), channel_id=1, source_target_pairs={{32,0},{33,1},{34,2},{35,3},{36,4},{37,5},{38,6},{39,7},{40,8},{41... | collective-permute-start | bytes 786440 | tf_op jit(solution)/shard_map/ppermute | solution.py:35
  371.7 30.2 %collective-permute-start.46 = (f32[512,128]{0,1:T(8,128)}, f32[512,128]{0,1:T(8,128)S(1)}, u32[]{:S(2)}, u32[]{:S(2)}) collective-permute-start(f32[512,128]{0,1:T(8,128)} %concatenate.105), channel_id=1, source_target_pairs={{32,0},{33,1},{34,2},{35,3},{36,4},{37,5},{38,6},{39,7},{40,8},{41... | collective-permute-start | bytes 786440 | tf_op jit(solution)/shard_map/ppermute | solution.py:35
  379.4 19.4 %collective-permute-start.35 = (f32[4,512]{1,0:T(4,128)S(1)}, f32[4,512]{1,0:T(4,128)S(1)}, u32[]{:S(2)}, u32[]{:S(2)}) collective-permute-start(f32[4,512]{1,0:T(4,128)S(1)} %fusion.22), channel_id=1, source_target_pairs={{8,0},{9,1},{10,2},{11,3},{12,4},{13,5},{14,6},{15,7},{16,8},{17,9... | collective-permute-start | bytes 24584 | tf_op jit(solution)/shard_map/ppermute | solution.py:35
  399.7 8.7 %collective-permute-start.38 = (f32[4,512]{1,0:T(4,128)S(1)}, f32[4,512]{1,0:T(4,128)S(1)}, u32[]{:S(2)}, u32[]{:S(2)}) collective-permute-start(f32[4,512]{1,0:T(4,128)S(1)} %fusion.20), channel_id=1, source_target_pairs={{16,0},{17,1},{18,2},{19,3},{20,4},{21,5},{22,6},{23,7},{24,8},{25... | collective-permute-start | bytes 24584 | tf_op jit(solution)/shard_map/ppermute | solution.py:35
  411.2 10.3 %collective-permute-start.41 = (f32[4,512]{1,0:T(4,128)S(1)}, f32[4,512]{1,0:T(4,128)S(1)}, u32[]{:S(2)}, u32[]{:S(2)}) collective-permute-start(f32[4,512]{1,0:T(4,128)S(1)} %fusion.18), channel_id=1, source_target_pairs={{32,0},{33,1},{34,2},{35,3},{36,4},{37,5},{38,6},{39,7},{40,8},{41... | collective-permute-start | bytes 24584 | tf_op jit(solution)/shard_map/ppermute | solution.py:35
  424.6 5.7 %collective-permute-start.44 = (f32[4,512]{1,0:T(4,128)S(1)}, f32[4,512]{1,0:T(4,128)S(1)}, u32[]{:S(2)}, u32[]{:S(2)}) collective-permute-start(f32[4,512]{1,0:T(4,128)S(1)} %fusion.16), channel_id=1, source_target_pairs={{64,0},{65,1},{66,2},{67,3},{68,4},{69,5},{70,6},{71,7},{72,8},{73... | collective-permute-start | bytes 24584 | tf_op jit(solution)/shard_map/ppermute | solution.py:35
  432.7 5.5 %collective-permute-start.47 = (f32[4,512]{1,0:T(4,128)S(1)}, f32[4,512]{1,0:T(4,128)S(1)}, u32[]{:S(2)}, u32[]{:S(2)}) collective-permute-start(f32[4,512]{1,0:T(4,128)S(1)} %fusion.14), channel_id=1, source_target_pairs={{64,0},{65,1},{66,2},{67,3},{68,4},{69,5},{70,6},{71,7},{72,8},{73... | collective-permute-start | bytes 24584 | tf_op jit(solution)/shard_map/ppermute | solution.py:35
  440.7 5.5 %collective-permute-start.48 = (f32[4,512]{1,0:T(4,128)S(1)}, f32[4,512]{1,0:T(4,128)S(1)}, u32[]{:S(2)}, u32[]{:S(2)}) collective-permute-start(f32[4,512]{1,0:T(4,128)S(1)} %fusion.12), channel_id=1, source_target_pairs={{64,0},{65,1},{66,2},{67,3},{68,4},{69,5},{70,6},{71,7},{72,8},{73... | collective-permute-start | bytes 24584 | tf_op jit(solution)/shard_map/ppermute | solution.py:35
  448.7 5.7 %collective-permute-start.49 = (f32[4,512]{1,0:T(4,128)S(1)}, f32[4,512]{1,0:T(4,128)S(1)}, u32[]{:S(2)}, u32[]{:S(2)}) collective-permute-start(f32[4,512]{1,0:T(4,128)S(1)} %fusion.10), channel_id=1, source_target_pairs={{1,0},{2,1},{3,2},{4,3},{5,4},{6,5},{7,6},{8,7},{9,8},{10,9},{11,1... | collective-permute-start | bytes 24584 | tf_op jit(solution)/shard_map/ppermute | solution.py:35
  (112 other events, 1165.8 us)
Sparse Core Ops, SparseCore 0:
  9.8 26.9 all-gather.1

commit v3 on v2

--- a/solution.py
+++ b/solution.py
@@ -36,11 +36,11 @@
 
 
 def filter_apply(rows, power, left, right, offsets):
-    return transposed(rows, power) + transposed(product(rows, right), left) + offsets
+    return transposed(rows, power) + product(transposed(rows, right), left) + offsets
 
 
 def smoother_apply(rows, power, left, right, offsets):
-    return product(rows, power) + transposed(product(rows, right), left) + offsets
+    return product(rows, power) + product(transposed(rows, right), left) + offsets
 
 
 def per_device(dynamics, pattern, initial_mean, observed, obs_index, obs_noise):
@@ -89,11 +89,11 @@
     moved = [hit_columns]
     for _ in range(last):
         moved.append(product(transition, moved[-1]))
-    filt_u = jnp.stack([-gains[j] * moved[last - j][:, j] for j in range(span)], axis=1)
+    filt_u = jnp.stack([-gains[j] * moved[last - j][:, j] for j in range(span)], axis=0)
     reach = product(hits, transition)
     for m in range(last - 1, -1, -1):
         reach = jnp.where(column > m, product(reach * scales[m][None, :], transition), reach)
-    filt_v = reach.T
+    filt_v = reach
     filt_b = pushes[0]
     for j in range(1, span):
         filt_b = transposed(filt_b, transition) * scales[j][None, :] + pushes[j]
@@ -104,35 +104,41 @@
     moved = [hit_columns]
     for _ in range(last):
         moved.append(leading(transition, moved[-1]))
-    smooth_u = jnp.stack([-gains[j] * moved[j][:, j] for j in range(span)], axis=1)
+    smooth_u = jnp.stack([-gains[j] * moved[j][:, j] for j in range(span)], axis=0)
     reach = transposed(hits, transition)
     for m in range(1, span):
         reach = jnp.where(column < m, transposed(reach * scales[m][None, :], transition), reach)
-    smooth_v = reach.T
+    smooth_v = reach
 
     stored = []
     level = 0
     while 2**level < chain:
         distance = 2**level
         power = powers[level]
-        arrived_u, arrived_v, arrived_b, arrived_value = shifted(
-            (filt_u, filt_v, filt_b, value), distance, segments
-        )
+        rank = filt_u.shape[0]
+        packed = jnp.concatenate([filt_u, filt_v, filt_b, value], axis=0)
+        packed = shifted(packed, distance, segments)
+        arrived_u = packed[:rank]
+        arrived_v = packed[rank : 2 * rank]
+        arrived_b = packed[2 * rank : 2 * rank + seq_total]
+        arrived_value = packed[2 * rank + seq_total :]
         new_value = filter_apply(arrived_value, power, filt_u, filt_v, filt_b)
         value = jnp.where((segment >= distance) & (segment < 2 * distance), new_value, value)
         new_u = jnp.concatenate(
-            [product(power, arrived_u) + product(filt_u, leading(filt_v, arrived_u)), filt_u], axis=1
+            [transposed(arrived_u, power) + product(transposed(arrived_u, filt_v), filt_u), filt_u], axis=0
         )
-        new_v = jnp.concatenate([arrived_v, leading(power, filt_v)], axis=1)
-        filt_b = transposed(arrived_b, power) + transposed(product(arrived_b, filt_v), filt_u) + filt_b
+        new_v = jnp.concatenate([arrived_v, product(filt_v, power)], axis=0)
+        filt_b = filter_apply(arrived_b, power, filt_u, filt_v, filt_b)
         filt_u, filt_v = new_u, new_v
 
         stored.append((smooth_u, smooth_v))
-        arrived_u, arrived_v = shifted((smooth_u, smooth_v), -distance, segments)
+        packed = shifted(jnp.concatenate([smooth_u, smooth_v], axis=0), -distance, segments)
+        arrived_u = packed[:rank]
+        arrived_v = packed[rank:]
         new_u = jnp.concatenate(
-            [leading(power, arrived_u) + product(smooth_u, leading(smooth_v, arrived_u)), smooth_u], axis=1
+            [product(arrived_u, power) + product(transposed(arrived_u, smooth_v), smooth_u), smooth_u], axis=0
         )
-        new_v = jnp.concatenate([arrived_v, product(power, smooth_v)], axis=1)
+        new_v = jnp.concatenate([arrived_v, transposed(smooth_v, power)], axis=0)
         smooth_u, smooth_v = new_u, new_v
         level += 1
     stored.append((smooth_u, smooth_v))

time: 486 us -> 460 us (0.947)
  the two profiles are of different devices: /device:TPU:232 before, /device:TPU:16 now
where the time goes in v3:
time: 460 us; the launch traced here: 453 us
  matrix products  160 us (35%)
  starting transfers between devices  111 us (24%)
  local copies, waits for them, and re-layouts  84.9 us (18%)
  waiting for transfers between devices  62.8 us (14%)
  between operations  18.9 us (4%)
  blocking collectives  11.7 us (3%)
    ppermute x26, starting transfers between devices, shifted(): return lax.ppermute(block, AXES, route)  110 us
    dot_general x79, matrix products, transposed(): lax.dot_general(left, right, (((1,), (1,)), ((), ())), precision=lax.Prec...  91.1 us
    dot_general x81, matrix products, product(): jnp.dot(left, right, precision=lax.Precision.HIGHEST, preferred_element_t...  66.8 us
    ppermute x26, waiting for transfers between devices, shifted(): return lax.ppermute(block, AXES, route)  40.4 us
    all_gather x1, waiting for transfers between devices, per_device(): lax.all_gather(dynamics, 'state', axis=0, tiled=True) * block_mask  21.7 us
    concatenate x6, local copies, waits for them, and re-layouts, per_device(): packed = jnp.concatenate([filt_u, filt_v, filt_b, value], axis=0)  19.2 us
    concatenate x6, local copies, waits for them, and re-layouts, per_device(): jnp.concatenate([smooth_u, smooth_v], axis=0)  18.5 us
    concatenate x6, local copies, waits for them, and re-layouts, per_device(): jnp.concatenate([transposed(arrived_u, power) + product(transposed(arrive...  14.2 us
  transfers between devices with their start and end apart: 27, of which 13 were waited for; matrix products, arithmetic and copies ran while one was open for 35% of the time, Pallas kernels for 0%

profile of v3, /device:TPU:16, one launch (start us, length us, event | category | flops | bytes accessed | tf_op | source)
XLA Modules:
  0.0 453.0 jit_solution(6202459274452799813)
XLA Ops:
  10.7 2.6 multiply_reduce_fusion
  17.5 21.7 %all-gather.2.cloned.1.call-done = f32[512,512]{1,0:T(8,128)} async-done(((f32[128,512]{1,0:T(8,128)}), f32[512,512]{1,0:T(8,128)}) %all-gather.2.cloned.1.call-update) | async-done | bytes 1048592 | tf_op jit(solution)/shard_map/all_gather | solution.py:61
  54.7 12.9 %fusion.69 = f32[4,512]{1,0:T(4,128)S(1)} fusion(f32[4,512]{1,0:T(4,128)S(1)} %fusion.70, f32[512,512]{1,0:T(8,128)S(1)} %bitcast_multiply_fusion, f32[512]{0:T(512)S(1)} %bitcast.340, f32[4]{0:T(128)S(1)} %get-tuple-element.2, f32[512]{0:T(512)S(1)} %bitcast.326), kind=kOutput, calls=%fused_computation.125 | convolution fusion | flops 12589056 | bytes 1069072 | tf_op jit(solution)/shard_map/dot_general | solution.py:14
  73.8 2.2 collective-permute-start
  84.5 2.8 fusion.280
  90.3 7.7 %collective-permute-start.12 = (f32[8,512]{1,0:T(8,128)S(1)}, f32[8,512]{1,0:T(8,128)S(1)}, u32[]{:S(2)}, u32[]{:S(2)}) collective-permute-start(f32[8,512]{1,0:T(8,128)S(1)} %concatenate.150), channel_id=1, source_target_pairs={{1,0},{2,1},{3,2},{4,3},{5,4},{6,5},{7,6},{8,7},{9,8},{10,9},{11,1... | collective-permute-start | bytes 49160 | tf_op jit(solution)/shard_map/ppermute | solution.py:35
  98.0 2.2 fusion.290
  103.4 2.5 collective-permute-start.14
  106.9 2.2 fusion.63
  111.8 5.5 %collective-permute-start.1 = (f32[24,512]{1,0:T(8,128)S(1)}, f32[24,512]{1,0:T(8,128)S(1)}, u32[]{:S(2)}, u32[]{:S(2)}) collective-permute-start(f32[24,512]{1,0:T(8,128)S(1)} %concatenate.133), channel_id=1, source_target_pairs={{0,2},{1,3},{2,4},{3,5},{4,6},{5,7},{6,8},{7,9},{8,10},{9,11},{10,... | collective-permute-start | bytes 147464 | tf_op jit(solution)/shard_map/ppermute | solution.py:35
  120.5 2.4 concatenate.156
  122.9 2.0 collective-permute-start.16
  125.9 2.2 fusion.60
  130.7 3.0 concatenate.136
  133.7 2.4 collective-permute-start.2
  137.9 3.9 collective-permute-done.2
  142.7 2.2 convolution_add_fusion.7
  145.8 2.2 fusion.57
  149.8 3.6 concatenate.139
  153.4 2.2 collective-permute-start.3
  157.6 5.3 %collective-permute-done.3 = f32[72,512]{1,0:T(8,128)S(1)} collective-permute-done((f32[72,512]{1,0:T(8,128)}, f32[72,512]{1,0:T(8,128)S(1)}, u32[]{:S(2)}, u32[]{:S(2)}) %collective-permute-start.3) | collective-permute-done | bytes 147488 | tf_op jit(solution)/shard_map/ppermute | solution.py:35
  167.2 4.3 concatenate.142
  176.1 3.0 concatenate.159
  179.2 3.4 collective-permute-start.18
  182.6 3.1 concatenate.144
  191.1 2.3 fusion.51
  193.3 2.7 convolution_add_fusion.3
  196.0 2.3 fusion.50
  198.3 8.1 %concatenate.145 = f32[264,512]{1,0:T(8,128)} concatenate(f32[64,512]{1,0:T(8,128)} %convolution_add_fusion.3, f32[32,512]{1,0:T(8,128)S(1)} %convolution_add_fusion.5, f32[16,512]{1,0:T(8,128)S(1)} %convolution_add_fusion.7, f32[8,512]{1,0:T(8,128)} %copy-done.35, f32[4,512]{1,0:T(4,128)} %copy-done.42, f32[1,512]{1,0:T(1,128)} %copy-done.56, f32[1,512]{1,0:T(1,128)} %copy-done.76, ...), dimensions={0} | concatenate | bytes 1081344 | tf_op jit(solution)/shard_map/concatenate | solution.py:119
  206.4 4.9 %collective-permute-start.5 = (f32[264,512]{1,0:T(8,128)}, f32[264,512]{1,0:T(8,128)}, u32[]{:S(2)}, u32[]{:S(2)}) collective-permute-start(f32[264,512]{1,0:T(8,128)} %concatenate.145), channel_id=1, source_target_pairs={{0,32},{1,33},{2,34},{3,35},{4,36},{5,37},{6,38},{7,39},{8,40},{9,... | collective-permute-start | bytes 1622024 | tf_op jit(solution)/shard_map/ppermute | solution.py:35
  211.3 2.9 fusion.108
  214.3 3.2 concatenate.158
  219.2 4.6 %concatenate.147 = f32[128,512]{1,0:T(8,128)} concatenate(f32[64,512]{1,0:T(8,128)} %convolution_add_fusion.3, f32[32,512]{1,0:T(8,128)S(1)} %convolution_add_fusion.5, f32[16,512]{1,0:T(8,128)S(1)} %convolution_add_fusion.7, f32[8,512]{1,0:T(8,128)S(1)} %copy-done.36, f32[4,512]{1,0:T(4,128)S(1)} %copy-done.43, f32[1,512]{1,0:T(1,128)S(1)} %copy-done.58, f32[1,512]{1,0:T(1,128)} %copy-done.76, ...), dimensions={0} | concatenate | bytes 524288 | tf_op jit(solution)/shard_map/concatenate | solution.py:127
  229.2 2.3 fusion.48
  231.5 4.8 %collective-permute-start.6 = (f32[4,512]{1,0:T(4,128)}, f32[4,512]{1,0:T(4,128)}, u32[]{:S(2)}, u32[]{:S(2)}) collective-permute-start(f32[4,512]{1,0:T(4,128)} %fusion.48), channel_id=1, source_target_pairs={{0,64},{1,65},{2,66},{3,67},{4,68},{5,69},{6,70},{7,71},{8,72},{9,... | collective-permute-start | bytes 24584 | tf_op jit(solution)/shard_map/ppermute | solution.py:35
  238.0 2.9 convolution_add_fusion.1
  240.9 2.3 fusion.44
  243.2 6.4 %concatenate.149 = f32[256,512]{1,0:T(8,128)} concatenate(f32[128,512]{1,0:T(8,128)} %convolution_add_fusion.1, f32[64,512]{1,0:T(8,128)} %convolution_add_fusion.3, f32[32,512]{1,0:T(8,128)S(1)} %convolution_add_fusion.5, f32[16,512]{1,0:T(8,128)S(1)} %convolution_add_fusion.7, f32[8,512]{1,0:T(8,128)S(1)} %copy-done.36, f32[4,512]{1,0:T(4,128)S(1)} %copy-done.43, ...), dimensions={0} | concatenate | bytes 1048576 | tf_op jit(solution)/shard_map/concatenate | solution.py:127
  255.1 2.1 collective-permute-start.7
  257.3 3.4 collective-permute-done.7
  264.5 2.2 convolution_add_fusion.4
  270.6 2.1 collective-permute-start.9
  273.9 2.4 concatenate.161
  276.4 3.7 concatenate.162
  280.1 13.9 %collective-permute-start.20 = (f32[128,512]{1,0:T(8,128)}, f32[128,512]{1,0:T(8,128)}, u32[]{:S(2)}, u32[]{:S(2)}) collective-permute-start(f32[128,512]{1,0:T(8,128)} %concatenate.162), channel_id=1, source_target_pairs={{16,0},{17,1},{18,2},{19,3},{20,4},{21,5},{22,6},{23,7},{24,8},{25... | collective-permute-start | bytes 786440 | tf_op jit(solution)/shard_map/ppermute | solution.py:35
  308.8 3.8 collective-permute-start.10
  315.4 3.8 collective-permute-start.11
  319.5 5.8 %collective-permute-done.11 = f32[4,512]{1,0:T(4,128)S(1)} collective-permute-done((f32[4,512]{1,0:T(4,128)S(1)}, f32[4,512]{1,0:T(4,128)S(1)}, u32[]{:S(2)}, u32[]{:S(2)}) %collective-permute-start.11) | collective-permute-done | bytes 8224 | tf_op jit(solution)/shard_map/ppermute | solution.py:35
  326.3 2.2 collective-permute-start.13
  328.4 2.3 convolution_add_fusion.2
  333.8 3.0 collective-permute-start.15
  338.0 7.0 %concatenate.164 = f32[128,512]{1,0:T(8,128)} concatenate(f32[64,512]{1,0:T(8,128)} %convolution_add_fusion.2, f32[32,512]{1,0:T(8,128)} %convolution_add_fusion.4, f32[16,512]{1,0:T(8,128)} %copy-done.28, f32[8,512]{1,0:T(8,128)} %copy-done.32, f32[4,512]{1,0:T(4,128)S(1)} %convolution_add_fusion.17, f32[1,512]{1,0:T(1,128)} %copy-done.59, f32[1,512]{1,0:T(1,128)} %copy-done.67, ...), dimensions={0} | concatenate | bytes 524288 | tf_op jit(solution)/shard_map/concatenate | solution.py:138
  345.0 9.2 %concatenate.165 = f32[256,512]{1,0:T(8,128)} concatenate(f32[64,512]{1,0:T(8,128)} %convolution_add_fusion.2, f32[32,512]{1,0:T(8,128)} %convolution_add_fusion.4, f32[16,512]{1,0:T(8,128)} %copy-done.28, f32[8,512]{1,0:T(8,128)} %copy-done.32, f32[4,512]{1,0:T(4,128)S(1)} %convolution_add_fusion.17, f32[1,512]{1,0:T(1,128)} %copy-done.59, f32[1,512]{1,0:T(1,128)} %copy-done.67, ...), dimensions={0} | concatenate | bytes 1048576 | tf_op jit(solution)/shard_map/concatenate | solution.py:135
  354.2 5.3 %collective-permute-start.22 = (f32[256,512]{1,0:T(8,128)}, f32[256,512]{1,0:T(8,128)S(1)}, u32[]{:S(2)}, u32[]{:S(2)}) collective-permute-start(f32[256,512]{1,0:T(8,128)} %concatenate.165), channel_id=1, source_target_pairs={{32,0},{33,1},{34,2},{35,3},{36,4},{37,5},{38,6},{39,7},{40,8},{41... | collective-permute-start | bytes 1572872 | tf_op jit(solution)/shard_map/ppermute | solution.py:35
  362.5 6.3 %collective-permute-start.17 = (f32[4,512]{1,0:T(4,128)S(1)}, f32[4,512]{1,0:T(4,128)S(1)}, u32[]{:S(2)}, u32[]{:S(2)}) collective-permute-start(f32[4,512]{1,0:T(4,128)S(1)} %fusion.20), channel_id=1, source_target_pairs={{16,0},{17,1},{18,2},{19,3},{20,4},{21,5},{22,6},{23,7},{24,8},{25... | collective-permute-start | bytes 24584 | tf_op jit(solution)/shard_map/ppermute | solution.py:35
  368.9 5.9 %collective-permute-done.22 = f32[256,512]{1,0:T(8,128)S(1)} collective-permute-done((f32[256,512]{1,0:T(8,128)}, f32[256,512]{1,0:T(8,128)S(1)}, u32[]{:S(2)}, u32[]{:S(2)}) %collective-permute-start.22) | collective-permute-done | bytes 524320 | tf_op jit(solution)/shard_map/ppermute | solution.py:35
  376.9 6.0 %collective-permute-start.19 = (f32[4,512]{1,0:T(4,128)S(1)}, f32[4,512]{1,0:T(4,128)S(1)}, u32[]{:S(2)}, u32[]{:S(2)}) collective-permute-start(f32[4,512]{1,0:T(4,128)S(1)} %fusion.18), channel_id=1, source_target_pairs={{32,0},{33,1},{34,2},{35,3},{36,4},{37,5},{38,6},{39,7},{40,8},{41... | collective-permute-start | bytes 24584 | tf_op jit(solution)/shard_map/ppermute | solution.py:35
  383.2 5.3 %collective-permute-done.19 = f32[4,512]{1,0:T(4,128)S(1)} collective-permute-done((f32[4,512]{1,0:T(4,128)S(1)}, f32[4,512]{1,0:T(4,128)S(1)}, u32[]{:S(2)}, u32[]{:S(2)}) %collective-permute-start.19) | collective-permute-done | bytes 8224 | tf_op jit(solution)/shard_map/ppermute | solution.py:35
  389.8 2.9 collective-permute-start.21
  399.7 3.6 collective-permute-done.23
  404.7 2.0 collective-permute-start.24
  406.7 3.6 collective-permute-done.24
  411.8 13.9 %collective-permute-start.25 = (f32[4,512]{1,0:T(4,128)S(1)}, f32[4,512]{1,0:T(4,128)S(1)}, u32[]{:S(2)}, u32[]{:S(2)}) collective-permute-start(f32[4,512]{1,0:T(4,128)S(1)} %fusion.10), channel_id=1, source_target_pairs={{1,0},{2,1},{3,2},{4,3},{5,4},{6,5},{7,6},{8,7},{9,8},{10,9},{11,1... | collective-permute-start | bytes 24584 | tf_op jit(solution)/shard_map/ppermute | solution.py:35
  432.9 11.7 %all_to_all.15 = f32[2,4,4,512]{3,1,0,2:T(4,128)S(1)} all-to-all(f32[2,4,4,512]{3,1,0,2:T(4,128)S(1)} %copy.10), channel_id=1, replica_groups=mesh['tm'=64,'state'=4] {'state'}, dimensions={2} | all-to-all | bytes 131072 | tf_op jit(solution)/shard_map/all_to_all | solution.py:192
  (502 shorter events, 143.7 us)
Async XLA Ops:
  7.2 32.1 %all-gather.2.cloned.1.call-start = ((), (), s32[]{:S(2)}) async-start(), calls=%async_computation.1 | async-start | bytes 1310720 | tf_op jit(solution)/shard_map/all_gather | solution.py:61
  13.4 36.4 %copy-start.128 = (f32[4]{0:T(128)}, f32[4]{0:T(128)S(1)}, u32[]{:S(2)}) copy-start(f32[4]{0:T(128)S(1)} %get-tuple-element.5) | copy-start | bytes 52
  13.4 37.3 %copy-start.129 = (f32[4]{0:T(128)}, f32[4]{0:T(128)S(1)}, u32[]{:S(2)}) copy-start(f32[4]{0:T(128)S(1)} %get-tuple-element.4) | copy-start | bytes 52
  13.4 39.3 %copy-start.133 = (f32[4]{0:T(128)}, f32[4]{0:T(128)S(1)}, u32[]{:S(2)}) copy-start(f32[4]{0:T(128)S(1)} %get-tuple-element.3) | copy-start | bytes 52
  13.4 41.3 %copy-start.131 = (f32[4]{0:T(128)}, f32[4]{0:T(128)S(1)}, u32[]{:S(2)}) copy-start(f32[4]{0:T(128)S(1)} %get-tuple-element.2) | copy-start | bytes 52
  16.9 103.6 %copy-start.59 = (f32[1,512]{1,0:T(1,128)}, f32[1,512]{1,0:T(1,128)S(1)}, u32[]{:S(2)}) copy-start(f32[1,512]{1,0:T(1,128)S(1)} %get-tuple-element.10) | copy-start | bytes 6148
  16.9 132.9 %copy-start.71 = (f32[1,512]{1,0:T(1,128)}, f32[1,512]{1,0:T(1,128)S(1)}, u32[]{:S(2)}) copy-start(f32[1,512]{1,0:T(1,128)S(1)} %get-tuple-element.11) | copy-start | bytes 6148
  17.5 55.1 %copy-start.111 = (f32[1,512]{1,0:T(1,128)}, f32[1,512]{1,0:T(1,128)S(1)}, u32[]{:S(2)}) copy-start(f32[1,512]{1,0:T(1,128)S(1)} %get-tuple-element.13) | copy-start | bytes 6148
  17.5 69.9 %copy-start.95 = (f32[1,512]{1,0:T(1,128)}, f32[1,512]{1,0:T(1,128)S(1)}, u32[]{:S(2)}) copy-start(f32[1,512]{1,0:T(1,128)S(1)} %get-tuple-element.14) | copy-start | bytes 6148
  17.5 70.8 %copy-start.98 = (f32[1,512]{1,0:T(1,128)}, f32[1,512]{1,0:T(1,128)S(1)}, u32[]{:S(2)}) copy-start(f32[1,512]{1,0:T(1,128)S(1)} %get-tuple-element.15) | copy-start | bytes 6148
  17.5 71.8 %copy-start.105 = (f32[1,512]{1,0:T(1,128)}, f32[1,512]{1,0:T(1,128)S(1)}, u32[]{:S(2)}) copy-start(f32[1,512]{1,0:T(1,128)S(1)} %get-tuple-element.12) | copy-start | bytes 6148
  17.5 32.3 %copy-start.126 = (f32[1,512]{1,0:T(1,128)}, f32[1,512]{1,0:T(1,128)S(1)}, u32[]{:S(2)}) copy-start(f32[1,512]{1,0:T(1,128)S(1)} %get-tuple-element.19) | copy-start | bytes 6148
  17.5 33.2 %copy-start.124 = (f32[1,512]{1,0:T(1,128)}, f32[1,512]{1,0:T(1,128)S(1)}, u32[]{:S(2)}) copy-start(f32[1,512]{1,0:T(1,128)S(1)} %get-tuple-element.18) | copy-start | bytes 6148
  17.5 35.2 %copy-start.122 = (f32[1,512]{1,0:T(1,128)}, f32[1,512]{1,0:T(1,128)S(1)}, u32[]{:S(2)}) copy-start(f32[1,512]{1,0:T(1,128)S(1)} %get-tuple-element.17) | copy-start | bytes 6148
  17.5 37.2 %copy-start.120 = (f32[1,512]{1,0:T(1,128)}, f32[1,512]{1,0:T(1,128)S(1)}, u32[]{:S(2)}) copy-start(f32[1,512]{1,0:T(1,128)S(1)} %get-tuple-element.16) | copy-start | bytes 6148
  46.7 103.1 %copy-start.56 = (f32[1,512]{1,0:T(1,128)}, f32[1,512]{1,0:T(1,128)S(1)}, u32[]{:S(2)}) copy-start(f32[1,512]{1,0:T(1,128)S(1)} %fusion.73) | copy-start | bytes 6148
  48.0 101.7 %copy-start.74 = (f32[1,512]{1,0:T(1,128)}, f32[1,512]{1,0:T(1,128)S(1)}, u32[]{:S(2)}) copy-start(f32[1,512]{1,0:T(1,128)S(1)} %get-tuple-element.28) | copy-start | bytes 6148
  48.0 101.7 %copy-start.76 = (f32[1,512]{1,0:T(1,128)}, f32[1,512]{1,0:T(1,128)S(1)}, u32[]{:S(2)}) copy-start(f32[1,512]{1,0:T(1,128)S(1)} %get-tuple-element.29) | copy-start | bytes 6148
  48.1 72.4 %copy-start.63 = (f32[1,512]{1,0:T(1,128)}, f32[1,512]{1,0:T(1,128)S(1)}, u32[]{:S(2)}) copy-start(f32[1,512]{1,0:T(1,128)S(1)} %get-tuple-element.30) | copy-start | bytes 6148
  48.1 72.4 %copy-start.67 = (f32[1,512]{1,0:T(1,128)}, f32[1,512]{1,0:T(1,128)S(1)}, u32[]{:S(2)}) copy-start(f32[1,512]{1,0:T(1,128)S(1)} %get-tuple-element.31) | copy-start | bytes 6148
  73.8 32.2 %collective-permute-start = (f32[16,512]{1,0:T(8,128)S(1)}, f32[16,512]{1,0:T(8,128)S(1)}, u32[]{:S(2)}, u32[]{:S(2)}) collective-permute-start(f32[16,512]{1,0:T(8,128)S(1)} %concatenate.132), channel_id=1, source_target_pairs={{0,1},{1,2},{2,3},{3,4},{4,5},{5,6},{6,7},{7,8},{8,9},{9,10},{10,1... | collective-permute-start | bytes 98312 | tf_op jit(solution)/shard_map/ppermute | solution.py:35
  90.3 9.9 %collective-permute-start.12 = (f32[8,512]{1,0:T(8,128)S(1)}, f32[8,512]{1,0:T(8,128)S(1)}, u32[]{:S(2)}, u32[]{:S(2)}) collective-permute-start(f32[8,512]{1,0:T(8,128)S(1)} %concatenate.150), channel_id=1, source_target_pairs={{1,0},{2,1},{3,2},{4,3},{5,4},{6,5},{7,6},{8,7},{9,8},{10,9},{11,1... | collective-permute-start | bytes 49160 | tf_op jit(solution)/shard_map/ppermute | solution.py:35
  100.2 17.1 %copy-start.85 = (f32[4,512]{1,0:T(4,128)}, f32[4,512]{1,0:T(4,128)S(1)}, u32[]{:S(2)}) copy-start(f32[4,512]{1,0:T(4,128)S(1)} %fusion.290) | copy-start | bytes 24580
  100.5 16.8 %copy-start.87 = (f32[4,512]{1,0:T(4,128)}, f32[4,512]{1,0:T(4,128)S(1)}, u32[]{:S(2)}) copy-start(f32[4,512]{1,0:T(4,128)S(1)} %slice.367) | copy-start | bytes 24580
  103.3 32.8 %copy-start.52 = (f32[8,512]{1,0:T(8,128)}, f32[8,512]{1,0:T(8,128)S(1)}, u32[]{:S(2)}) copy-start(f32[8,512]{1,0:T(8,128)S(1)} %fusion.131) | copy-start | bytes 49156
  103.4 13.8 %collective-permute-start.14 = (f32[16,512]{1,0:T(8,128)S(1)}, f32[16,512]{1,0:T(8,128)S(1)}, u32[]{:S(2)}, u32[]{:S(2)}) collective-permute-start(f32[16,512]{1,0:T(8,128)S(1)} %concatenate.153), channel_id=1, source_target_pairs={{2,0},{3,1},{4,2},{5,3},{6,4},{7,5},{8,6},{9,7},{10,8},{11,9},{12,... | collective-permute-start | bytes 98312 | tf_op jit(solution)/shard_map/ppermute | solution.py:35
  110.0 72.5 %copy-start.42 = (f32[4,512]{1,0:T(4,128)}, f32[4,512]{1,0:T(4,128)S(1)}, u32[]{:S(2)}) copy-start(f32[4,512]{1,0:T(4,128)S(1)} %convolution_add_fusion.35) | copy-start | bytes 24580
  111.8 13.2 %collective-permute-start.1 = (f32[24,512]{1,0:T(8,128)S(1)}, f32[24,512]{1,0:T(8,128)S(1)}, u32[]{:S(2)}, u32[]{:S(2)}) collective-permute-start(f32[24,512]{1,0:T(8,128)S(1)} %concatenate.133), channel_id=1, source_target_pairs={{0,2},{1,3},{2,4},{3,5},{4,6},{5,7},{6,8},{7,9},{8,10},{9,11},{10,... | collective-permute-start | bytes 147464 | tf_op jit(solution)/shard_map/ppermute | solution.py:35
  117.6 18.6 %copy-start.54 = (f32[8,512]{1,0:T(8,128)}, f32[8,512]{1,0:T(8,128)S(1)}, u32[]{:S(2)}) copy-start(f32[8,512]{1,0:T(8,128)S(1)} %slice.369) | copy-start | bytes 49156
  119.4 56.7 %copy-start.32 = (f32[8,512]{1,0:T(8,128)}, f32[8,512]{1,0:T(8,128)S(1)}, u32[]{:S(2)}) copy-start(f32[8,512]{1,0:T(8,128)S(1)} %convolution_add_fusion.8) | copy-start | bytes 49156
  120.4 55.7 %copy-start.48 = (f32[16,512]{1,0:T(8,128)}, f32[16,512]{1,0:T(8,128)S(1)}, u32[]{:S(2)}) copy-start(f32[16,512]{1,0:T(8,128)S(1)} %fusion.119) | copy-start | bytes 98308
  120.5 16.6 %copy-start.81 = (f32[16,512]{1,0:T(8,128)}, f32[16,512]{1,0:T(8,128)S(1)}, u32[]{:S(2)}) copy-start(f32[16,512]{1,0:T(8,128)S(1)} %concatenate.155) | copy-start | bytes 98308
  122.9 13.2 %collective-permute-start.16 = (f32[32,512]{1,0:T(8,128)}, f32[32,512]{1,0:T(8,128)}, u32[]{:S(2)}, u32[]{:S(2)}) collective-permute-start(f32[32,512]{1,0:T(8,128)} %concatenate.156), channel_id=1, source_target_pairs={{4,0},{5,1},{6,2},{7,3},{8,4},{9,5},{10,6},{11,7},{12,8},{13,9},{1... | collective-permute-start | bytes 196616 | tf_op jit(solution)/shard_map/ppermute | solution.py:35
  129.0 53.5 %copy-start.35 = (f32[8,512]{1,0:T(8,128)}, f32[8,512]{1,0:T(8,128)S(1)}, u32[]{:S(2)}) copy-start(f32[8,512]{1,0:T(8,128)S(1)} %convolution_add_fusion.9) | copy-start | bytes 49156
  133.7 8.1 %collective-permute-start.2 = (f32[40,512]{1,0:T(8,128)}, f32[40,512]{1,0:T(8,128)S(1)}, u32[]{:S(2)}, u32[]{:S(2)}) collective-permute-start(f32[40,512]{1,0:T(8,128)} %concatenate.136), channel_id=1, source_target_pairs={{0,4},{1,5},{2,6},{3,7},{4,8},{5,9},{6,10},{7,11},{8,12},{9,13},{1... | collective-permute-start | bytes 245768 | tf_op jit(solution)/shard_map/ppermute | solution.py:35
  148.0 16.0 %copy-start.101 = (f32[4,512]{1,0:T(4,128)}, f32[4,512]{1,0:T(4,128)S(1)}, u32[]{:S(2)}) copy-start(f32[4,512]{1,0:T(4,128)S(1)} %fusion.57) | copy-start | bytes 24580
  153.4 9.5 %collective-permute-start.3 = (f32[72,512]{1,0:T(8,128)}, f32[72,512]{1,0:T(8,128)S(1)}, u32[]{:S(2)}, u32[]{:S(2)}) collective-permute-start(f32[72,512]{1,0:T(8,128)} %concatenate.139), channel_id=1, source_target_pairs={{0,8},{1,9},{2,10},{3,11},{4,12},{5,13},{6,14},{7,15},{8,16},{9,17... | collective-permute-start | bytes 442376 | tf_op jit(solution)/shard_map/ppermute | solution.py:35
  171.5 14.9 %collective-permute-start.4 = (f32[136,512]{1,0:T(8,128)}, f32[136,512]{1,0:T(8,128)}, u32[]{:S(2)}, u32[]{:S(2)}) collective-permute-start(f32[136,512]{1,0:T(8,128)} %concatenate.142), channel_id=1, source_target_pairs={{0,16},{1,17},{2,18},{3,19},{4,20},{5,21},{6,22},{7,23},{8,24},{9,... | collective-permute-start | bytes 835592 | tf_op jit(solution)/shard_map/ppermute | solution.py:35
  175.3 39.0 %copy-start.28 = (f32[16,512]{1,0:T(8,128)}, f32[16,512]{1,0:T(8,128)S(1)}, u32[]{:S(2)}) copy-start(f32[16,512]{1,0:T(8,128)S(1)} %convolution_add_fusion.6) | copy-start | bytes 98308
  179.2 38.3 %collective-permute-start.18 = (f32[64,512]{1,0:T(8,128)}, f32[64,512]{1,0:T(8,128)}, u32[]{:S(2)}, u32[]{:S(2)}) collective-permute-start(f32[64,512]{1,0:T(8,128)} %concatenate.159), channel_id=1, source_target_pairs={{8,0},{9,1},{10,2},{11,3},{12,4},{13,5},{14,6},{15,7},{16,8},{17,9... | collective-permute-start | bytes 393224 | tf_op jit(solution)/shard_map/ppermute | solution.py:35
  206.4 19.8 %collective-permute-start.5 = (f32[264,512]{1,0:T(8,128)}, f32[264,512]{1,0:T(8,128)}, u32[]{:S(2)}, u32[]{:S(2)}) collective-permute-start(f32[264,512]{1,0:T(8,128)} %concatenate.145), channel_id=1, source_target_pairs={{0,32},{1,33},{2,34},{3,35},{4,36},{5,37},{6,38},{7,39},{8,40},{9,... | collective-permute-start | bytes 1622024 | tf_op jit(solution)/shard_map/ppermute | solution.py:35
  231.5 19.1 %collective-permute-start.6 = (f32[4,512]{1,0:T(4,128)}, f32[4,512]{1,0:T(4,128)}, u32[]{:S(2)}, u32[]{:S(2)}) collective-permute-start(f32[4,512]{1,0:T(4,128)} %fusion.48), channel_id=1, source_target_pairs={{0,64},{1,65},{2,66},{3,67},{4,68},{5,69},{6,70},{7,71},{8,72},{9,... | collective-permute-start | bytes 24584 | tf_op jit(solution)/shard_map/ppermute | solution.py:35
  255.1 5.7 %collective-permute-start.7 = (f32[4,512]{1,0:T(4,128)S(1)}, f32[4,512]{1,0:T(4,128)S(1)}, u32[]{:S(2)}, u32[]{:S(2)}) collective-permute-start(f32[4,512]{1,0:T(4,128)S(1)} %fusion.46), channel_id=1, source_target_pairs={{0,64},{1,65},{2,66},{3,67},{4,68},{5,69},{6,70},{7,71},{8,72},{9,... | collective-permute-start | bytes 24584 | tf_op jit(solution)/shard_map/ppermute | solution.py:35
  262.6 5.5 %collective-permute-start.8 = (f32[4,512]{1,0:T(4,128)S(1)}, f32[4,512]{1,0:T(4,128)S(1)}, u32[]{:S(2)}, u32[]{:S(2)}) collective-permute-start(f32[4,512]{1,0:T(4,128)S(1)} %fusion.43), channel_id=1, source_target_pairs={{0,64},{1,65},{2,66},{3,67},{4,68},{5,69},{6,70},{7,71},{8,72},{9,... | collective-permute-start | bytes 24584 | tf_op jit(solution)/shard_map/ppermute | solution.py:35
  270.6 23.4 %collective-permute-start.9 = (f32[4,512]{1,0:T(4,128)}, f32[4,512]{1,0:T(4,128)}, u32[]{:S(2)}, u32[]{:S(2)}) collective-permute-start(f32[4,512]{1,0:T(4,128)} %fusion.41), channel_id=1, source_target_pairs={{0,1},{1,2},{2,3},{3,4},{4,5},{5,6},{6,7},{7,8},{8,9},{9,10},{10,1... | collective-permute-start | bytes 24584 | tf_op jit(solution)/shard_map/ppermute | solution.py:35
  280.1 15.7 %copy-start.125 = (f32[1,512]{1,0:T(1,128)S(1)}, f32[1,512]{1,0:T(1,128)}, u32[]{:S(2)}) copy-start(f32[1,512]{1,0:T(1,128)} %copy-done.124) | copy-start | bytes 6148
  280.1 15.7 %copy-start.130 = (f32[4]{0:T(128)S(1)}, f32[4]{0:T(128)}, u32[]{:S(2)}) copy-start(f32[4]{0:T(128)} %copy-done.129) | copy-start | bytes 52
  280.1 32.5 %collective-permute-start.20 = (f32[128,512]{1,0:T(8,128)}, f32[128,512]{1,0:T(8,128)}, u32[]{:S(2)}, u32[]{:S(2)}) collective-permute-start(f32[128,512]{1,0:T(8,128)} %concatenate.162), channel_id=1, source_target_pairs={{16,0},{17,1},{18,2},{19,3},{20,4},{21,5},{22,6},{23,7},{24,8},{25... | collective-permute-start | bytes 786440 | tf_op jit(solution)/shard_map/ppermute | solution.py:35
  308.8 16.8 %copy-start.13 = (f32[512,512]{1,0:T(8,128)S(1)}, f32[512,512]{1,0:T(8,128)}, u32[]{:S(2)}) copy-start(f32[512,512]{1,0:T(8,128)} %copy-done.9) | copy-start | bytes 3145732
  308.8 5.7 %collective-permute-start.10 = (f32[4,512]{1,0:T(4,128)S(1)}, f32[4,512]{1,0:T(4,128)S(1)}, u32[]{:S(2)}, u32[]{:S(2)}) collective-permute-start(f32[4,512]{1,0:T(4,128)S(1)} %fusion.28), channel_id=1, source_target_pairs={{1,0},{2,1},{3,2},{4,3},{5,4},{6,5},{7,6},{8,7},{9,8},{10,9},{11,1... | collective-permute-start | bytes 24584 | tf_op jit(solution)/shard_map/ppermute | solution.py:35
  315.4 9.9 %collective-permute-start.11 = (f32[4,512]{1,0:T(4,128)S(1)}, f32[4,512]{1,0:T(4,128)S(1)}, u32[]{:S(2)}, u32[]{:S(2)}) collective-permute-start(f32[4,512]{1,0:T(4,128)S(1)} %fusion.26), channel_id=1, source_target_pairs={{2,0},{3,1},{4,2},{5,3},{6,4},{7,5},{8,6},{9,7},{10,8},{11,9},{12,... | collective-permute-start | bytes 24584 | tf_op jit(solution)/shard_map/ppermute | solution.py:35
  326.3 5.4 %collective-permute-start.13 = (f32[4,512]{1,0:T(4,128)S(1)}, f32[4,512]{1,0:T(4,128)S(1)}, u32[]{:S(2)}, u32[]{:S(2)}) collective-permute-start(f32[4,512]{1,0:T(4,128)S(1)} %fusion.24), channel_id=1, source_target_pairs={{4,0},{5,1},{6,2},{7,3},{8,4},{9,5},{10,6},{11,7},{12,8},{13,9},{1... | collective-permute-start | bytes 24584 | tf_op jit(solution)/shard_map/ppermute | solution.py:35
  333.8 25.7 %collective-permute-start.15 = (f32[4,512]{1,0:T(4,128)}, f32[4,512]{1,0:T(4,128)}, u32[]{:S(2)}, u32[]{:S(2)}) collective-permute-start(f32[4,512]{1,0:T(4,128)} %fusion.22), channel_id=1, source_target_pairs={{8,0},{9,1},{10,2},{11,3},{12,4},{13,5},{14,6},{15,7},{16,8},{17,9... | collective-permute-start | bytes 24584 | tf_op jit(solution)/shard_map/ppermute | solution.py:35
  354.2 20.6 %collective-permute-start.22 = (f32[256,512]{1,0:T(8,128)}, f32[256,512]{1,0:T(8,128)S(1)}, u32[]{:S(2)}, u32[]{:S(2)}) collective-permute-start(f32[256,512]{1,0:T(8,128)} %concatenate.165), channel_id=1, source_target_pairs={{32,0},{33,1},{34,2},{35,3},{36,4},{37,5},{38,6},{39,7},{40,8},{41... | collective-permute-start | bytes 1572872 | tf_op jit(solution)/shard_map/ppermute | solution.py:35
  362.5 12.6 %collective-permute-start.17 = (f32[4,512]{1,0:T(4,128)S(1)}, f32[4,512]{1,0:T(4,128)S(1)}, u32[]{:S(2)}, u32[]{:S(2)}) collective-permute-start(f32[4,512]{1,0:T(4,128)S(1)} %fusion.20), channel_id=1, source_target_pairs={{16,0},{17,1},{18,2},{19,3},{20,4},{21,5},{22,6},{23,7},{24,8},{25... | collective-permute-start | bytes 24584 | tf_op jit(solution)/shard_map/ppermute | solution.py:35
  374.8 17.9 %copy-start.44 = (f32[256,512]{1,0:T(8,128)}, f32[256,512]{1,0:T(8,128)S(1)}, u32[]{:S(2)}) copy-start(f32[256,512]{1,0:T(8,128)S(1)} %collective-permute-done.22) | copy-start | bytes 1572868
  376.9 11.7 %collective-permute-start.19 = (f32[4,512]{1,0:T(4,128)S(1)}, f32[4,512]{1,0:T(4,128)S(1)}, u32[]{:S(2)}, u32[]{:S(2)}) collective-permute-start(f32[4,512]{1,0:T(4,128)S(1)} %fusion.18), channel_id=1, source_target_pairs={{32,0},{33,1},{34,2},{35,3},{36,4},{37,5},{38,6},{39,7},{40,8},{41... | collective-permute-start | bytes 24584 | tf_op jit(solution)/shard_map/ppermute | solution.py:35
  389.8 6.4 %collective-permute-start.21 = (f32[4,512]{1,0:T(4,128)S(1)}, f32[4,512]{1,0:T(4,128)S(1)}, u32[]{:S(2)}, u32[]{:S(2)}) collective-permute-start(f32[4,512]{1,0:T(4,128)S(1)} %fusion.16), channel_id=1, source_target_pairs={{64,0},{65,1},{66,2},{67,3},{68,4},{69,5},{70,6},{71,7},{72,8},{73... | collective-permute-start | bytes 24584 | tf_op jit(solution)/shard_map/ppermute | solution.py:35
  397.7 5.5 %collective-permute-start.23 = (f32[4,512]{1,0:T(4,128)S(1)}, f32[4,512]{1,0:T(4,128)S(1)}, u32[]{:S(2)}, u32[]{:S(2)}) collective-permute-start(f32[4,512]{1,0:T(4,128)S(1)} %fusion.14), channel_id=1, source_target_pairs={{64,0},{65,1},{66,2},{67,3},{68,4},{69,5},{70,6},{71,7},{72,8},{73... | collective-permute-start | bytes 24584 | tf_op jit(solution)/shard_map/ppermute | solution.py:35
  404.7 5.5 %collective-permute-start.24 = (f32[4,512]{1,0:T(4,128)S(1)}, f32[4,512]{1,0:T(4,128)S(1)}, u32[]{:S(2)}, u32[]{:S(2)}) collective-permute-start(f32[4,512]{1,0:T(4,128)S(1)} %fusion.12), channel_id=1, source_target_pairs={{64,0},{65,1},{66,2},{67,3},{68,4},{69,5},{70,6},{71,7},{72,8},{73... | collective-permute-start | bytes 24584 | tf_op jit(solution)/shard_map/ppermute | solution.py:35
  411.2 15.9 %copy-start.80 = (f32[4,4,512]{2,1,0:T(4,128)S(1)}, f32[4,4,512]{2,1,0:T(4,128)}, u32[]{:S(2)}) copy-start(f32[4,4,512]{2,1,0:T(4,128)} %copy-done.79) | copy-start | bytes 98308
  411.2 15.9 %copy-start.107 = (f32[1,512]{1,0:T(1,128)S(1)}, f32[1,512]{1,0:T(1,128)}, u32[]{:S(2)}) copy-start(f32[1,512]{1,0:T(1,128)} %copy-done.105) | copy-start | bytes 6148
  411.8 16.5 %copy-start.100 = (f32[1,512]{1,0:T(1,128)S(1)}, f32[1,512]{1,0:T(1,128)}, u32[]{:S(2)}) copy-start(f32[1,512]{1,0:T(1,128)} %copy-done.98) | copy-start | bytes 6148
  411.8 15.3 %collective-permute-start.25 = (f32[4,512]{1,0:T(4,128)S(1)}, f32[4,512]{1,0:T(4,128)S(1)}, u32[]{:S(2)}, u32[]{:S(2)}) collective-permute-start(f32[4,512]{1,0:T(4,128)S(1)} %fusion.10), channel_id=1, source_target_pairs={{1,0},{2,1},{3,2},{4,3},{5,4},{6,5},{7,6},{8,7},{9,8},{10,9},{11,1... | collective-permute-start | bytes 24584 | tf_op jit(solution)/shard_map/ppermute | solution.py:35
  (101 other events, 374.9 us)
Sparse Core Ops, SparseCore 0:
  9.8 29.4 all-gather.1

commit v4 on v3

--- a/solution.py
+++ b/solution.py
@@ -58,7 +58,13 @@
 
     present = jnp.maximum(pattern, jnp.eye(blocks, dtype=jnp.int32))
     block_mask = jnp.repeat(jnp.repeat(present, block_span, 0), block_span, 1).astype(jnp.float32)
-    transition = lax.all_gather(dynamics, "state", axis=0, tiled=True) * block_mask
+    pieces = [dynamics]
+    for step in range(1, members):
+        route = [(i, (i + step) % members) for i in range(members)]
+        pieces.append(lax.ppermute(dynamics, "state", route))
+    order = (member - jnp.arange(members, dtype=jnp.int32)) % members
+    gathered = jnp.take(jnp.stack(pieces), order, axis=0).reshape(state_width, state_width)
+    transition = gathered * block_mask
 
     first = member * span
     obs_here = lax.dynamic_slice_in_dim(observed, first, span, 0)
@@ -129,7 +135,7 @@
         )
         new_v = jnp.concatenate([arrived_v, product(filt_v, power)], axis=0)
         filt_b = filter_apply(arrived_b, power, filt_u, filt_v, filt_b)
-        filt_u, filt_v = new_u, new_v
+        filt_u, filt_v, filt_b = lax.optimization_barrier((new_u, new_v, filt_b))
 
         stored.append((smooth_u, smooth_v))
         packed = shifted(jnp.concatenate([smooth_u, smooth_v], axis=0), -distance, segments)
@@ -139,7 +145,7 @@
             [product(arrived_u, power) + product(transposed(arrived_u, smooth_v), smooth_u), smooth_u], axis=0
         )
         new_v = jnp.concatenate([arrived_v, transposed(smooth_v, power)], axis=0)
-        smooth_u, smooth_v = new_u, new_v
+        smooth_u, smooth_v = lax.optimization_barrier((new_u, new_v))
         level += 1
     stored.append((smooth_u, smooth_v))
     power = powers[level]

time: 460 us -> 344 us (0.75)
  the two profiles are of different devices: /device:TPU:16 before, /device:TPU:232 now
where the time goes in v4:
time: 344 us; the launch traced here: 339 us
  matrix products  122 us (35%)
  waiting for transfers between devices  102 us (30%)
  starting transfers between devices  86.1 us (25%)
  blocking collectives  10.6 us (3%)
  local copies, waits for them, and re-layouts  9.45 us (3%)
  between operations  4.7 us (1%)
  other arithmetic  4.37 us (1%)
    ppermute x26, waiting for transfers between devices, shifted(): return lax.ppermute(block, AXES, route)  100 us
    ppermute x26, starting transfers between devices, shifted(): return lax.ppermute(block, AXES, route)  81.6 us
    dot_general x81, matrix products, product(): jnp.dot(left, right, precision=lax.Precision.HIGHEST, preferred_element_t...  65.4 us
    dot_general x79, matrix products, transposed(): lax.dot_general(left, right, (((1,), (1,)), ((), ())), precision=lax.Prec...  54.5 us
    all_to_all x1, blocking collectives, per_device(): lax.all_to_all(both, 'state', split_axis=2, concat_axis=1, tiled=True)  10.6 us
  transfers between devices with their start and end apart: 29, of which 18 were waited for; matrix products, arithmetic and copies ran while one was open for 17% of the time, Pallas kernels for 0%

profile of v4, /device:TPU:232, one launch (start us, length us, event | category | flops | bytes accessed | tf_op | source)
XLA Modules:
  0.0 339.4 jit_solution(8622516401337828239)
XLA Ops:
  0.6 2.8 collective-permute-start.2
  10.3 2.8 multiply_reduce_fusion
  15.1 1.4 convert_element_type.46
  16.5 2.1 collective-permute-done
  32.8 14.1 %fusion.205 = f32[512,512]{1,0:T(8,128)S(1)} fusion(f32[512,512]{1,0:T(8,128)S(1)} %bitcast.359), kind=kOutput, calls=%fused_computation.350 | convolution fusion | flops 1610612736 | bytes 2097152 | tf_op jit(solution)/shard_map/dot_general | solution.py:10
  47.0 1.8 fusion.206
  48.8 1.8 fusion.208
  53.2 1.9 collective-permute-start.3
  55.1 1.8 fusion.213
  57.0 1.8 fusion.218
  59.8 1.8 fusion.223
  61.7 1.8 fusion.228
  63.5 2.8 fusion.230
  69.3 5.9 %collective-permute-start.15 = (f32[8,512]{1,0:T(8,128)S(1)}, f32[8,512]{1,0:T(8,128)S(1)}, u32[]{:S(2)}, u32[]{:S(2)}) collective-permute-start(f32[8,512]{1,0:T(8,128)S(1)} %concatenate.130), channel_id=1, source_target_pairs={{1,0},{2,1},{3,2},{4,3},{5,4},{6,5},{7,6},{8,7},{9,8},{10,9},{11,1... | collective-permute-start | bytes 49160 | tf_op jit(solution)/shard_map/ppermute | solution.py:35
  75.2 2.2 fusion.242
  78.4 2.3 fusion.246
  80.7 2.5 collective-permute-start.17
  85.1 2.3 fusion.65
  89.0 5.3 %collective-permute-start.4 = (f32[24,512]{1,0:T(8,128)S(1)}, f32[24,512]{1,0:T(8,128)S(1)}, u32[]{:S(2)}, u32[]{:S(2)}) collective-permute-start(f32[24,512]{1,0:T(8,128)S(1)} %pad_maximum_fusion.26), channel_id=1, source_target_pairs={{0,2},{1,3},{2,4},{3,5},{4,6},{5,7},{6,8},{7,9},{8,10},{9,11},{10,... | collective-permute-start | bytes 147464 | tf_op jit(solution)/shard_map/ppermute | solution.py:35
  96.2 1.9 collective-permute-start.19
  102.6 2.5 collective-permute-start.5
  107.3 2.9 collective-permute-start.21
  114.1 5.2 %collective-permute-start.6 = (f32[72,512]{1,0:T(8,128)S(1)}, f32[72,512]{1,0:T(8,128)S(1)}, u32[]{:S(2)}, u32[]{:S(2)}) collective-permute-start(f32[72,512]{1,0:T(8,128)S(1)} %pad_maximum_fusion.13), channel_id=1, source_target_pairs={{0,8},{1,9},{2,10},{3,11},{4,12},{5,13},{6,14},{7,15},{8,16},{9,17... | collective-permute-start | bytes 442376 | tf_op jit(solution)/shard_map/ppermute | solution.py:35
  126.9 3.6 %collective-permute-start.7 = (f32[136,512]{1,0:T(8,128)S(1)}, f32[136,512]{1,0:T(8,128)S(1)}, u32[]{:S(2)}, u32[]{:S(2)}) collective-permute-start(f32[136,512]{1,0:T(8,128)S(1)} %pad_maximum_fusion.7), channel_id=1, source_target_pairs={{0,16},{1,17},{2,18},{3,19},{4,20},{5,21},{6,22},{7,23},{8,24},{9,... | collective-permute-start | bytes 835592 | tf_op jit(solution)/shard_map/ppermute | solution.py:35
  130.5 3.2 collective-permute-start.23
  134.4 10.8 %collective-permute-done.7 = f32[136,512]{1,0:T(8,128)S(1)} collective-permute-done((f32[136,512]{1,0:T(8,128)S(1)}, f32[136,512]{1,0:T(8,128)S(1)}, u32[]{:S(2)}, u32[]{:S(2)}) %collective-permute-start.7) | collective-permute-done | bytes 278560 | tf_op jit(solution)/shard_map/ppermute | solution.py:35
  149.7 4.9 %collective-permute-start.8 = (f32[264,512]{1,0:T(8,128)S(1)}, f32[264,512]{1,0:T(8,128)S(1)}, u32[]{:S(2)}, u32[]{:S(2)}) collective-permute-start(f32[264,512]{1,0:T(8,128)S(1)} %pad_maximum_fusion.1), channel_id=1, source_target_pairs={{0,32},{1,33},{2,34},{3,35},{4,36},{5,37},{6,38},{7,39},{8,40},{9,... | collective-permute-start | bytes 1622024 | tf_op jit(solution)/shard_map/ppermute | solution.py:35
  156.0 23.6 %collective-permute-done.8 = f32[264,512]{1,0:T(8,128)S(1)} collective-permute-done((f32[264,512]{1,0:T(8,128)S(1)}, f32[264,512]{1,0:T(8,128)S(1)}, u32[]{:S(2)}, u32[]{:S(2)}) %collective-permute-start.8) | collective-permute-done | bytes 540704 | tf_op jit(solution)/shard_map/ppermute | solution.py:35
  180.8 1.2 convolution_add_fusion.1
  183.6 4.5 %collective-permute-start.9 = (f32[4,512]{1,0:T(4,128)S(1)}, f32[4,512]{1,0:T(4,128)S(1)}, u32[]{:S(2)}, u32[]{:S(2)}) collective-permute-start(f32[4,512]{1,0:T(4,128)S(1)} %fusion.50), channel_id=1, source_target_pairs={{0,64},{1,65},{2,66},{3,67},{4,68},{5,69},{6,70},{7,71},{8,72},{9,... | collective-permute-start | bytes 24584 | tf_op jit(solution)/shard_map/ppermute | solution.py:35
  191.3 4.2 %collective-permute-start.10 = (f32[4,512]{1,0:T(4,128)S(1)}, f32[4,512]{1,0:T(4,128)S(1)}, u32[]{:S(2)}, u32[]{:S(2)}) collective-permute-start(f32[4,512]{1,0:T(4,128)S(1)} %fusion.48), channel_id=1, source_target_pairs={{0,64},{1,65},{2,66},{3,67},{4,68},{5,69},{6,70},{7,71},{8,72},{9,... | collective-permute-start | bytes 24584 | tf_op jit(solution)/shard_map/ppermute | solution.py:35
  198.7 4.2 %collective-permute-start.11 = (f32[4,512]{1,0:T(4,128)S(1)}, f32[4,512]{1,0:T(4,128)S(1)}, u32[]{:S(2)}, u32[]{:S(2)}) collective-permute-start(f32[4,512]{1,0:T(4,128)S(1)} %fusion.45), channel_id=1, source_target_pairs={{0,64},{1,65},{2,66},{3,67},{4,68},{5,69},{6,70},{7,71},{8,72},{9,... | collective-permute-start | bytes 24584 | tf_op jit(solution)/shard_map/ppermute | solution.py:35
  203.0 1.3 collective-permute-done.11
  206.1 3.0 collective-permute-start.12
  209.2 4.0 %collective-permute-done.12 = f32[4,512]{1,0:T(4,128)S(1)} collective-permute-done((f32[4,512]{1,0:T(4,128)S(1)}, f32[4,512]{1,0:T(4,128)S(1)}, u32[]{:S(2)}, u32[]{:S(2)}) %collective-permute-start.12) | collective-permute-done | bytes 8224 | tf_op jit(solution)/shard_map/ppermute | solution.py:35
  218.8 1.2 fusion.36
  220.0 1.3 fusion.34
  221.3 1.2 fusion.32
  222.5 1.2 fusion.30
  223.7 1.9 collective-permute-start.13
  226.8 2.4 collective-permute-done.13
  230.2 1.9 collective-permute-start.14
  232.1 4.3 %collective-permute-start.25 = (f32[256,512]{1,0:T(8,128)S(1)}, f32[256,512]{1,0:T(8,128)S(1)}, u32[]{:S(2)}, u32[]{:S(2)}) collective-permute-start(f32[256,512]{1,0:T(8,128)S(1)} %pad_maximum_fusion.4), channel_id=1, source_target_pairs={{32,0},{33,1},{34,2},{35,3},{36,4},{37,5},{38,6},{39,7},{40,8},{41... | collective-permute-start | bytes 1572872 | tf_op jit(solution)/shard_map/ppermute | solution.py:35
  238.1 2.7 collective-permute-start.16
  240.9 15.3 %collective-permute-done.25 = f32[256,512]{1,0:T(8,128)S(1)} collective-permute-done((f32[256,512]{1,0:T(8,128)S(1)}, f32[256,512]{1,0:T(8,128)S(1)}, u32[]{:S(2)}, u32[]{:S(2)}) %collective-permute-start.25) | collective-permute-done | bytes 524320 | tf_op jit(solution)/shard_map/ppermute | solution.py:35
  257.5 1.9 collective-permute-start.18
  259.8 13.7 %collective-permute-done.18 = f32[4,512]{1,0:T(4,128)S(1)} collective-permute-done((f32[4,512]{1,0:T(4,128)S(1)}, f32[4,512]{1,0:T(4,128)S(1)}, u32[]{:S(2)}, u32[]{:S(2)}) %collective-permute-start.18) | collective-permute-done | bytes 8224 | tf_op jit(solution)/shard_map/ppermute | solution.py:35
  274.4 2.4 collective-permute-start.20
  277.6 5.4 %collective-permute-done.20 = f32[4,512]{1,0:T(4,128)S(1)} collective-permute-done((f32[4,512]{1,0:T(4,128)S(1)}, f32[4,512]{1,0:T(4,128)S(1)}, u32[]{:S(2)}, u32[]{:S(2)}) %collective-permute-start.20) | collective-permute-done | bytes 8224 | tf_op jit(solution)/shard_map/ppermute | solution.py:35
  284.0 2.9 collective-permute-start.22
  287.0 7.3 %collective-permute-done.22 = f32[4,512]{1,0:T(4,128)S(1)} collective-permute-done((f32[4,512]{1,0:T(4,128)S(1)}, f32[4,512]{1,0:T(4,128)S(1)}, u32[]{:S(2)}, u32[]{:S(2)}) %collective-permute-start.22) | collective-permute-done | bytes 8224 | tf_op jit(solution)/shard_map/ppermute | solution.py:35
  295.5 1.9 collective-permute-start.24
  297.5 3.6 %collective-permute-done.24 = f32[4,512]{1,0:T(4,128)S(1)} collective-permute-done((f32[4,512]{1,0:T(4,128)S(1)}, f32[4,512]{1,0:T(4,128)S(1)}, u32[]{:S(2)}, u32[]{:S(2)}) %collective-permute-start.24) | collective-permute-done | bytes 8224 | tf_op jit(solution)/shard_map/ppermute | solution.py:35
  302.6 1.9 collective-permute-start.26
  304.5 3.6 %collective-permute-done.26 = f32[4,512]{1,0:T(4,128)S(1)} collective-permute-done((f32[4,512]{1,0:T(4,128)S(1)}, f32[4,512]{1,0:T(4,128)S(1)}, u32[]{:S(2)}, u32[]{:S(2)}) %collective-permute-start.26) | collective-permute-done | bytes 8224 | tf_op jit(solution)/shard_map/ppermute | solution.py:35
  309.6 1.9 collective-permute-start.27
  311.5 3.6 %collective-permute-done.27 = f32[4,512]{1,0:T(4,128)S(1)} collective-permute-done((f32[4,512]{1,0:T(4,128)S(1)}, f32[4,512]{1,0:T(4,128)S(1)}, u32[]{:S(2)}, u32[]{:S(2)}) %collective-permute-start.27) | collective-permute-done | bytes 8224 | tf_op jit(solution)/shard_map/ppermute | solution.py:35
  316.6 1.9 collective-permute-start.28
  318.6 3.6 %collective-permute-done.28 = f32[4,512]{1,0:T(4,128)S(1)} collective-permute-done((f32[4,512]{1,0:T(4,128)S(1)}, f32[4,512]{1,0:T(4,128)S(1)}, u32[]{:S(2)}, u32[]{:S(2)}) %collective-permute-start.28) | collective-permute-done | bytes 8224 | tf_op jit(solution)/shard_map/ppermute | solution.py:35
  322.2 1.2 fusion.10
  323.4 1.3 fusion.8
  324.7 1.2 fusion.6
  325.9 1.2 fusion.4
  327.2 10.6 %all_to_all.15 = f32[2,4,4,512]{3,1,0,2:T(4,128)S(1)} all-to-all(f32[2,4,4,512]{3,1,0,2:T(4,128)S(1)} %copy.10), channel_id=1, replica_groups=mesh['tm'=64,'state'=4] {'state'}, dimensions={2} | all-to-all | bytes 131072 | tf_op jit(solution)/shard_map/all_to_all | solution.py:198
  (290 shorter events, 89.4 us)
Async XLA Ops:
  0.6 7.6 %copy-start = (f32[16,4]{0,1:T(4,128)S(1)}, f32[16,4]{0,1:T(4,128)}, u32[]{:S(2)}) copy-start(f32[16,4]{0,1:T(4,128)} %param.9) | copy-start | bytes 772
  0.6 15.9 %collective-permute-start.2 = (f32[128,512]{1,0:T(8,128)}, f32[128,512]{1,0:T(8,128)S(1)}, u32[]{:S(2)}, u32[]{:S(2)}) collective-permute-start(f32[128,512]{1,0:T(8,128)} %param.6), channel_id=1, source_target_pairs={{0,3},{1,0},{2,1},{3,2},{4,7},{5,4},{6,5},{7,6},{8,11},{9,8},{10,9... | collective-permute-start | bytes 786440 | tf_op jit(solution)/shard_map/ppermute | solution.py:64
  3.5 13.0 %collective-permute-start.1 = (f32[128,512]{1,0:T(8,128)}, f32[128,512]{1,0:T(8,128)S(1)}, u32[]{:S(2)}, u32[]{:S(2)}) collective-permute-start(f32[128,512]{1,0:T(8,128)} %param.6), channel_id=1, source_target_pairs={{0,2},{1,3},{2,0},{3,1},{4,6},{5,7},{6,4},{7,5},{8,10},{9,11},{10,... | collective-permute-start | bytes 786440 | tf_op jit(solution)/shard_map/ppermute | solution.py:64
  4.3 14.3 %collective-permute-start = (f32[128,512]{1,0:T(8,128)}, f32[128,512]{1,0:T(8,128)S(1)}, u32[]{:S(2)}, u32[]{:S(2)}) collective-permute-start(f32[128,512]{1,0:T(8,128)} %param.6), channel_id=1, source_target_pairs={{0,1},{1,2},{2,3},{3,0},{4,5},{5,6},{6,7},{7,4},{8,9},{9,10},{10,1... | collective-permute-start | bytes 786440 | tf_op jit(solution)/shard_map/ppermute | solution.py:64
  5.2 0.7 copy-start.19
  5.9 0.7 copy-start.20
  7.5 0.7 copy-start.18
  15.1 3.5 %copy-start.16 = (f32[128,512]{1,0:T(8,128)S(1)}, f32[128,512]{1,0:T(8,128)}, u32[]{:S(2)}) copy-start(f32[128,512]{1,0:T(8,128)} %param.6) | copy-start | bytes 786436
  25.0 0.7 copy-start.17
  30.5 2.0 copy-start.13
  48.8 3.7 %copy-start.7 = (f32[512,512]{1,0:T(8,128)}, f32[512,512]{1,0:T(8,128)S(1)}, u32[]{:S(2)}) copy-start(f32[512,512]{1,0:T(8,128)S(1)} %fusion.206) | copy-start | bytes 3145732
  50.7 4.4 %copy-start.5 = (f32[512,512]{1,0:T(8,128)}, f32[512,512]{1,0:T(8,128)S(1)}, u32[]{:S(2)}) copy-start(f32[512,512]{1,0:T(8,128)S(1)} %fusion.208) | copy-start | bytes 3145732
  53.2 30.0 %collective-permute-start.3 = (f32[16,512]{1,0:T(8,128)S(1)}, f32[16,512]{1,0:T(8,128)S(1)}, u32[]{:S(2)}, u32[]{:S(2)}) collective-permute-start(f32[16,512]{1,0:T(8,128)S(1)} %concatenate.112), channel_id=1, source_target_pairs={{0,1},{1,2},{2,3},{3,4},{4,5},{5,6},{6,7},{7,8},{8,9},{9,10},{10,1... | collective-permute-start | bytes 98312 | tf_op jit(solution)/shard_map/ppermute | solution.py:35
  57.0 1.9 copy-start.3
  58.9 1.0 copy-start.1
  69.3 8.4 %copy-start.8 = (f32[512,512]{1,0:T(8,128)S(1)}, f32[512,512]{1,0:T(8,128)}, u32[]{:S(2)}) copy-start(f32[512,512]{1,0:T(8,128)} %copy-done.7) | copy-start | bytes 3145732
  69.3 8.1 %collective-permute-start.15 = (f32[8,512]{1,0:T(8,128)S(1)}, f32[8,512]{1,0:T(8,128)S(1)}, u32[]{:S(2)}, u32[]{:S(2)}) collective-permute-start(f32[8,512]{1,0:T(8,128)S(1)} %concatenate.130), channel_id=1, source_target_pairs={{1,0},{2,1},{3,2},{4,3},{5,4},{6,5},{7,6},{8,7},{9,8},{10,9},{11,1... | collective-permute-start | bytes 49160 | tf_op jit(solution)/shard_map/ppermute | solution.py:35
  78.4 5.4 %copy-start.9 = (f32[512,512]{1,0:T(8,128)S(1)}, f32[512,512]{1,0:T(8,128)}, u32[]{:S(2)}) copy-start(f32[512,512]{1,0:T(8,128)} %copy-done.7) | copy-start | bytes 3145732
  80.7 13.6 %collective-permute-start.17 = (f32[16,512]{1,0:T(8,128)S(1)}, f32[16,512]{1,0:T(8,128)S(1)}, u32[]{:S(2)}, u32[]{:S(2)}) collective-permute-start(f32[16,512]{1,0:T(8,128)S(1)} %pad_maximum_fusion.30), channel_id=1, source_target_pairs={{2,0},{3,1},{4,2},{5,3},{6,4},{7,5},{8,6},{9,7},{10,8},{11,9},{12,... | collective-permute-start | bytes 98312 | tf_op jit(solution)/shard_map/ppermute | solution.py:35
  84.8 2.6 copy-start.6
  85.1 2.9 copy-start.10
  88.0 7.2 %copy-start.4 = (f32[512,512]{1,0:T(8,128)S(1)}, f32[512,512]{1,0:T(8,128)}, u32[]{:S(2)}) copy-start(f32[512,512]{1,0:T(8,128)} %copy-done.3) | copy-start | bytes 3145732
  89.0 9.2 %collective-permute-start.4 = (f32[24,512]{1,0:T(8,128)S(1)}, f32[24,512]{1,0:T(8,128)S(1)}, u32[]{:S(2)}, u32[]{:S(2)}) collective-permute-start(f32[24,512]{1,0:T(8,128)S(1)} %pad_maximum_fusion.26), channel_id=1, source_target_pairs={{0,2},{1,3},{2,4},{3,5},{4,6},{5,7},{6,8},{7,9},{8,10},{9,11},{10,... | collective-permute-start | bytes 147464 | tf_op jit(solution)/shard_map/ppermute | solution.py:35
  96.2 9.0 %collective-permute-start.19 = (f32[32,512]{1,0:T(8,128)S(1)}, f32[32,512]{1,0:T(8,128)S(1)}, u32[]{:S(2)}, u32[]{:S(2)}) collective-permute-start(f32[32,512]{1,0:T(8,128)S(1)} %pad_maximum_fusion.22), channel_id=1, source_target_pairs={{4,0},{5,1},{6,2},{7,3},{8,4},{9,5},{10,6},{11,7},{12,8},{13,9},{1... | collective-permute-start | bytes 196616 | tf_op jit(solution)/shard_map/ppermute | solution.py:35
  102.6 3.6 %copy-start.2 = (f32[512,512]{1,0:T(8,128)S(1)}, f32[512,512]{1,0:T(8,128)}, u32[]{:S(2)}) copy-start(f32[512,512]{1,0:T(8,128)} %copy-done.1) | copy-start | bytes 3145732
  102.6 7.6 %collective-permute-start.5 = (f32[40,512]{1,0:T(8,128)S(1)}, f32[40,512]{1,0:T(8,128)S(1)}, u32[]{:S(2)}, u32[]{:S(2)}) collective-permute-start(f32[40,512]{1,0:T(8,128)S(1)} %pad_maximum_fusion.19), channel_id=1, source_target_pairs={{0,4},{1,5},{2,6},{3,7},{4,8},{5,9},{6,10},{7,11},{8,12},{9,13},{1... | collective-permute-start | bytes 245768 | tf_op jit(solution)/shard_map/ppermute | solution.py:35
  107.3 12.8 %collective-permute-start.21 = (f32[64,512]{1,0:T(8,128)S(1)}, f32[64,512]{1,0:T(8,128)S(1)}, u32[]{:S(2)}, u32[]{:S(2)}) collective-permute-start(f32[64,512]{1,0:T(8,128)S(1)} %pad_maximum_fusion.16), channel_id=1, source_target_pairs={{8,0},{9,1},{10,2},{11,3},{12,4},{13,5},{14,6},{15,7},{16,8},{17,9... | collective-permute-start | bytes 393224 | tf_op jit(solution)/shard_map/ppermute | solution.py:35
  114.1 8.6 %collective-permute-start.6 = (f32[72,512]{1,0:T(8,128)S(1)}, f32[72,512]{1,0:T(8,128)S(1)}, u32[]{:S(2)}, u32[]{:S(2)}) collective-permute-start(f32[72,512]{1,0:T(8,128)S(1)} %pad_maximum_fusion.13), channel_id=1, source_target_pairs={{0,8},{1,9},{2,10},{3,11},{4,12},{5,13},{6,14},{7,15},{8,16},{9,17... | collective-permute-start | bytes 442376 | tf_op jit(solution)/shard_map/ppermute | solution.py:35
  126.9 18.3 %collective-permute-start.7 = (f32[136,512]{1,0:T(8,128)S(1)}, f32[136,512]{1,0:T(8,128)S(1)}, u32[]{:S(2)}, u32[]{:S(2)}) collective-permute-start(f32[136,512]{1,0:T(8,128)S(1)} %pad_maximum_fusion.7), channel_id=1, source_target_pairs={{0,16},{1,17},{2,18},{3,19},{4,20},{5,21},{6,22},{7,23},{8,24},{9,... | collective-permute-start | bytes 835592 | tf_op jit(solution)/shard_map/ppermute | solution.py:35
  130.5 24.2 %collective-permute-start.23 = (f32[128,512]{1,0:T(8,128)S(1)}, f32[128,512]{1,0:T(8,128)S(1)}, u32[]{:S(2)}, u32[]{:S(2)}) collective-permute-start(f32[128,512]{1,0:T(8,128)S(1)} %pad_maximum_fusion.10), channel_id=1, source_target_pairs={{16,0},{17,1},{18,2},{19,3},{20,4},{21,5},{22,6},{23,7},{24,8},{25... | collective-permute-start | bytes 786440 | tf_op jit(solution)/shard_map/ppermute | solution.py:35
  149.7 29.8 %collective-permute-start.8 = (f32[264,512]{1,0:T(8,128)S(1)}, f32[264,512]{1,0:T(8,128)S(1)}, u32[]{:S(2)}, u32[]{:S(2)}) collective-permute-start(f32[264,512]{1,0:T(8,128)S(1)} %pad_maximum_fusion.1), channel_id=1, source_target_pairs={{0,32},{1,33},{2,34},{3,35},{4,36},{5,37},{6,38},{7,39},{8,40},{9,... | collective-permute-start | bytes 1622024 | tf_op jit(solution)/shard_map/ppermute | solution.py:35
  154.7 48.3 %copy-start.15 = (f32[128,512]{1,0:T(8,128)}, f32[128,512]{1,0:T(8,128)S(1)}, u32[]{:S(2)}) copy-start(f32[128,512]{1,0:T(8,128)S(1)} %collective-permute-done.23) | copy-start | bytes 786436
  183.6 5.9 %collective-permute-start.9 = (f32[4,512]{1,0:T(4,128)S(1)}, f32[4,512]{1,0:T(4,128)S(1)}, u32[]{:S(2)}, u32[]{:S(2)}) collective-permute-start(f32[4,512]{1,0:T(4,128)S(1)} %fusion.50), channel_id=1, source_target_pairs={{0,64},{1,65},{2,66},{3,67},{4,68},{5,69},{6,70},{7,71},{8,72},{9,... | collective-permute-start | bytes 24584 | tf_op jit(solution)/shard_map/ppermute | solution.py:35
  189.1 1.2 copy-start.11
  191.3 5.6 %collective-permute-start.10 = (f32[4,512]{1,0:T(4,128)S(1)}, f32[4,512]{1,0:T(4,128)S(1)}, u32[]{:S(2)}, u32[]{:S(2)}) collective-permute-start(f32[4,512]{1,0:T(4,128)S(1)} %fusion.48), channel_id=1, source_target_pairs={{0,64},{1,65},{2,66},{3,67},{4,68},{5,69},{6,70},{7,71},{8,72},{9,... | collective-permute-start | bytes 24584 | tf_op jit(solution)/shard_map/ppermute | solution.py:35
  198.7 5.6 %collective-permute-start.11 = (f32[4,512]{1,0:T(4,128)S(1)}, f32[4,512]{1,0:T(4,128)S(1)}, u32[]{:S(2)}, u32[]{:S(2)}) collective-permute-start(f32[4,512]{1,0:T(4,128)S(1)} %fusion.45), channel_id=1, source_target_pairs={{0,64},{1,65},{2,66},{3,67},{4,68},{5,69},{6,70},{7,71},{8,72},{9,... | collective-permute-start | bytes 24584 | tf_op jit(solution)/shard_map/ppermute | solution.py:35
  205.2 4.0 %slice-start.1 = ((f32[128,512]{1,0:T(8,128)}), f32[64,512]{1,0:T(8,128)S(1)}, s32[]{:S(2)}) async-start(f32[128,512]{1,0:T(8,128)} %copy-done.15), calls=%async_computation.2 | async-start | bytes 262144 | tf_op jit(solution)/shard_map/slice | solution.py:143
  206.1 7.1 %collective-permute-start.12 = (f32[4,512]{1,0:T(4,128)S(1)}, f32[4,512]{1,0:T(4,128)S(1)}, u32[]{:S(2)}, u32[]{:S(2)}) collective-permute-start(f32[4,512]{1,0:T(4,128)S(1)} %fusion.43), channel_id=1, source_target_pairs={{0,1},{1,2},{2,3},{3,4},{4,5},{5,6},{6,7},{7,8},{8,9},{9,10},{10,1... | collective-permute-start | bytes 24584 | tf_op jit(solution)/shard_map/ppermute | solution.py:35
  223.7 5.5 %collective-permute-start.13 = (f32[4,512]{1,0:T(4,128)S(1)}, f32[4,512]{1,0:T(4,128)S(1)}, u32[]{:S(2)}, u32[]{:S(2)}) collective-permute-start(f32[4,512]{1,0:T(4,128)S(1)} %fusion.30), channel_id=1, source_target_pairs={{1,0},{2,1},{3,2},{4,3},{5,4},{6,5},{7,6},{8,7},{9,8},{10,9},{11,1... | collective-permute-start | bytes 24584 | tf_op jit(solution)/shard_map/ppermute | solution.py:35
  230.2 7.0 %collective-permute-start.14 = (f32[4,512]{1,0:T(4,128)S(1)}, f32[4,512]{1,0:T(4,128)S(1)}, u32[]{:S(2)}, u32[]{:S(2)}) collective-permute-start(f32[4,512]{1,0:T(4,128)S(1)} %fusion.28), channel_id=1, source_target_pairs={{2,0},{3,1},{4,2},{5,3},{6,4},{7,5},{8,6},{9,7},{10,8},{11,9},{12,... | collective-permute-start | bytes 24584 | tf_op jit(solution)/shard_map/ppermute | solution.py:35
  232.1 24.1 %collective-permute-start.25 = (f32[256,512]{1,0:T(8,128)S(1)}, f32[256,512]{1,0:T(8,128)S(1)}, u32[]{:S(2)}, u32[]{:S(2)}) collective-permute-start(f32[256,512]{1,0:T(8,128)S(1)} %pad_maximum_fusion.4), channel_id=1, source_target_pairs={{32,0},{33,1},{34,2},{35,3},{36,4},{37,5},{38,6},{39,7},{40,8},{41... | collective-permute-start | bytes 1572872 | tf_op jit(solution)/shard_map/ppermute | solution.py:35
  238.1 18.5 %collective-permute-start.16 = (f32[4,512]{1,0:T(4,128)S(1)}, f32[4,512]{1,0:T(4,128)S(1)}, u32[]{:S(2)}, u32[]{:S(2)}) collective-permute-start(f32[4,512]{1,0:T(4,128)S(1)} %fusion.26), channel_id=1, source_target_pairs={{4,0},{5,1},{6,2},{7,3},{8,4},{9,5},{10,6},{11,7},{12,8},{13,9},{1... | collective-permute-start | bytes 24584 | tf_op jit(solution)/shard_map/ppermute | solution.py:35
  256.2 30.8 %copy-start.14 = (f32[256,512]{1,0:T(8,128)}, f32[256,512]{1,0:T(8,128)S(1)}, u32[]{:S(2)}) copy-start(f32[256,512]{1,0:T(8,128)S(1)} %collective-permute-done.25) | copy-start | bytes 1572868
  257.5 16.0 %collective-permute-start.18 = (f32[4,512]{1,0:T(4,128)S(1)}, f32[4,512]{1,0:T(4,128)S(1)}, u32[]{:S(2)}, u32[]{:S(2)}) collective-permute-start(f32[4,512]{1,0:T(4,128)S(1)} %fusion.24), channel_id=1, source_target_pairs={{8,0},{9,1},{10,2},{11,3},{12,4},{13,5},{14,6},{15,7},{16,8},{17,9... | collective-permute-start | bytes 24584 | tf_op jit(solution)/shard_map/ppermute | solution.py:35
  274.4 8.6 %collective-permute-start.20 = (f32[4,512]{1,0:T(4,128)S(1)}, f32[4,512]{1,0:T(4,128)S(1)}, u32[]{:S(2)}, u32[]{:S(2)}) collective-permute-start(f32[4,512]{1,0:T(4,128)S(1)} %fusion.22), channel_id=1, source_target_pairs={{16,0},{17,1},{18,2},{19,3},{20,4},{21,5},{22,6},{23,7},{24,8},{25... | collective-permute-start | bytes 24584 | tf_op jit(solution)/shard_map/ppermute | solution.py:35
  284.0 10.3 %collective-permute-start.22 = (f32[4,512]{1,0:T(4,128)S(1)}, f32[4,512]{1,0:T(4,128)S(1)}, u32[]{:S(2)}, u32[]{:S(2)}) collective-permute-start(f32[4,512]{1,0:T(4,128)S(1)} %fusion.20), channel_id=1, source_target_pairs={{32,0},{33,1},{34,2},{35,3},{36,4},{37,5},{38,6},{39,7},{40,8},{41... | collective-permute-start | bytes 24584 | tf_op jit(solution)/shard_map/ppermute | solution.py:35
  294.9 2.5 slice-start
  295.5 5.5 %collective-permute-start.24 = (f32[4,512]{1,0:T(4,128)S(1)}, f32[4,512]{1,0:T(4,128)S(1)}, u32[]{:S(2)}, u32[]{:S(2)}) collective-permute-start(f32[4,512]{1,0:T(4,128)S(1)} %fusion.18), channel_id=1, source_target_pairs={{64,0},{65,1},{66,2},{67,3},{68,4},{69,5},{70,6},{71,7},{72,8},{73... | collective-permute-start | bytes 24584 | tf_op jit(solution)/shard_map/ppermute | solution.py:35
  302.6 5.5 %collective-permute-start.26 = (f32[4,512]{1,0:T(4,128)S(1)}, f32[4,512]{1,0:T(4,128)S(1)}, u32[]{:S(2)}, u32[]{:S(2)}) collective-permute-start(f32[4,512]{1,0:T(4,128)S(1)} %fusion.16), channel_id=1, source_target_pairs={{64,0},{65,1},{66,2},{67,3},{68,4},{69,5},{70,6},{71,7},{72,8},{73... | collective-permute-start | bytes 24584 | tf_op jit(solution)/shard_map/ppermute | solution.py:35
  309.0 7.0 %copy-start.12 = (f32[512,512]{1,0:T(8,128)S(1)}, f32[512,512]{1,0:T(8,128)}, u32[]{:S(2)}) copy-start(f32[512,512]{1,0:T(8,128)} %fusion.230) | copy-start | bytes 3145732
  309.6 5.5 %collective-permute-start.27 = (f32[4,512]{1,0:T(4,128)S(1)}, f32[4,512]{1,0:T(4,128)S(1)}, u32[]{:S(2)}, u32[]{:S(2)}) collective-permute-start(f32[4,512]{1,0:T(4,128)S(1)} %fusion.14), channel_id=1, source_target_pairs={{64,0},{65,1},{66,2},{67,3},{68,4},{69,5},{70,6},{71,7},{72,8},{73... | collective-permute-start | bytes 24584 | tf_op jit(solution)/shard_map/ppermute | solution.py:35
  316.6 5.5 %collective-permute-start.28 = (f32[4,512]{1,0:T(4,128)S(1)}, f32[4,512]{1,0:T(4,128)S(1)}, u32[]{:S(2)}, u32[]{:S(2)}) collective-permute-start(f32[4,512]{1,0:T(4,128)S(1)} %fusion.12), channel_id=1, source_target_pairs={{1,0},{2,1},{3,2},{4,3},{5,4},{6,5},{7,6},{8,7},{9,8},{10,9},{11,1... | collective-permute-start | bytes 24584 | tf_op jit(solution)/shard_map/ppermute | solution.py:35

commit v5 on v4

--- a/solution.py
+++ b/solution.py
@@ -30,8 +30,25 @@
     )
 
 
+PLACEMENTS = {256: (4, 1, 7, 6, 0, 2, 3, 5), 16: (2, 0, 3, 1)}
+
+
+def placement(total):
+    bits = PLACEMENTS.get(total)
+    if bits is None:
+        return list(range(total))
+    order = []
+    for seg in range(total):
+        device = 0
+        for place, bit in enumerate(bits):
+            device |= ((seg >> place) & 1) << bit
+        order.append(device)
+    return order
+
+
 def shifted(block, distance, total):
-    route = [(i, i + distance) for i in range(total) if 0 <= i + distance < total]
+    order = placement(total)
+    route = [(order[i], order[i + distance]) for i in range(total) if 0 <= i + distance < total]
     return lax.ppermute(block, AXES, route)
 
 
@@ -51,7 +68,11 @@
     members = lax.axis_size("state")
     segments = lax.axis_size("tm") * members
     member = lax.axis_index("state")
-    segment = lax.axis_index(AXES)
+    order = placement(segments)
+    owner = [0] * segments
+    for seg, device in enumerate(order):
+        owner[device] = seg
+    segment = jnp.asarray(owner, jnp.int32)[lax.axis_index(AXES)]
     span = observed.shape[0] // members
     steps_total = span * segments
     last = span - 1
@@ -62,14 +83,19 @@
     for step in range(1, members):
         route = [(i, (i + step) % members) for i in range(members)]
         pieces.append(lax.ppermute(dynamics, "state", route))
-    order = (member - jnp.arange(members, dtype=jnp.int32)) % members
-    gathered = jnp.take(jnp.stack(pieces), order, axis=0).reshape(state_width, state_width)
+    sources = (member - jnp.arange(members, dtype=jnp.int32)) % members
+    gathered = jnp.take(jnp.stack(pieces), sources, axis=0).reshape(state_width, state_width)
     transition = gathered * block_mask
 
     first = member * span
     obs_here = lax.dynamic_slice_in_dim(observed, first, span, 0)
     index_here = lax.dynamic_slice_in_dim(obs_index, first, span, 0)
     noise_here = lax.dynamic_slice_in_dim(obs_noise, first, span, 0)
+    route = [(seg, order[seg]) for seg in range(segments)]
+    floats = lax.ppermute(jnp.concatenate([obs_here, noise_here[:, None]], axis=1), AXES, route)
+    index_here = lax.ppermute(index_here, AXES, route)
+    obs_here = floats[:, :seq_total]
+    noise_here = floats[:, seq_total]
     gains = 1.0 / (1.0 + noise_here)
     state_index = jnp.arange(state_width, dtype=jnp.int32)
     hits = (state_index[None, :] == index_here[:, None]).astype(jnp.float32)
@@ -195,8 +221,18 @@
     smoothed = jnp.stack(smoothed)
 
     both = jnp.stack([filtered, smoothed])
-    both = lax.all_to_all(both, "state", split_axis=2, concat_axis=1, tiled=True)
-    return (both[0], both[1])
+    received = []
+    for turn in range(members):
+        piece = lax.dynamic_index_in_dim(both, (segment % members + turn) % members, axis=2, keepdims=False)
+        route = [
+            (order[seg], (seg // members) * members + (seg % members + turn) % members)
+            for seg in range(segments)
+        ]
+        received.append(lax.ppermute(piece, AXES, route))
+    picks = (member - jnp.arange(members, dtype=jnp.int32)) % members
+    placed = jnp.take(jnp.stack(received), picks, axis=0)
+    placed = jnp.moveaxis(placed, 1, 0).reshape(2, members * span, 1, state_width)
+    return (placed[0], placed[1])
 
 
 def solution(mesh):

time: 344 us -> 387 us (1.12)
  the two profiles are of different devices: /device:TPU:232 before, /device:TPU:123 now
where the time goes in v5:
time: 387 us; the launch traced here: 382 us
  starting transfers between devices  140 us (36%)
  matrix products  122 us (32%)
  waiting for transfers between devices  81.2 us (21%)
  between operations  24.3 us (6%)
  local copies, waits for them, and re-layouts  10.2 us (3%)
  other arithmetic  4.46 us (1%)
    ppermute x26, starting transfers between devices, shifted(): return lax.ppermute(block, AXES, route)  108 us
    ppermute x26, waiting for transfers between devices, shifted(): return lax.ppermute(block, AXES, route)  74.2 us
    dot_general x81, matrix products, product(): jnp.dot(left, right, precision=lax.Precision.HIGHEST, preferred_element_t...  65.5 us
    dot_general x79, matrix products, transposed(): lax.dot_general(left, right, (((1,), (1,)), ((), ())), precision=lax.Prec...  54.5 us
    ppermute x4, starting transfers between devices, per_device(): received.append(lax.ppermute(piece, AXES, route))  18.7 us
  transfers between devices with their start and end apart: 35, of which 18 were waited for; matrix products, arithmetic and copies ran while one was open for 16% of the time, Pallas kernels for 0%

profile of v5, /device:TPU:123, one launch (start us, length us, event | category | flops | bytes accessed | tf_op | source)
XLA Modules:
  0.0 381.7 jit_solution(4585664431312075414)
XLA Ops:
  1.0 2.1 collective-permute-start.2
  3.1 1.5 collective-permute-start.1
  5.5 7.5 %collective-permute-start = (f32[4,5]{0,1:T(8,128)S(1)}, f32[4,5]{0,1:T(8,128)S(1)}, u32[]{:S(2)}, u32[]{:S(2)}) collective-permute-start(f32[4,5]{0,1:T(8,128)S(1)} %pad_maximum_fusion.37), channel_id=1, source_target_pairs={{0,0},{1,16},{2,2},{3,18},{4,128},{5,144},{6,130},{7,146},{8,64},{... | collective-permute-start | bytes 248 | tf_op jit(solution)/shard_map/ppermute | solution.py:95
  13.1 1.9 collective-permute-start.4
  34.0 1.4 convert_element_type.46
  38.3 2.8 multiply_reduce_fusion
  55.5 1.8 fusion.209
  57.4 14.2 %fusion.210 = f32[512,512]{1,0:T(8,128)S(1)} fusion(f32[512,512]{1,0:T(8,128)S(1)} %fusion.209), kind=kOutput, calls=%fused_computation.370 | convolution fusion | flops 1610612736 | bytes 2097152 | tf_op jit(solution)/shard_map/dot_general | solution.py:10
  71.6 1.8 fusion.212
  76.4 4.6 %collective-permute-start.5 = (f32[16,512]{1,0:T(8,128)S(1)}, f32[16,512]{1,0:T(8,128)S(1)}, u32[]{:S(2)}, u32[]{:S(2)}) collective-permute-start(f32[16,512]{1,0:T(8,128)S(1)} %concatenate.116), channel_id=1, source_target_pairs={{0,16},{16,2},{2,18},{18,128},{128,144},{144,130},{130,146},{146,6... | collective-permute-start | bytes 98312 | tf_op jit(solution)/shard_map/ppermute | solution.py:52
  81.1 1.8 fusion.217
  82.9 1.8 fusion.222
  85.8 1.8 fusion.227
  87.6 1.8 fusion.232
  89.5 2.9 fusion.234
  95.9 2.1 collective-permute-start.17
  98.0 2.2 fusion.246
  100.1 3.7 collective-permute-done.17
  104.9 2.3 fusion.250
  107.1 9.4 %collective-permute-start.19 = (f32[16,512]{1,0:T(8,128)S(1)}, f32[16,512]{1,0:T(8,128)S(1)}, u32[]{:S(2)}, u32[]{:S(2)}) collective-permute-start(f32[16,512]{1,0:T(8,128)S(1)} %pad_maximum_fusion.30), channel_id=1, source_target_pairs={{2,0},{18,16},{128,2},{144,18},{130,128},{146,144},{64,130},{80,14... | collective-permute-start | bytes 98312 | tf_op jit(solution)/shard_map/ppermute | solution.py:52
  118.5 2.3 fusion.63
  122.4 1.9 collective-permute-start.6
  126.2 2.5 collective-permute-start.21
  128.8 2.4 collective-permute-done.6
  135.6 7.6 %collective-permute-start.7 = (f32[40,512]{1,0:T(8,128)S(1)}, f32[40,512]{1,0:T(8,128)S(1)}, u32[]{:S(2)}, u32[]{:S(2)}) collective-permute-start(f32[40,512]{1,0:T(8,128)S(1)} %pad_maximum_fusion.19), channel_id=1, source_target_pairs={{0,128},{16,144},{2,130},{18,146},{128,64},{144,80},{130,66},{146,... | collective-permute-start | bytes 245768 | tf_op jit(solution)/shard_map/ppermute | solution.py:52
  145.3 1.9 collective-permute-start.23
  151.2 8.6 %collective-permute-start.8 = (f32[72,512]{1,0:T(8,128)S(1)}, f32[72,512]{1,0:T(8,128)S(1)}, u32[]{:S(2)}, u32[]{:S(2)}) collective-permute-start(f32[72,512]{1,0:T(8,128)S(1)} %pad_maximum_fusion.13), channel_id=1, source_target_pairs={{0,64},{16,80},{2,66},{18,82},{128,192},{144,208},{130,194},{146,2... | collective-permute-start | bytes 442376 | tf_op jit(solution)/shard_map/ppermute | solution.py:52
  167.0 2.4 collective-permute-start.9
  169.4 2.9 collective-permute-start.25
  173.0 2.3 collective-permute-done.9
  179.8 5.8 %collective-permute-start.10 = (f32[264,512]{1,0:T(8,128)S(1)}, f32[264,512]{1,0:T(8,128)S(1)}, u32[]{:S(2)}, u32[]{:S(2)}) collective-permute-start(f32[264,512]{1,0:T(8,128)S(1)} %pad_maximum_fusion.1), channel_id=1, source_target_pairs={{0,4},{16,20},{2,6},{18,22},{128,132},{144,148},{130,134},{146,150... | collective-permute-start | bytes 1622024 | tf_op jit(solution)/shard_map/ppermute | solution.py:52
  186.9 9.0 %collective-permute-done.10 = f32[264,512]{1,0:T(8,128)S(1)} collective-permute-done((f32[264,512]{1,0:T(8,128)S(1)}, f32[264,512]{1,0:T(8,128)S(1)}, u32[]{:S(2)}, u32[]{:S(2)}) %collective-permute-start.10) | collective-permute-done | bytes 540704 | tf_op jit(solution)/shard_map/ppermute | solution.py:52
  200.0 1.9 collective-permute-start.11
  203.0 1.4 collective-permute-done.11
  206.3 4.9 %collective-permute-start.12 = (f32[4,512]{1,0:T(4,128)S(1)}, f32[4,512]{1,0:T(4,128)S(1)}, u32[]{:S(2)}, u32[]{:S(2)}) collective-permute-start(f32[4,512]{1,0:T(4,128)S(1)} %fusion.46), channel_id=1, source_target_pairs={{0,8},{16,24},{2,10},{18,26},{128,136},{144,152},{130,138},{146,15... | collective-permute-start | bytes 24584 | tf_op jit(solution)/shard_map/ppermute | solution.py:52
  213.8 6.6 %collective-permute-start.13 = (f32[4,512]{1,0:T(4,128)S(1)}, f32[4,512]{1,0:T(4,128)S(1)}, u32[]{:S(2)}, u32[]{:S(2)}) collective-permute-start(f32[4,512]{1,0:T(4,128)S(1)} %fusion.43), channel_id=1, source_target_pairs={{0,8},{16,24},{2,10},{18,26},{128,136},{144,152},{130,138},{146,15... | collective-permute-start | bytes 24584 | tf_op jit(solution)/shard_map/ppermute | solution.py:52
  223.1 2.3 collective-permute-start.14
  225.5 2.9 collective-permute-done.14
  238.9 3.6 collective-permute-start.15
  243.7 2.9 collective-permute-done.15
  247.5 6.2 %collective-permute-start.16 = (f32[4,512]{1,0:T(4,128)S(1)}, f32[4,512]{1,0:T(4,128)S(1)}, u32[]{:S(2)}, u32[]{:S(2)}) collective-permute-start(f32[4,512]{1,0:T(4,128)S(1)} %fusion.26), channel_id=1, source_target_pairs={{2,0},{18,16},{128,2},{144,18},{130,128},{146,144},{64,130},{80,14... | collective-permute-start | bytes 24584 | tf_op jit(solution)/shard_map/ppermute | solution.py:52
  253.8 13.2 %collective-permute-start.27 = (f32[256,512]{1,0:T(8,128)S(1)}, f32[256,512]{1,0:T(8,128)S(1)}, u32[]{:S(2)}, u32[]{:S(2)}) collective-permute-start(f32[256,512]{1,0:T(8,128)S(1)} %pad_maximum_fusion.4), channel_id=1, source_target_pairs={{4,0},{20,16},{6,2},{22,18},{132,128},{148,144},{134,130},{150,146... | collective-permute-start | bytes 1572872 | tf_op jit(solution)/shard_map/ppermute | solution.py:52
  268.0 5.2 %collective-permute-start.18 = (f32[4,512]{1,0:T(4,128)S(1)}, f32[4,512]{1,0:T(4,128)S(1)}, u32[]{:S(2)}, u32[]{:S(2)}) collective-permute-start(f32[4,512]{1,0:T(4,128)S(1)} %fusion.24), channel_id=1, source_target_pairs={{128,0},{144,16},{130,2},{146,18},{64,128},{80,144},{66,130},{82,1... | collective-permute-start | bytes 24584 | tf_op jit(solution)/shard_map/ppermute | solution.py:52
  273.2 5.6 %collective-permute-done.27 = f32[256,512]{1,0:T(8,128)S(1)} collective-permute-done((f32[256,512]{1,0:T(8,128)S(1)}, f32[256,512]{1,0:T(8,128)S(1)}, u32[]{:S(2)}, u32[]{:S(2)}) %collective-permute-start.27) | collective-permute-done | bytes 524320 | tf_op jit(solution)/shard_map/ppermute | solution.py:52
  279.2 4.4 %collective-permute-done.18 = f32[4,512]{1,0:T(4,128)S(1)} collective-permute-done((f32[4,512]{1,0:T(4,128)S(1)}, f32[4,512]{1,0:T(4,128)S(1)}, u32[]{:S(2)}, u32[]{:S(2)}) %collective-permute-start.18) | collective-permute-done | bytes 8224 | tf_op jit(solution)/shard_map/ppermute | solution.py:52
  284.5 1.9 collective-permute-start.20
  286.8 7.5 %collective-permute-done.20 = f32[4,512]{1,0:T(4,128)S(1)} collective-permute-done((f32[4,512]{1,0:T(4,128)S(1)}, f32[4,512]{1,0:T(4,128)S(1)}, u32[]{:S(2)}, u32[]{:S(2)}) %collective-permute-start.20) | collective-permute-done | bytes 8224 | tf_op jit(solution)/shard_map/ppermute | solution.py:52
  295.2 1.9 collective-permute-start.22
  297.9 6.2 %collective-permute-done.22 = f32[4,512]{1,0:T(4,128)S(1)} collective-permute-done((f32[4,512]{1,0:T(4,128)S(1)}, f32[4,512]{1,0:T(4,128)S(1)}, u32[]{:S(2)}, u32[]{:S(2)}) %collective-permute-start.22) | collective-permute-done | bytes 8224 | tf_op jit(solution)/shard_map/ppermute | solution.py:52
  305.1 2.1 collective-permute-start.24
  307.3 5.8 %collective-permute-done.24 = f32[4,512]{1,0:T(4,128)S(1)} collective-permute-done((f32[4,512]{1,0:T(4,128)S(1)}, f32[4,512]{1,0:T(4,128)S(1)}, u32[]{:S(2)}, u32[]{:S(2)}) %collective-permute-start.24) | collective-permute-done | bytes 8224 | tf_op jit(solution)/shard_map/ppermute | solution.py:52
  314.3 1.9 collective-permute-start.26
  316.3 5.4 %collective-permute-done.26 = f32[4,512]{1,0:T(4,128)S(1)} collective-permute-done((f32[4,512]{1,0:T(4,128)S(1)}, f32[4,512]{1,0:T(4,128)S(1)}, u32[]{:S(2)}, u32[]{:S(2)}) %collective-permute-start.26) | collective-permute-done | bytes 8224 | tf_op jit(solution)/shard_map/ppermute | solution.py:52
  323.2 1.9 collective-permute-start.28
  325.1 5.5 %collective-permute-done.28 = f32[4,512]{1,0:T(4,128)S(1)} collective-permute-done((f32[4,512]{1,0:T(4,128)S(1)}, f32[4,512]{1,0:T(4,128)S(1)}, u32[]{:S(2)}, u32[]{:S(2)}) %collective-permute-start.28) | collective-permute-done | bytes 8224 | tf_op jit(solution)/shard_map/ppermute | solution.py:52
  332.1 1.9 collective-permute-start.29
  336.7 2.8 collective-permute-done.29
  341.0 2.2 collective-permute-start.30
  343.2 5.5 %collective-permute-done.30 = f32[4,512]{1,0:T(4,128)S(1)} collective-permute-done((f32[4,512]{1,0:T(4,128)S(1)}, f32[4,512]{1,0:T(4,128)S(1)}, u32[]{:S(2)}, u32[]{:S(2)}) %collective-permute-start.30) | collective-permute-done | bytes 8224 | tf_op jit(solution)/shard_map/ppermute | solution.py:52
  349.9 1.2 fusion.6
  353.9 3.5 collective-permute-start.33
  357.4 13.1 %collective-permute-start.32 = (f32[2,4,512]{2,1,0:T(4,128)S(1)}, f32[2,4,512]{2,1,0:T(4,128)S(1)}, u32[]{:S(2)}, u32[]{:S(2)}) collective-permute-start(f32[2,4,512]{2,1,0:T(4,128)S(1)} %bitcast.438), channel_id=1, source_target_pairs={{0,1},{16,2},{2,3},{18,0},{128,5},{144,6},{130,7},{146,4},{64,9},{... | collective-permute-start | bytes 49160 | tf_op jit(solution)/shard_map/ppermute | solution.py:231
  370.5 1.9 collective-permute-start.31
  372.5 7.0 %collective-permute-done.31 = f32[2,4,512]{2,1,0:T(4,128)S(1)} collective-permute-done((f32[2,4,512]{2,1,0:T(4,128)S(1)}, f32[2,4,512]{2,1,0:T(4,128)S(1)}, u32[]{:S(2)}, u32[]{:S(2)}) %collective-permute-start.31) | collective-permute-done | bytes 16416 | tf_op jit(solution)/shard_map/ppermute | solution.py:231
  (313 shorter events, 97.4 us)
Async XLA Ops:
  0.6 4.7 %copy-start = (f32[16,4]{0,1:T(4,128)S(1)}, f32[16,4]{0,1:T(4,128)}, u32[]{:S(2)}) copy-start(f32[16,4]{0,1:T(4,128)} %param.10) | copy-start | bytes 772
  0.6 41.7 %collective-permute-start.3 = (f32[128,512]{1,0:T(8,128)}, f32[128,512]{1,0:T(8,128)S(1)}, u32[]{:S(2)}, u32[]{:S(2)}) collective-permute-start(f32[128,512]{1,0:T(8,128)} %param.7), channel_id=1, source_target_pairs={{0,3},{1,0},{2,1},{3,2},{4,7},{5,4},{6,5},{7,6},{8,11},{9,8},{10,9... | collective-permute-start | bytes 786440 | tf_op jit(solution)/shard_map/ppermute | solution.py:85
  1.0 41.4 %collective-permute-start.2 = (f32[128,512]{1,0:T(8,128)}, f32[128,512]{1,0:T(8,128)S(1)}, u32[]{:S(2)}, u32[]{:S(2)}) collective-permute-start(f32[128,512]{1,0:T(8,128)} %param.7), channel_id=1, source_target_pairs={{0,2},{1,3},{2,0},{3,1},{4,6},{5,7},{6,4},{7,5},{8,10},{9,11},{10,... | collective-permute-start | bytes 786440 | tf_op jit(solution)/shard_map/ppermute | solution.py:85
  3.1 39.3 %collective-permute-start.1 = (f32[128,512]{1,0:T(8,128)}, f32[128,512]{1,0:T(8,128)S(1)}, u32[]{:S(2)}, u32[]{:S(2)}) collective-permute-start(f32[128,512]{1,0:T(8,128)} %param.7), channel_id=1, source_target_pairs={{0,1},{1,2},{2,3},{3,0},{4,5},{5,6},{6,7},{7,4},{8,9},{9,10},{10,1... | collective-permute-start | bytes 786440 | tf_op jit(solution)/shard_map/ppermute | solution.py:85
  4.6 0.7 copy-start.19
  5.4 7.5 %copy-start.20 = (s32[16]{0:T(128)S(1)}, s32[16]{0:T(128)}, u32[]{:S(2)}) copy-start(s32[16]{0:T(128)} %param.11) | copy-start | bytes 196
  5.5 30.8 %collective-permute-start = (f32[4,5]{0,1:T(8,128)S(1)}, f32[4,5]{0,1:T(8,128)S(1)}, u32[]{:S(2)}, u32[]{:S(2)}) collective-permute-start(f32[4,5]{0,1:T(8,128)S(1)} %pad_maximum_fusion.37), channel_id=1, source_target_pairs={{0,0},{1,16},{2,2},{3,18},{4,128},{5,144},{6,130},{7,146},{8,64},{... | collective-permute-start | bytes 248 | tf_op jit(solution)/shard_map/ppermute | solution.py:95
  13.1 23.0 %collective-permute-start.4 = (s32[4]{0:T(128)S(1)}, s32[4]{0:T(128)S(1)}, u32[]{:S(2)}, u32[]{:S(2)}) collective-permute-start(s32[4]{0:T(128)S(1)} %dynamic_slice.28), channel_id=1, source_target_pairs={{0,0},{1,16},{2,2},{3,18},{4,128},{5,144},{6,130},{7,146},{8,64},{... | collective-permute-start | bytes 56 | tf_op jit(solution)/shard_map/ppermute | solution.py:96
  15.1 0.7 copy-start.21
  31.9 1.3 copy-start.18
  33.9 8.4 %copy-start.16 = (f32[128,512]{1,0:T(8,128)S(1)}, f32[128,512]{1,0:T(8,128)}, u32[]{:S(2)}) copy-start(f32[128,512]{1,0:T(8,128)} %param.7) | copy-start | bytes 786436
  47.7 0.7 copy-start.17
  53.3 2.0 copy-start.13
  71.6 4.2 %copy-start.7 = (f32[512,512]{1,0:T(8,128)}, f32[512,512]{1,0:T(8,128)S(1)}, u32[]{:S(2)}) copy-start(f32[512,512]{1,0:T(8,128)S(1)} %fusion.210) | copy-start | bytes 3145732
  73.4 7.6 %copy-start.5 = (f32[512,512]{1,0:T(8,128)}, f32[512,512]{1,0:T(8,128)S(1)}, u32[]{:S(2)}) copy-start(f32[512,512]{1,0:T(8,128)S(1)} %fusion.212) | copy-start | bytes 3145732
  76.4 40.1 %collective-permute-start.5 = (f32[16,512]{1,0:T(8,128)S(1)}, f32[16,512]{1,0:T(8,128)S(1)}, u32[]{:S(2)}, u32[]{:S(2)}) collective-permute-start(f32[16,512]{1,0:T(8,128)S(1)} %concatenate.116), channel_id=1, source_target_pairs={{0,16},{16,2},{2,18},{18,128},{128,144},{144,130},{130,146},{146,6... | collective-permute-start | bytes 98312 | tf_op jit(solution)/shard_map/ppermute | solution.py:52
  82.9 1.9 copy-start.3
  84.8 1.0 copy-start.1
  95.9 8.3 %copy-start.8 = (f32[512,512]{1,0:T(8,128)S(1)}, f32[512,512]{1,0:T(8,128)}, u32[]{:S(2)}) copy-start(f32[512,512]{1,0:T(8,128)} %copy-done.7) | copy-start | bytes 3145732
  95.9 8.0 %collective-permute-start.17 = (f32[8,512]{1,0:T(8,128)S(1)}, f32[8,512]{1,0:T(8,128)S(1)}, u32[]{:S(2)}, u32[]{:S(2)}) collective-permute-start(f32[8,512]{1,0:T(8,128)S(1)} %concatenate.134), channel_id=1, source_target_pairs={{16,0},{2,16},{18,2},{128,18},{144,128},{130,144},{146,130},{64,14... | collective-permute-start | bytes 49160 | tf_op jit(solution)/shard_map/ppermute | solution.py:52
  104.8 12.3 %copy-start.9 = (f32[512,512]{1,0:T(8,128)S(1)}, f32[512,512]{1,0:T(8,128)}, u32[]{:S(2)}) copy-start(f32[512,512]{1,0:T(8,128)} %copy-done.7) | copy-start | bytes 3145732
  107.1 17.2 %collective-permute-start.19 = (f32[16,512]{1,0:T(8,128)S(1)}, f32[16,512]{1,0:T(8,128)S(1)}, u32[]{:S(2)}, u32[]{:S(2)}) collective-permute-start(f32[16,512]{1,0:T(8,128)S(1)} %pad_maximum_fusion.30), channel_id=1, source_target_pairs={{2,0},{18,16},{128,2},{144,18},{130,128},{146,144},{64,130},{80,14... | collective-permute-start | bytes 98312 | tf_op jit(solution)/shard_map/ppermute | solution.py:52
  118.2 2.6 copy-start.6
  118.5 2.9 copy-start.10
  121.4 3.9 %copy-start.4 = (f32[512,512]{1,0:T(8,128)S(1)}, f32[512,512]{1,0:T(8,128)}, u32[]{:S(2)}) copy-start(f32[512,512]{1,0:T(8,128)} %copy-done.3) | copy-start | bytes 3145732
  122.4 8.7 %collective-permute-start.6 = (f32[24,512]{1,0:T(8,128)S(1)}, f32[24,512]{1,0:T(8,128)S(1)}, u32[]{:S(2)}, u32[]{:S(2)}) collective-permute-start(f32[24,512]{1,0:T(8,128)S(1)} %pad_maximum_fusion.26), channel_id=1, source_target_pairs={{0,2},{16,18},{2,128},{18,144},{128,130},{144,146},{130,64},{146,8... | collective-permute-start | bytes 147464 | tf_op jit(solution)/shard_map/ppermute | solution.py:52
  126.2 17.0 %collective-permute-start.21 = (f32[32,512]{1,0:T(8,128)S(1)}, f32[32,512]{1,0:T(8,128)S(1)}, u32[]{:S(2)}, u32[]{:S(2)}) collective-permute-start(f32[32,512]{1,0:T(8,128)S(1)} %pad_maximum_fusion.22), channel_id=1, source_target_pairs={{128,0},{144,16},{130,2},{146,18},{64,128},{80,144},{66,130},{82,1... | collective-permute-start | bytes 196616 | tf_op jit(solution)/shard_map/ppermute | solution.py:52
  135.5 8.7 %copy-start.2 = (f32[512,512]{1,0:T(8,128)S(1)}, f32[512,512]{1,0:T(8,128)}, u32[]{:S(2)}) copy-start(f32[512,512]{1,0:T(8,128)} %copy-done.1) | copy-start | bytes 3145732
  135.6 11.7 %collective-permute-start.7 = (f32[40,512]{1,0:T(8,128)S(1)}, f32[40,512]{1,0:T(8,128)S(1)}, u32[]{:S(2)}, u32[]{:S(2)}) collective-permute-start(f32[40,512]{1,0:T(8,128)S(1)} %pad_maximum_fusion.19), channel_id=1, source_target_pairs={{0,128},{16,144},{2,130},{18,146},{128,64},{144,80},{130,66},{146,... | collective-permute-start | bytes 245768 | tf_op jit(solution)/shard_map/ppermute | solution.py:52
  145.3 15.2 %collective-permute-start.23 = (f32[64,512]{1,0:T(8,128)S(1)}, f32[64,512]{1,0:T(8,128)S(1)}, u32[]{:S(2)}, u32[]{:S(2)}) collective-permute-start(f32[64,512]{1,0:T(8,128)S(1)} %pad_maximum_fusion.16), channel_id=1, source_target_pairs={{64,0},{80,16},{66,2},{82,18},{192,128},{208,144},{194,130},{210,1... | collective-permute-start | bytes 393224 | tf_op jit(solution)/shard_map/ppermute | solution.py:52
  151.2 11.6 %collective-permute-start.8 = (f32[72,512]{1,0:T(8,128)S(1)}, f32[72,512]{1,0:T(8,128)S(1)}, u32[]{:S(2)}, u32[]{:S(2)}) collective-permute-start(f32[72,512]{1,0:T(8,128)S(1)} %pad_maximum_fusion.13), channel_id=1, source_target_pairs={{0,64},{16,80},{2,66},{18,82},{128,192},{144,208},{130,194},{146,2... | collective-permute-start | bytes 442376 | tf_op jit(solution)/shard_map/ppermute | solution.py:52
  167.0 8.3 %collective-permute-start.9 = (f32[136,512]{1,0:T(8,128)S(1)}, f32[136,512]{1,0:T(8,128)S(1)}, u32[]{:S(2)}, u32[]{:S(2)}) collective-permute-start(f32[136,512]{1,0:T(8,128)S(1)} %pad_maximum_fusion.7), channel_id=1, source_target_pairs={{0,1},{16,17},{2,3},{18,19},{128,129},{144,145},{130,131},{146,147... | collective-permute-start | bytes 835592 | tf_op jit(solution)/shard_map/ppermute | solution.py:52
  169.4 16.3 %collective-permute-start.25 = (f32[128,512]{1,0:T(8,128)S(1)}, f32[128,512]{1,0:T(8,128)S(1)}, u32[]{:S(2)}, u32[]{:S(2)}) collective-permute-start(f32[128,512]{1,0:T(8,128)S(1)} %pad_maximum_fusion.10), channel_id=1, source_target_pairs={{1,0},{17,16},{3,2},{19,18},{129,128},{145,144},{131,130},{147,146... | collective-permute-start | bytes 786440 | tf_op jit(solution)/shard_map/ppermute | solution.py:52
  179.8 16.1 %collective-permute-start.10 = (f32[264,512]{1,0:T(8,128)S(1)}, f32[264,512]{1,0:T(8,128)S(1)}, u32[]{:S(2)}, u32[]{:S(2)}) collective-permute-start(f32[264,512]{1,0:T(8,128)S(1)} %pad_maximum_fusion.1), channel_id=1, source_target_pairs={{0,4},{16,20},{2,6},{18,22},{128,132},{144,148},{130,134},{146,150... | collective-permute-start | bytes 1622024 | tf_op jit(solution)/shard_map/ppermute | solution.py:52
  185.7 34.8 %copy-start.15 = (f32[128,512]{1,0:T(8,128)}, f32[128,512]{1,0:T(8,128)S(1)}, u32[]{:S(2)}) copy-start(f32[128,512]{1,0:T(8,128)S(1)} %collective-permute-done.25) | copy-start | bytes 786436
  200.0 4.4 %collective-permute-start.11 = (f32[4,512]{1,0:T(4,128)S(1)}, f32[4,512]{1,0:T(4,128)S(1)}, u32[]{:S(2)}, u32[]{:S(2)}) collective-permute-start(f32[4,512]{1,0:T(4,128)S(1)} %fusion.48), channel_id=1, source_target_pairs={{0,8},{16,24},{2,10},{18,26},{128,136},{144,152},{130,138},{146,15... | collective-permute-start | bytes 24584 | tf_op jit(solution)/shard_map/ppermute | solution.py:52
  202.9 2.4 copy-start.11
  206.3 5.7 %collective-permute-start.12 = (f32[4,512]{1,0:T(4,128)S(1)}, f32[4,512]{1,0:T(4,128)S(1)}, u32[]{:S(2)}, u32[]{:S(2)}) collective-permute-start(f32[4,512]{1,0:T(4,128)S(1)} %fusion.46), channel_id=1, source_target_pairs={{0,8},{16,24},{2,10},{18,26},{128,136},{144,152},{130,138},{146,15... | collective-permute-start | bytes 24584 | tf_op jit(solution)/shard_map/ppermute | solution.py:52
  213.8 7.4 %collective-permute-start.13 = (f32[4,512]{1,0:T(4,128)S(1)}, f32[4,512]{1,0:T(4,128)S(1)}, u32[]{:S(2)}, u32[]{:S(2)}) collective-permute-start(f32[4,512]{1,0:T(4,128)S(1)} %fusion.43), channel_id=1, source_target_pairs={{0,8},{16,24},{2,10},{18,26},{128,136},{144,152},{130,138},{146,15... | collective-permute-start | bytes 24584 | tf_op jit(solution)/shard_map/ppermute | solution.py:52
  222.1 3.3 slice-start.1
  223.1 5.3 %collective-permute-start.14 = (f32[4,512]{1,0:T(4,128)S(1)}, f32[4,512]{1,0:T(4,128)S(1)}, u32[]{:S(2)}, u32[]{:S(2)}) collective-permute-start(f32[4,512]{1,0:T(4,128)S(1)} %fusion.41), channel_id=1, source_target_pairs={{0,16},{16,2},{2,18},{18,128},{128,144},{144,130},{130,146},{146,6... | collective-permute-start | bytes 24584 | tf_op jit(solution)/shard_map/ppermute | solution.py:52
  238.9 7.7 %collective-permute-start.15 = (f32[4,512]{1,0:T(4,128)S(1)}, f32[4,512]{1,0:T(4,128)S(1)}, u32[]{:S(2)}, u32[]{:S(2)}) collective-permute-start(f32[4,512]{1,0:T(4,128)S(1)} %fusion.28), channel_id=1, source_target_pairs={{16,0},{2,16},{18,2},{128,18},{144,128},{130,144},{146,130},{64,14... | collective-permute-start | bytes 24584 | tf_op jit(solution)/shard_map/ppermute | solution.py:52
  247.5 19.5 %collective-permute-start.16 = (f32[4,512]{1,0:T(4,128)S(1)}, f32[4,512]{1,0:T(4,128)S(1)}, u32[]{:S(2)}, u32[]{:S(2)}) collective-permute-start(f32[4,512]{1,0:T(4,128)S(1)} %fusion.26), channel_id=1, source_target_pairs={{2,0},{18,16},{128,2},{144,18},{130,128},{146,144},{64,130},{80,14... | collective-permute-start | bytes 24584 | tf_op jit(solution)/shard_map/ppermute | solution.py:52
  253.8 25.0 %collective-permute-start.27 = (f32[256,512]{1,0:T(8,128)S(1)}, f32[256,512]{1,0:T(8,128)S(1)}, u32[]{:S(2)}, u32[]{:S(2)}) collective-permute-start(f32[256,512]{1,0:T(8,128)S(1)} %pad_maximum_fusion.4), channel_id=1, source_target_pairs={{4,0},{20,16},{6,2},{22,18},{132,128},{148,144},{134,130},{150,146... | collective-permute-start | bytes 1572872 | tf_op jit(solution)/shard_map/ppermute | solution.py:52
  268.0 15.7 %collective-permute-start.18 = (f32[4,512]{1,0:T(4,128)S(1)}, f32[4,512]{1,0:T(4,128)S(1)}, u32[]{:S(2)}, u32[]{:S(2)}) collective-permute-start(f32[4,512]{1,0:T(4,128)S(1)} %fusion.24), channel_id=1, source_target_pairs={{128,0},{144,16},{130,2},{146,18},{64,128},{80,144},{66,130},{82,1... | collective-permute-start | bytes 24584 | tf_op jit(solution)/shard_map/ppermute | solution.py:52
  278.8 28.5 %copy-start.14 = (f32[256,512]{1,0:T(8,128)}, f32[256,512]{1,0:T(8,128)S(1)}, u32[]{:S(2)}) copy-start(f32[256,512]{1,0:T(8,128)S(1)} %collective-permute-done.27) | copy-start | bytes 1572868
  284.5 9.8 %collective-permute-start.20 = (f32[4,512]{1,0:T(4,128)S(1)}, f32[4,512]{1,0:T(4,128)S(1)}, u32[]{:S(2)}, u32[]{:S(2)}) collective-permute-start(f32[4,512]{1,0:T(4,128)S(1)} %fusion.22), channel_id=1, source_target_pairs={{64,0},{80,16},{66,2},{82,18},{192,128},{208,144},{194,130},{210,1... | collective-permute-start | bytes 24584 | tf_op jit(solution)/shard_map/ppermute | solution.py:52
  295.2 8.9 %collective-permute-start.22 = (f32[4,512]{1,0:T(4,128)S(1)}, f32[4,512]{1,0:T(4,128)S(1)}, u32[]{:S(2)}, u32[]{:S(2)}) collective-permute-start(f32[4,512]{1,0:T(4,128)S(1)} %fusion.20), channel_id=1, source_target_pairs={{1,0},{17,16},{3,2},{19,18},{129,128},{145,144},{131,130},{147,146... | collective-permute-start | bytes 24584 | tf_op jit(solution)/shard_map/ppermute | solution.py:52
  305.1 8.0 %collective-permute-start.24 = (f32[4,512]{1,0:T(4,128)S(1)}, f32[4,512]{1,0:T(4,128)S(1)}, u32[]{:S(2)}, u32[]{:S(2)}) collective-permute-start(f32[4,512]{1,0:T(4,128)S(1)} %fusion.18), channel_id=1, source_target_pairs={{4,0},{20,16},{6,2},{22,18},{132,128},{148,144},{134,130},{150,146... | collective-permute-start | bytes 24584 | tf_op jit(solution)/shard_map/ppermute | solution.py:52
  313.7 2.5 slice-start
  314.3 7.4 %collective-permute-start.26 = (f32[4,512]{1,0:T(4,128)S(1)}, f32[4,512]{1,0:T(4,128)S(1)}, u32[]{:S(2)}, u32[]{:S(2)}) collective-permute-start(f32[4,512]{1,0:T(4,128)S(1)} %fusion.16), channel_id=1, source_target_pairs={{8,0},{24,16},{10,2},{26,18},{136,128},{152,144},{138,130},{154,14... | collective-permute-start | bytes 24584 | tf_op jit(solution)/shard_map/ppermute | solution.py:52
  323.2 7.4 %collective-permute-start.28 = (f32[4,512]{1,0:T(4,128)S(1)}, f32[4,512]{1,0:T(4,128)S(1)}, u32[]{:S(2)}, u32[]{:S(2)}) collective-permute-start(f32[4,512]{1,0:T(4,128)S(1)} %fusion.14), channel_id=1, source_target_pairs={{8,0},{24,16},{10,2},{26,18},{136,128},{152,144},{138,130},{154,14... | collective-permute-start | bytes 24584 | tf_op jit(solution)/shard_map/ppermute | solution.py:52
  331.5 8.9 %copy-start.12 = (f32[512,512]{1,0:T(8,128)S(1)}, f32[512,512]{1,0:T(8,128)}, u32[]{:S(2)}) copy-start(f32[512,512]{1,0:T(8,128)} %fusion.234) | copy-start | bytes 3145732
  332.1 7.4 %collective-permute-start.29 = (f32[4,512]{1,0:T(4,128)S(1)}, f32[4,512]{1,0:T(4,128)S(1)}, u32[]{:S(2)}, u32[]{:S(2)}) collective-permute-start(f32[4,512]{1,0:T(4,128)S(1)} %fusion.12), channel_id=1, source_target_pairs={{8,0},{24,16},{10,2},{26,18},{136,128},{152,144},{138,130},{154,14... | collective-permute-start | bytes 24584 | tf_op jit(solution)/shard_map/ppermute | solution.py:52
  341.0 7.7 %collective-permute-start.30 = (f32[4,512]{1,0:T(4,128)S(1)}, f32[4,512]{1,0:T(4,128)S(1)}, u32[]{:S(2)}, u32[]{:S(2)}) collective-permute-start(f32[4,512]{1,0:T(4,128)S(1)} %fusion.10), channel_id=1, source_target_pairs={{16,0},{2,16},{18,2},{128,18},{144,128},{130,144},{146,130},{64,14... | collective-permute-start | bytes 24584 | tf_op jit(solution)/shard_map/ppermute | solution.py:52
  353.8 18.7 %collective-permute-start.34 = (f32[2,4,512]{2,1,0:T(4,128)S(1)}, f32[2,4,512]{2,1,0:T(4,128)S(1)}, u32[]{:S(2)}, u32[]{:S(2)}) collective-permute-start(f32[2,4,512]{2,1,0:T(4,128)S(1)} %bitcast.436), channel_id=1, source_target_pairs={{0,3},{16,0},{2,1},{18,2},{128,7},{144,4},{130,5},{146,6},{64,11},... | collective-permute-start | bytes 49160 | tf_op jit(solution)/shard_map/ppermute | solution.py:231
  353.9 18.6 %collective-permute-start.33 = (f32[2,4,512]{2,1,0:T(4,128)S(1)}, f32[2,4,512]{2,1,0:T(4,128)S(1)}, u32[]{:S(2)}, u32[]{:S(2)}) collective-permute-start(f32[2,4,512]{2,1,0:T(4,128)S(1)} %bitcast.437), channel_id=1, source_target_pairs={{0,2},{16,3},{2,0},{18,1},{128,6},{144,7},{130,4},{146,5},{64,10},... | collective-permute-start | bytes 49160 | tf_op jit(solution)/shard_map/ppermute | solution.py:231
  357.4 15.1 %collective-permute-start.32 = (f32[2,4,512]{2,1,0:T(4,128)S(1)}, f32[2,4,512]{2,1,0:T(4,128)S(1)}, u32[]{:S(2)}, u32[]{:S(2)}) collective-permute-start(f32[2,4,512]{2,1,0:T(4,128)S(1)} %bitcast.438), channel_id=1, source_target_pairs={{0,1},{16,2},{2,3},{18,0},{128,5},{144,6},{130,7},{146,4},{64,9},{... | collective-permute-start | bytes 49160 | tf_op jit(solution)/shard_map/ppermute | solution.py:231
  370.5 9.0 %collective-permute-start.31 = (f32[2,4,512]{2,1,0:T(4,128)S(1)}, f32[2,4,512]{2,1,0:T(4,128)S(1)}, u32[]{:S(2)}, u32[]{:S(2)}) collective-permute-start(f32[2,4,512]{2,1,0:T(4,128)S(1)} %bitcast.439), channel_id=1, source_target_pairs={{0,0},{16,1},{2,2},{18,3},{128,4},{144,5},{130,6},{146,7},{64,8},{... | collective-permute-start | bytes 49160 | tf_op jit(solution)/shard_map/ppermute | solution.py:231
